TPU v7x, 768 devices: a whole 4x8x12 slice. The times are simulated.
768 devices in a mesh: tok: 96 (over x, z, core), mdl: 8 (over y).
Axes of the slice: x: 4, y: 8, z: 12, core: 2. Of those that a mesh axis runs over, the one named last changes fastest.
Arguments:
- hidden: bfloat16 [8, 24576, 5120], P('mdl', 'tok'), may hold values from -6 to 6
- sketch: bfloat16 [5120, 256], replicated, may hold values from -0.078125 to 0.078125
Outputs:
- cross_gram: float32 [2048, 2048], P('mdl')
- similarity: float32 [8, 8], P('mdl')
All inputs are finite; a program needn't handle non-finite values.
Results may differ from a plain program's by a relative error of at most 0.0025.
Values may be sent and summed in bfloat16 or wider, within the bound.
No kernel may reach another device: no remote copies, remote signals or barrier semaphores. Data moves between devices by JAX's collectives and lax.ppermute only.
A program may use at most 64 MiB of HBM per device.

v0:
```python
import jax
import jax.numpy as jnp
from jax import lax
from jax.sharding import PartitionSpec as P


def right_solve(factor, block):
    return lax.linalg.triangular_solve(factor, block, left_side=False, lower=True, transpose_a=True)


def on_device(hidden, sketch):
    states = hidden[0]
    projected = jnp.dot(states, sketch, preferred_element_type=jnp.float32).astype(jnp.bfloat16)
    basis_width = projected.shape[1]
    models = lax.axis_size("mdl")
    local_row = jnp.dot(
        projected.T,
        lax.all_gather(projected, "mdl", axis=1, tiled=True),
        preferred_element_type=jnp.float32,
    )
    row_sums = lax.psum(local_row, "tok")
    row_tiles = row_sums.reshape(basis_width, models, basis_width)
    local_gram = jnp.dot(projected.T, projected, preferred_element_type=jnp.float32)
    gram_total = lax.psum(local_gram, "tok")
    factor = jnp.linalg.cholesky(gram_total)
    factors = lax.all_gather(factor[None], "mdl", axis=0, tiled=True)
    flat_row = row_tiles.reshape(basis_width, models * basis_width)
    left_done = lax.linalg.triangular_solve(factor, flat_row, left_side=True, lower=True)
    left_done = left_done.reshape(basis_width, models, basis_width)
    right_done = jax.vmap(right_solve, in_axes=(0, 1), out_axes=1)(factors, left_done)
    cross_gram = right_done.reshape(basis_width, models * basis_width)
    similarity = jnp.sum(right_done * right_done, axis=(0, 2)) / basis_width
    return (cross_gram, similarity[None, :])


def solution(mesh):
    return jax.shard_map(
        on_device,
        mesh=mesh,
        in_specs=(P("mdl", "tok", None), P()),
        out_specs=(P("mdl", None), P("mdl", None)),
        check_vma=False,
    )
```

profile of v0, /device:TPU:1, one launch (start us, length us, event | category | flops | bytes accessed | tf_op | source)
XLA Modules:
  0.0 623.4 jit_solution(14881997351899788093)
XLA Ops:
  7.2 0.0 all-gather.4.cloned.1.call-start
  7.2 1.7 copy-done
  8.9 3.2 fusion.3
  12.1 0.0 all-gather.4.cloned.1.call-update
  12.2 0.0 all-reduce.4.cloned.1.call-start
  12.2 1.9 fusion.21
  14.1 46.6 %all-gather.4.cloned.1.call-done = bf16[256,2048]{1,0:T(8,128)(2,1)} async-done(((bf16[256,256]{1,0:T(8,128)(2,1)}), bf16[256,2048]{1,0:T(8,128)(2,1)}) %all-gather.4.cloned.1.call-update) | async-done | bytes 1048592 | tf_op jit(solution)/shard_map/all_gather | solution.py:18
  60.7 3.1 fusion.22
  63.8 0.0 all-reduce.4.cloned.1.call-update
  63.8 0.0 all-gather.6.cloned.1.call-start
  63.9 290.0 %all-reduce.4.cloned.1.call-done = (f32[256,2048]{1,0:T(8,128)}, f32[256,256]{0,1:T(8,128)}) async-done(((f32[256,2048]{1,0:T(8,128)}, f32[256,256]{0,1:T(8,128)}), (f32[256,2048]{1,0:T(8,128)}, f32[256,256]{0,1:T(8,128)})) %all-reduce.4.cloned.1.call-update) | async-done | bytes 2359312 | tf_op jit(solution)/shard_map/psum | solution.py:21
  353.8 1.1 copy.5
  354.9 1.0 fusion.12
  355.9 11.7 %cholesky.50 = f32[128,128]{1,0:T(8,128)S(1)} custom-call(f32[128,128]{1,0:T(8,128)S(1)} %cholesky.118), custom_call_target="Cholesky" | custom-call | tf_op jit(solution)/shard_map/jit(cholesky)/cholesky | solution.py:25
  367.7 9.8 %custom-call.17 = f32[1,128,128]{1,2,0:T(8,128)S(1)} custom-call(f32[1,128,128]{2,1,0:T(8,128)S(1)} %get-tuple-element.47), custom_call_target="InvertDiagBlocksLowerTriangular" | custom-call | tf_op jit(solution)/shard_map/jit(cholesky)/cholesky | solution.py:25
  377.5 0.2 constant_dynamic-update-slice_fusion.1
  377.7 0.3 convolution_subtract_fusion.2
  378.0 11.7 %cholesky.105 = f32[128,128]{1,0:T(8,128)S(1)} custom-call(f32[128,128]{1,0:T(8,128)S(1)} %convolution_subtract_fusion.2), custom_call_target="Cholesky" | custom-call | tf_op jit(solution)/shard_map/jit(cholesky)/cholesky | solution.py:25
  389.7 0.6 compare_reduce_fusion
  391.7 0.7 fusion.13
  392.4 0.0 all-gather.6.cloned.1.call-update
  392.5 0.1 triangular_solve.103
  392.6 4.2 while.2
  392.7 0.6 fusion.36
  393.3 1.4 bitcast_dynamic-update-slice_fusion.4
  394.8 0.6 fusion.36
  395.4 1.4 bitcast_dynamic-update-slice_fusion.4
  396.8 19.7 %custom-call.18 = f32[2,128,128]{1,2,0:T(8,128)S(1)} custom-call(f32[2,128,128]{2,1,0:T(8,128)S(1)} %get-tuple-element.9), custom_call_target="InvertDiagBlocksLowerTriangular" | custom-call | tf_op jit(solution)/shard_map/triangular_solve | solution.py:28
  416.5 2.4 fusion.8
  418.9 1.0 convolution_subtract_fusion
  420.0 1.1 fusion.15
  421.0 0.2 pad_maximum_fusion
  421.2 1.5 copy.22
  422.8 12.0 %all-gather.6.cloned.1.call-done = f32[2048,256]{1,0:T(8,128)} async-done(((f32[256,256]{1,0:T(8,128)}), f32[2048,256]{1,0:T(8,128)}) %all-gather.6.cloned.1.call-update) | async-done | bytes 2097168 | tf_op jit(solution)/shard_map/all_gather | solution.py:26
  434.7 3.2 broadcast_select_fusion
  437.9 8.3 %while.3 = (s32[]{:T(128)}, f32[8,256,256]{2,1,0:T(8,128)}, s32[2,2]{1,0:T(2,128)S(1)}, f32[2,8,128,128]{3,2,0,1:T(8,128)}, s32[]{:T(128)}) while((s32[]{:T(128)}, f32[8,256,256]{2,1,0:T(8,128)}, s32[2,2]{1,0:T(2,128)S(1)}, f32[2,8,128,128]{3,2,0,1:T(8,128)}, s32[]{:T(128)}) %tuple.56), condition=%wide.while_cond.1, body=%wide.while_body.1.sunk | while | flops 2 | bytes 1049709 | solution.py:8
  437.9 0.6 fusion.37
  438.5 3.6 bitcast_dynamic-update-slice_fusion.5
  442.1 0.6 fusion.37
  442.7 3.5 bitcast_dynamic-update-slice_fusion.5
  446.2 158.6 %custom-call.19 = f32[8,2,128,128]{2,3,1,0:T(8,128)} custom-call(f32[8,2,128,128]{3,2,1,0:T(8,128)} %bitcast.83), custom_call_target="InvertDiagBlocksLowerTriangular" | custom-call | tf_op jit(solution)/shard_map/vmap()/triangular_solve | solution.py:8
  604.8 2.6 fusion.6
  607.5 3.1 convolution_subtract_fusion.1
  610.6 1.1 fusion.10
  611.7 0.3 fusion.2
  611.9 1.6 pad_maximum_fusion.1
  613.5 2.9 copy.10
  616.4 0.5 multiply_bitcast_fusion
  (19 shorter events, 0.2 us)
Async XLA Ops:
  7.2 1.7 copy-start
  7.2 53.5 %all-gather.4.cloned.1.call-start = ((), (), s32[]{:S(2)}) async-start(), calls=%async_computation | async-start | bytes 1179648 | tf_op jit(solution)/shard_map/all_gather | solution.py:18
  12.2 341.7 %all-reduce.4.cloned.1.call-start = ((), (), s32[]{:S(2)}) async-start(), calls=%async_computation.2 | async-start | bytes 4718592 | tf_op jit(solution)/shard_map/psum | solution.py:21
  63.8 370.9 %all-gather.6.cloned.1.call-start = ((), (), s32[]{:S(2)}) async-start(), calls=%async_computation.1 | async-start | bytes 2359296 | tf_op jit(solution)/shard_map/all_gather | solution.py:26
  416.5 2.4 copy-start.2
  604.8 2.6 copy-start.1
  607.4 3.1 copy-start.3
Sparse Core Ops, SparseCore 0:
  12.3 48.3 all-gather.3
  64.9 288.9 all-reduce.3
  392.6 42.1 all-gather.5
where the time goes:
time: 627 us; the launch traced here: 623 us
  waiting for transfers between devices  349 us (56%)
  other arithmetic  220 us (35%)
  matrix products  19.9 us (3%)
  local copies, waits for them, and re-layouts  19.6 us (3%)
  between operations  15.2 us (2%)
    psum x1, waiting for transfers between devices, on_device(): row_sums = lax.psum(local_row, 'tok')  290 us
    another operation x3, other arithmetic, right_solve(): lax.linalg.triangular_solve(factor, block, left_side=False, lower=True, t...  163 us
    all_gather x1, waiting for transfers between devices, on_device(): lax.all_gather(projected, 'mdl', axis=1, tiled=True)  46.6 us
    another operation x6, other arithmetic, on_device(): factor = jnp.linalg.cholesky(gram_total)  34 us
    another operation x5, other arithmetic, on_device(): lax.linalg.triangular_solve(factor, flat_row, left_side=True, lower=True)  20.7 us
  transfers between devices with their start and end apart: 3, of which 3 were waited for; matrix products, arithmetic and copies ran while one was open for 5% of the time, Pallas kernels for 0%

commit v1 on v0

v1 whole, which is shorter than its diff:
```python
import jax
import jax.numpy as jnp
from jax import lax
from jax.sharding import Mesh
from jax.sharding import PartitionSpec as P

HIGH = lax.Precision.HIGHEST


def scatter_sum(chunks, axes):
    return lax.all_to_all(chunks, axes, 0, 0, tiled=True).sum(axis=0)


def gather_all(piece, axes, count):
    copies = jnp.broadcast_to(piece[None], (count,) + piece.shape)
    return lax.all_to_all(copies, axes, 0, 0, tiled=True)


def sum_over_tokens(row, inner, outer):
    rows, cols = row.shape
    n_in = lax.axis_size(inner)
    n_out = lax.axis_size(outer)
    width = cols // n_in
    part = scatter_sum(row.reshape(rows, n_in, width).transpose(1, 0, 2), inner)
    pad = (-rows) % n_out
    padded = jnp.pad(part, ((0, pad), (0, 0))).reshape(n_out, (rows + pad) // n_out, width)
    piece = scatter_sum(padded, outer)
    part = gather_all(piece, outer, n_out).reshape(rows + pad, width)[:rows]
    full = gather_all(part, inner, n_in)
    return full.transpose(1, 0, 2).reshape(rows, cols)


def on_device(hidden, sketch):
    states = hidden[0]
    projected = jnp.dot(states, sketch, preferred_element_type=jnp.float32).astype(jnp.bfloat16)
    basis_width = projected.shape[1]
    models = lax.axis_size("mdl")
    me = lax.axis_index("mdl")
    everyone = gather_all(projected, "mdl", models)
    everyone = everyone.transpose(1, 0, 2).reshape(projected.shape[0], models * basis_width)
    local_row = jnp.dot(projected.T, everyone, preferred_element_type=jnp.float32)
    row_sums = sum_over_tokens(local_row, ("x", "c"), "z")
    row_tiles = row_sums.reshape(basis_width, models, basis_width)
    gram_total = lax.dynamic_index_in_dim(row_tiles, me, 1, keepdims=False)
    factor = jnp.linalg.cholesky(gram_total)
    eye = jnp.eye(basis_width, dtype=jnp.float32)
    inverse = lax.linalg.triangular_solve(factor, eye, left_side=True, lower=True)
    inverses = gather_all(inverse, "mdl", models)
    left_done = jnp.einsum("ab,bjc->ajc", inverse, row_tiles, precision=HIGH)
    right_done = jnp.einsum("ajc,jdc->ajd", left_done, inverses, precision=HIGH)
    cross_gram = right_done.reshape(basis_width, models * basis_width)
    similarity = jnp.sum(right_done * right_done, axis=(0, 2)) / basis_width
    return (cross_gram, similarity[None, :])


def solution(mesh):
    tok_size = mesh.shape["tok"]
    cores = 2
    z_size = tok_size // (4 * cores)
    devices = mesh.devices.reshape(tok_size // (z_size * cores), z_size, cores, mesh.shape["mdl"])
    sub = Mesh(devices, ("x", "z", "c", "mdl"))
    return jax.shard_map(
        on_device,
        mesh=sub,
        in_specs=(P("mdl", ("x", "z", "c"), None), P()),
        out_specs=(P("mdl", None), P("mdl", None)),
        check_vma=False,
    )
```

time: 627 us -> 288 us (0.46)
  waiting for transfers between devices: 349 us -> 69.9 us
  other arithmetic: 220 us -> 57.2 us
  blocking collectives: 0 us -> 118 us
  between operations: 15.2 us -> 2.1 us
  starting transfers between devices: 0.12 us -> 11.3 us
  local copies, waits for them, and re-layouts: 19.6 us -> 13 us
    psum x1 -> x0, waiting for transfers between devices: 290 us -> none  [on_device(): row_sums = lax.psum(local_row, 'tok')]
    another operation x8 -> x4, other arithmetic: 184 us -> 19.9 us  [on_device(): lax.linalg.triangular_solve(factor, eye, left_side=True, lower=True)]
    all_to_all x0 -> x4, blocking collectives: none -> 118 us  [the longest x2 66.6 us: scatter_sum(): return lax.all_to_all(chunks, axes, 0, 0, tiled=True).sum(axis=0)]
    all_to_all x0 -> x2, waiting for transfers between devices: none -> 69.9 us  [gather_all(): return lax.all_to_all(copies, axes, 0, 0, tiled=True)]
    all_gather x2 -> x0, waiting for transfers between devices: 58.6 us -> none  [the longest x1 46.6 us: on_device(): lax.all_gather(projected, 'mdl', axis=1, tiled=True)]
    all_to_all x0 -> x2, starting transfers between devices: none -> 11.3 us  [gather_all(): return lax.all_to_all(copies, axes, 0, 0, tiled=True)]
    another operation x6 -> x3, matrix products: 11.3 us -> 0.83 us  [on_device(): lax.linalg.triangular_solve(factor, eye, left_side=True, lower=True)]
    another operation x13 -> x9, local copies, waits for them, and re-layouts: 12.4 us -> 5.06 us
  transfers between devices with their start and end apart: 3 -> 2, of which waited for: 3 -> 2; matrix products, arithmetic and copies ran while one was open for 5% -> 2% of each run, Pallas kernels for 0% -> 0%
where the time goes in v1:
time: 288 us; the launch traced here: 286 us
  blocking collectives  118 us (41%)
  waiting for transfers between devices  69.9 us (24%)
  other arithmetic  57.2 us (20%)
  matrix products  14.9 us (5%)
  local copies, waits for them, and re-layouts  13 us (5%)
  starting transfers between devices  11.3 us (4%)
    all_to_all x2, waiting for transfers between devices, gather_all(): return lax.all_to_all(copies, axes, 0, 0, tiled=True)  69.9 us
    all_to_all x2, blocking collectives, scatter_sum(): return lax.all_to_all(chunks, axes, 0, 0, tiled=True).sum(axis=0)  66.6 us
    all_to_all x2, blocking collectives, gather_all(): return lax.all_to_all(copies, axes, 0, 0, tiled=True)  51 us
    another operation x6, other arithmetic, on_device(): factor = jnp.linalg.cholesky(gram_total)  34 us
    another operation x4, other arithmetic, on_device(): lax.linalg.triangular_solve(factor, eye, left_side=True, lower=True)  19.9 us
    all_to_all x2, starting transfers between devices, gather_all(): return lax.all_to_all(copies, axes, 0, 0, tiled=True)  11.3 us
  transfers between devices with their start and end apart: 2, of which 2 were waited for; matrix products, arithmetic and copies ran while one was open for 2% of the time, Pallas kernels for 0%

profile of v1, /device:TPU:1, one launch (start us, length us, event | category | flops | bytes accessed | tf_op | source)
XLA Modules:
  0.0 286.0 jit_solution(14113303294136748322)
XLA Ops:
  0.6 0.0 copy-start
  0.6 1.7 copy-done
  2.4 2.6 fusion.5
  5.0 0.1 copy.13
  5.1 0.1 broadcast_in_dim.9
  5.1 30.2 %all_to_all.30 = bf16[8,256,256]{1,2,0:T(8,128)(2,1)S(1)} all-to-all(bf16[8,256,256]{1,2,0:T(8,128)(2,1)S(1)} %broadcast_in_dim.9), channel_id=1, replica_groups=mesh['x'=4,'z'=12,'c'=2,'mdl'=8] {'mdl'}, dimensions={0} | all-to-all | bytes 2097152 | tf_op jit(solution)/shard_map/all_to_all | solution.py:16
  35.3 0.5 convolution_bitcast_fusion
  35.8 37.6 %all_to_all.31 = f32[8,256,256]{2,1,0:T(8,128)} all-to-all(f32[8,256,256]{2,1,0:T(8,128)S(1)} %convolution_bitcast_fusion), channel_id=1, replica_groups=mesh['x'=4,'z'=12,'c'=2,'mdl'=8] {'x','c'}, dimensions={0} | all-to-all | bytes 4194304 | tf_op jit(solution)/shard_map/all_to_all | solution.py:11
  73.4 1.8 reduce_sum.27
  75.3 28.9 %all_to_all.32 = f32[12,22,256]{2,1,0:T(8,128)S(1)} all-to-all(f32[12,22,256]{2,1,0:T(8,128)S(1)} %reshape.51), channel_id=1, replica_groups=mesh['x'=4,'z'=12,'c'=2,'mdl'=8] {'z'}, dimensions={0} | all-to-all | bytes 540672 | tf_op jit(solution)/shard_map/all_to_all | solution.py:11
  104.2 20.9 %all_to_all.33 = f32[12,22,256]{2,1,0:T(8,128)S(1)} all-to-all(f32[12,22,256]{2,1,0:T(8,128)S(1)} %broadcast_in_dim.10), channel_id=1, replica_groups=mesh['x'=4,'z'=12,'c'=2,'mdl'=8] {'z'}, dimensions={0} | all-to-all | bytes 540672 | tf_op jit(solution)/shard_map/all_to_all | solution.py:16
  125.2 1.5 broadcast_in_dim.11
  126.7 7.0 %all-to-all-start.4 = ((f32[8,256,256]{2,1,0:T(8,128)}), f32[8,256,256]{2,1,0:T(8,128)}, u32[]{:S(2)}, u32[]{:S(2)}) async-start(f32[8,256,256]{2,1,0:T(8,128)} %broadcast_in_dim.11), calls=%async_computation.4 | async-start | bytes 4194304 | tf_op jit(solution)/shard_map/all_to_all | solution.py:16
  133.7 26.4 %all-to-all-done.4 = f32[8,256,256]{2,1,0:T(8,128)} async-done(((f32[8,256,256]{2,1,0:T(8,128)}), f32[8,256,256]{2,1,0:T(8,128)}, u32[]{:S(2)}, u32[]{:S(2)}) %all-to-all-start.4) | async-done | bytes 2097184 | tf_op jit(solution)/shard_map/all_to_all | solution.py:16
  160.1 1.0 constant_dynamic-slice_fusion.1
  161.1 0.1 copy.15
  161.2 1.0 fusion.9
  162.2 11.7 %cholesky.50 = f32[128,128]{1,0:T(8,128)S(1)} custom-call(f32[128,128]{1,0:T(8,128)S(1)} %cholesky.118), custom_call_target="Cholesky" | custom-call | tf_op jit(solution)/shard_map/jit(cholesky)/cholesky | solution.py:45
  174.0 9.8 %custom-call.14 = f32[1,128,128]{1,2,0:T(8,128)S(1)} custom-call(f32[1,128,128]{2,1,0:T(8,128)S(1)} %get-tuple-element.29), custom_call_target="InvertDiagBlocksLowerTriangular" | custom-call | tf_op jit(solution)/shard_map/jit(cholesky)/cholesky | solution.py:45
  183.8 0.2 constant_dynamic-update-slice_fusion.1
  184.0 0.3 convolution_subtract_fusion.1
  184.3 11.7 %cholesky.105 = f32[128,128]{1,0:T(8,128)S(1)} custom-call(f32[128,128]{1,0:T(8,128)S(1)} %convolution_subtract_fusion.1), custom_call_target="Cholesky" | custom-call | tf_op jit(solution)/shard_map/jit(cholesky)/cholesky | solution.py:45
  196.0 0.7 compare_reduce_fusion
  198.0 0.1 triangular_solve.63
  198.1 3.9 %while.1 = (s32[]{:T(128)}, f32[256,256]{1,0:T(8,128)S(1)}, s32[2,2]{1,0:T(2,128)S(1)}, f32[2,128,128]{2,1,0:T(8,128)S(1)}, s32[]{:T(128)}) while((s32[]{:T(128)}, f32[256,256]{1,0:T(8,128)S(1)}, s32[2,2]{1,0:T(2,128)S(1)}, f32[2,128,128]{2,1,0:T(8,128)S(1)}, s32[]{:T(128)}) %tuple.31), condition=%wide.while_cond, body=%wide.while_body.sunk | while | flops 2 | bytes 131189 | solution.py:47
  198.1 0.6 fusion.28
  198.7 1.4 bitcast_dynamic-update-slice_fusion.2
  200.0 0.6 fusion.28
  200.6 1.4 bitcast_dynamic-update-slice_fusion.2
  202.0 19.9 %custom-call.15 = f32[2,128,128]{1,2,0:T(8,128)S(1)} custom-call(f32[2,128,128]{2,1,0:T(8,128)S(1)} %get-tuple-element.9), custom_call_target="InvertDiagBlocksLowerTriangular" | custom-call | tf_op jit(solution)/shard_map/triangular_solve | solution.py:47
  221.9 0.3 fusion.12
  222.2 0.3 convolution_subtract_fusion
  222.4 0.3 fusion.15
  222.8 1.5 broadcast_in_dim.12
  224.3 4.4 %all-to-all-start.5 = ((f32[8,256,256]{2,1,0:T(8,128)}), f32[8,256,256]{2,1,0:T(8,128)}, u32[]{:S(2)}, u32[]{:S(2)}) async-start(f32[8,256,256]{2,1,0:T(8,128)} %broadcast_in_dim.12), calls=%async_computation.5 | async-start | bytes 4194304 | tf_op jit(solution)/shard_map/all_to_all | solution.py:16
  228.7 4.8 %fusion.3 = f32[256,8,256]{2,0,1:T(8,128)} fusion(f32[8,256,256]{2,1,0:T(8,128)} %all-to-all-done.4, f32[128,256]{1,0:T(8,128)S(1)} %fusion.15, f32[128,256]{1,0:T(8,128)S(1)} %fusion.12), kind=kOutput, calls=%fused_computation.6 | convolution fusion | flops 1610678272 | bytes 4456448 | tf_op jit(solution)/shard_map/ab,bjc->ajc/dot_general | solution.py:49
  233.5 43.4 %all-to-all-done.5 = f32[8,256,256]{2,1,0:T(8,128)} async-done(((f32[8,256,256]{2,1,0:T(8,128)}), f32[8,256,256]{2,1,0:T(8,128)}, u32[]{:S(2)}, u32[]{:S(2)}) %all-to-all-start.5) | async-done | bytes 2097184 | tf_op jit(solution)/shard_map/all_to_all | solution.py:16
  276.9 5.7 %fusion.2 = (f32[8]{0:T(128)S(1)}, f32[8,256,256]{2,1,0:T(8,128)}) fusion(f32[8,256,256]{2,1,0:T(8,128)} %all-to-all-done.5, f32[256,8,256]{2,0,1:T(8,128)} %fusion.3), kind=kOutput, calls=%fused_computation.5 | convolution fusion | flops 1611661312 | bytes 6291488 | tf_op jit(solution)/shard_map/ajc,jdc->ajd/dot_general | solution.py:50
  282.6 0.5 multiply_bitcast_fusion
  283.1 2.9 %copy.17 = f32[256,2048]{1,0:T(8,128)} copy(f32[256,2048]{0,1:T(8,128)} %bitcast.71) | data formatting | bytes 4194304
  (17 shorter events, 0.3 us)
Async XLA Ops:
  0.6 1.7 copy-start
  126.7 33.4 %all-to-all-start.4 = ((f32[8,256,256]{2,1,0:T(8,128)}), f32[8,256,256]{2,1,0:T(8,128)}, u32[]{:S(2)}, u32[]{:S(2)}) async-start(f32[8,256,256]{2,1,0:T(8,128)} %broadcast_in_dim.11), calls=%async_computation.4 | async-start | bytes 4194304 | tf_op jit(solution)/shard_map/all_to_all | solution.py:16
  224.3 52.6 %all-to-all-start.5 = ((f32[8,256,256]{2,1,0:T(8,128)}), f32[8,256,256]{2,1,0:T(8,128)}, u32[]{:S(2)}, u32[]{:S(2)}) async-start(f32[8,256,256]{2,1,0:T(8,128)} %broadcast_in_dim.12), calls=%async_computation.5 | async-start | bytes 4194304 | tf_op jit(solution)/shard_map/all_to_all | solution.py:16

commit v2 on v1

--- a/solution.py
+++ b/solution.py
@@ -30,6 +30,23 @@
     return full.transpose(1, 0, 2).reshape(rows, cols)
 
 
+def pack_lower(m):
+    h = m.shape[0] // 2
+    top, low_right = m[:h, :h], m[h:, h:]
+    folded = jnp.tril(top, -1) + low_right.T
+    return jnp.concatenate([m[h:, :h], folded, jnp.diagonal(top)[None]], axis=0)
+
+
+def unpack_lower(p):
+    h = p.shape[-1]
+    low_left, folded, diag = p[..., :h, :], p[..., h:2 * h, :], p[..., 2 * h, :]
+    top = jnp.tril(folded, -1) + diag[..., :, None] * jnp.eye(h, dtype=p.dtype)
+    low_right = jnp.swapaxes(jnp.triu(folded), -1, -2)
+    upper = jnp.concatenate([top, jnp.zeros_like(top)], axis=-1)
+    lower = jnp.concatenate([low_left, low_right], axis=-1)
+    return jnp.concatenate([upper, lower], axis=-2)
+
+
 def on_device(hidden, sketch):
     states = hidden[0]
     projected = jnp.dot(states, sketch, preferred_element_type=jnp.float32).astype(jnp.bfloat16)
@@ -45,7 +62,7 @@
     factor = jnp.linalg.cholesky(gram_total)
     eye = jnp.eye(basis_width, dtype=jnp.float32)
     inverse = lax.linalg.triangular_solve(factor, eye, left_side=True, lower=True)
-    inverses = gather_all(inverse, "mdl", models)
+    inverses = unpack_lower(gather_all(pack_lower(inverse), "mdl", models))
     left_done = jnp.einsum("ab,bjc->ajc", inverse, row_tiles, precision=HIGH)
     right_done = jnp.einsum("ajc,jdc->ajd", left_done, inverses, precision=HIGH)
     cross_gram = right_done.reshape(basis_width, models * basis_width)

time: 288 us -> 276 us (0.958)
  waiting for transfers between devices: 69.9 us -> 51.2 us
  local copies, waits for them, and re-layouts: 13 us -> 19.6 us
    all_to_all x2, waiting for transfers between devices: 69.9 us -> 51.2 us  [gather_all(): return lax.all_to_all(copies, axes, 0, 0, tiled=True)]
    slice x0 -> x3, local copies, waits for them, and re-layouts: none -> 3.06 us  [the longest x1 2.29 us: unpack_lower(): p[..., :h, :]]
    unnamed x3 -> x6, local copies, waits for them, and re-layouts: 4.62 us -> 7.18 us
    another operation x4 -> x3, other arithmetic: 19.9 us -> 19.9 us  [on_device(): lax.linalg.triangular_solve(factor, eye, left_side=True, lower=True)]
where the time goes in v2:
time: 276 us; the launch traced here: 275 us
  blocking collectives  118 us (43%)
  other arithmetic  58.5 us (21%)
  waiting for transfers between devices  51.2 us (19%)
  local copies, waits for them, and re-layouts  19.6 us (7%)
  matrix products  14.5 us (5%)
  starting transfers between devices  11.2 us (4%)
    all_to_all x2, blocking collectives, scatter_sum(): return lax.all_to_all(chunks, axes, 0, 0, tiled=True).sum(axis=0)  66.6 us
    all_to_all x2, waiting for transfers between devices, gather_all(): return lax.all_to_all(copies, axes, 0, 0, tiled=True)  51.2 us
    all_to_all x2, blocking collectives, gather_all(): return lax.all_to_all(copies, axes, 0, 0, tiled=True)  51 us
    another operation x6, other arithmetic, on_device(): factor = jnp.linalg.cholesky(gram_total)  34 us
    another operation x3, other arithmetic, on_device(): lax.linalg.triangular_solve(factor, eye, left_side=True, lower=True)  19.9 us
    all_to_all x2, starting transfers between devices, gather_all(): return lax.all_to_all(copies, axes, 0, 0, tiled=True)  11.2 us
    unnamed x6, local copies, waits for them, and re-layouts  7.18 us
  transfers between devices with their start and end apart: 2, of which 2 were waited for; matrix products, arithmetic and copies ran while one was open for 2% of the time, Pallas kernels for 0%

profile of v2, /device:TPU:1, one launch (start us, length us, event | category | flops | bytes accessed | tf_op | source)
XLA Modules:
  0.0 274.9 jit_solution(4306385606125737312)
XLA Ops:
  0.6 1.7 copy-done
  2.4 2.6 fusion.10
  5.0 0.1 copy.37
  5.1 30.2 %all_to_all.30 = bf16[8,256,256]{1,2,0:T(8,128)(2,1)S(1)} all-to-all(bf16[8,256,256]{1,2,0:T(8,128)(2,1)S(1)} %broadcast_in_dim.31), channel_id=1, replica_groups=mesh['x'=4,'z'=12,'c'=2,'mdl'=8] {'mdl'}, dimensions={0} | all-to-all | bytes 2097152 | tf_op jit(solution)/shard_map/all_to_all | solution.py:16
  35.3 0.5 convolution_bitcast_fusion
  35.8 37.6 %all_to_all.31 = f32[8,256,256]{2,1,0:T(8,128)} all-to-all(f32[8,256,256]{2,1,0:T(8,128)S(1)} %convolution_bitcast_fusion), channel_id=1, replica_groups=mesh['x'=4,'z'=12,'c'=2,'mdl'=8] {'x','c'}, dimensions={0} | all-to-all | bytes 4194304 | tf_op jit(solution)/shard_map/all_to_all | solution.py:11
  73.4 1.8 reduce_sum.27
  75.3 28.9 %all_to_all.32 = f32[12,22,256]{2,1,0:T(8,128)S(1)} all-to-all(f32[12,22,256]{2,1,0:T(8,128)S(1)} %reshape.62), channel_id=1, replica_groups=mesh['x'=4,'z'=12,'c'=2,'mdl'=8] {'z'}, dimensions={0} | all-to-all | bytes 540672 | tf_op jit(solution)/shard_map/all_to_all | solution.py:11
  104.2 20.9 %all_to_all.33 = f32[12,22,256]{2,1,0:T(8,128)S(1)} all-to-all(f32[12,22,256]{2,1,0:T(8,128)S(1)} %broadcast_in_dim.32), channel_id=1, replica_groups=mesh['x'=4,'z'=12,'c'=2,'mdl'=8] {'z'}, dimensions={0} | all-to-all | bytes 540672 | tf_op jit(solution)/shard_map/all_to_all | solution.py:16
  125.2 1.5 broadcast_in_dim.35
  126.7 7.0 %all-to-all-start.4 = ((f32[8,256,256]{2,1,0:T(8,128)}), f32[8,256,256]{2,1,0:T(8,128)}, u32[]{:S(2)}, u32[]{:S(2)}) async-start(f32[8,256,256]{2,1,0:T(8,128)} %broadcast_in_dim.35), calls=%async_computation.4 | async-start | bytes 4194304 | tf_op jit(solution)/shard_map/all_to_all | solution.py:16
  133.7 26.4 %all-to-all-done.4 = f32[8,256,256]{2,1,0:T(8,128)} async-done(((f32[8,256,256]{2,1,0:T(8,128)}), f32[8,256,256]{2,1,0:T(8,128)}, u32[]{:S(2)}, u32[]{:S(2)}) %all-to-all-start.4) | async-done | bytes 2097184 | tf_op jit(solution)/shard_map/all_to_all | solution.py:16
  160.1 1.0 constant_dynamic-slice_fusion.1
  161.1 0.1 copy.39
  161.2 1.0 fusion.18
  162.2 11.7 %cholesky.48 = f32[128,128]{1,0:T(8,128)S(1)} custom-call(f32[128,128]{1,0:T(8,128)S(1)} %cholesky.114), custom_call_target="Cholesky" | custom-call | tf_op jit(solution)/shard_map/jit(cholesky)/cholesky | solution.py:62
  174.0 9.8 %custom-call.14 = f32[1,128,128]{1,2,0:T(8,128)S(1)} custom-call(f32[1,128,128]{2,1,0:T(8,128)S(1)} %get-tuple-element.39), custom_call_target="InvertDiagBlocksLowerTriangular" | custom-call | tf_op jit(solution)/shard_map/jit(cholesky)/cholesky | solution.py:62
  183.8 0.2 constant_dynamic-update-slice_fusion.1
  184.0 0.3 convolution_subtract_fusion.1
  184.3 11.7 %cholesky.101 = f32[128,128]{1,0:T(8,128)S(1)} custom-call(f32[128,128]{1,0:T(8,128)S(1)} %convolution_subtract_fusion.1), custom_call_target="Cholesky" | custom-call | tf_op jit(solution)/shard_map/jit(cholesky)/cholesky | solution.py:62
  196.0 0.7 compare_reduce_fusion
  198.1 3.9 %while.1 = (s32[]{:T(128)}, f32[256,256]{1,0:T(8,128)S(1)}, s32[2,2]{1,0:T(2,128)S(1)}, f32[2,128,128]{2,1,0:T(8,128)S(1)}, s32[]{:T(128)}) while((s32[]{:T(128)}, f32[256,256]{1,0:T(8,128)S(1)}, s32[2,2]{1,0:T(2,128)S(1)}, f32[2,128,128]{2,1,0:T(8,128)S(1)}, s32[]{:T(128)}) %tuple.36), condition=%wide.while_cond, body=%wide.while_body.sunk | while | flops 2 | bytes 131189 | solution.py:64
  198.1 0.6 fusion.42
  198.7 1.4 bitcast_dynamic-update-slice_fusion.2
  200.0 0.6 fusion.42
  200.6 1.4 bitcast_dynamic-update-slice_fusion.2
  202.0 19.9 %custom-call.15 = f32[2,128,128]{1,2,0:T(8,128)S(1)} custom-call(f32[2,128,128]{2,1,0:T(8,128)S(1)} %get-tuple-element.9), custom_call_target="InvertDiagBlocksLowerTriangular" | custom-call | tf_op jit(solution)/shard_map/triangular_solve | solution.py:64
  221.9 0.3 fusion.20
  222.2 0.3 convolution_subtract_fusion
  222.4 0.3 fusion.23
  222.8 0.1 copy.50
  222.9 0.1 bitcast_add_fusion.1
  223.0 1.2 gather_fusion
  224.2 1.1 broadcast_in_dim.57
  225.3 4.3 %all-to-all-start.5 = ((f32[8,257,128]{2,1,0:T(8,128)}), f32[8,257,128]{2,1,0:T(8,128)}, u32[]{:S(2)}, u32[]{:S(2)}) async-start(f32[8,257,128]{2,1,0:T(8,128)} %broadcast_in_dim.57), calls=%async_computation.5 | async-start | bytes 2162688 | tf_op jit(solution)/shard_map/all_to_all | solution.py:16
  229.6 0.1 iota_compare_fusion.6
  229.7 0.1 copy.36
  229.8 0.1 copy.44
  229.9 4.8 %fusion.8 = f32[256,8,256]{2,0,1:T(8,128)} fusion(f32[8,256,256]{2,1,0:T(8,128)} %all-to-all-done.4, f32[128,256]{1,0:T(8,128)S(1)} %fusion.23, f32[128,256]{1,0:T(8,128)S(1)} %fusion.20), kind=kOutput, calls=%fused_computation.14 | convolution fusion | flops 1610678272 | bytes 4456448 | tf_op jit(solution)/shard_map/ab,bjc->ajc/dot_general | solution.py:66
  234.7 24.8 %all-to-all-done.5 = f32[8,257,128]{2,1,0:T(8,128)} async-done(((f32[8,257,128]{2,1,0:T(8,128)}), f32[8,257,128]{2,1,0:T(8,128)}, u32[]{:S(2)}, u32[]{:S(2)}) %all-to-all-start.5) | async-done | bytes 1052704 | tf_op jit(solution)/shard_map/all_to_all | solution.py:16
  259.5 2.3 fusion.33
  261.8 1.2 copy.51
  263.0 0.8 slice.92
  263.8 1.1 select_bitcast_fusion
  264.9 1.2 copy.53
  266.2 5.3 %fusion.7 = (f32[8]{0:T(128)S(1)}, f32[8,256,256]{2,1,0:T(8,128)}) fusion(f32[256,8,256]{2,0,1:T(8,128)} %fusion.8, f32[8,128,128]{2,1,0:T(8,128)S(1)} %copy.53, f32[8,128,128]{2,1,0:T(8,128)} %get-tuple-element.30, f32[8,128,128]{2,1,0:T(8,128)} %get-tuple-element.28), kind=kOutput, calls=%fused_computation.13 | convolution fusion | flops 1613758464 | bytes 5767200 | tf_op jit(solution)/shard_map/ajc,jdc->ajd/dot_general | solution.py:67
  271.5 0.5 multiply_bitcast_fusion
  272.0 2.9 %copy.46 = f32[256,2048]{1,0:T(8,128)} copy(f32[256,2048]{0,1:T(8,128)} %bitcast.80) | data formatting | bytes 4194304
  (24 shorter events, 0.5 us)
Async XLA Ops:
  0.6 1.7 copy-start
  126.7 33.4 %all-to-all-start.4 = ((f32[8,256,256]{2,1,0:T(8,128)}), f32[8,256,256]{2,1,0:T(8,128)}, u32[]{:S(2)}, u32[]{:S(2)}) async-start(f32[8,256,256]{2,1,0:T(8,128)} %broadcast_in_dim.35), calls=%async_computation.4 | async-start | bytes 4194304 | tf_op jit(solution)/shard_map/all_to_all | solution.py:16
  225.3 34.2 %all-to-all-start.5 = ((f32[8,257,128]{2,1,0:T(8,128)}), f32[8,257,128]{2,1,0:T(8,128)}, u32[]{:S(2)}, u32[]{:S(2)}) async-start(f32[8,257,128]{2,1,0:T(8,128)} %broadcast_in_dim.57), calls=%async_computation.5 | async-start | bytes 2162688 | tf_op jit(solution)/shard_map/all_to_all | solution.py:16

commit v3 on v2

--- a/solution.py
+++ b/solution.py
@@ -47,26 +47,50 @@
     return jnp.concatenate([upper, lower], axis=-2)
 
 
+def to_halves(a):
+    w = a.shape[-1] // 2
+    return jnp.concatenate([a[..., :w], a[..., w:]], axis=-2)
+
+
+def symmetric(lower):
+    return lower + lower.T - jnp.diag(jnp.diagonal(lower))
+
+
 def on_device(hidden, sketch):
     states = hidden[0]
     projected = jnp.dot(states, sketch, preferred_element_type=jnp.float32).astype(jnp.bfloat16)
-    basis_width = projected.shape[1]
+    tokens, width = projected.shape
     models = lax.axis_size("mdl")
     me = lax.axis_index("mdl")
+    inner, outer = ("x", "c"), "z"
+    n_out = lax.axis_size(outer)
+    assert lax.axis_size(inner) == models
     everyone = gather_all(projected, "mdl", models)
-    everyone = everyone.transpose(1, 0, 2).reshape(projected.shape[0], models * basis_width)
-    local_row = jnp.dot(projected.T, everyone, preferred_element_type=jnp.float32)
-    row_sums = sum_over_tokens(local_row, ("x", "c"), "z")
-    row_tiles = row_sums.reshape(basis_width, models, basis_width)
-    gram_total = lax.dynamic_index_in_dim(row_tiles, me, 1, keepdims=False)
-    factor = jnp.linalg.cholesky(gram_total)
-    eye = jnp.eye(basis_width, dtype=jnp.float32)
+    local_row = jnp.einsum("ta,jtc->jac", projected, everyone, preferred_element_type=jnp.float32)
+    local_grams = jnp.einsum("jta,jtc->jac", everyone, everyone, preferred_element_type=jnp.float32)
+    packed_grams = jax.vmap(pack_lower)(jnp.tril(local_grams))
+    payload = jnp.concatenate([to_halves(local_row), packed_grams], axis=1)
+    part = scatter_sum(payload, inner)
+    rows = part.shape[0]
+    pad = (-rows) % n_out
+    padded = jnp.pad(part, ((0, pad), (0, 0))).reshape(n_out, (rows + pad) // n_out, part.shape[1])
+    piece = scatter_sum(padded, outer)
+    part = gather_all(piece, outer, n_out).reshape(rows + pad, part.shape[1])[:rows]
+    half = width // 2
+    tile = jnp.concatenate([part[:width], part[width:2 * width]], axis=1)
+    gram = symmetric(unpack_lower(part[2 * width:]))
+    factor = jnp.linalg.cholesky(gram)
+    eye = jnp.eye(width, dtype=jnp.float32)
     inverse = lax.linalg.triangular_solve(factor, eye, left_side=True, lower=True)
-    inverses = unpack_lower(gather_all(pack_lower(inverse), "mdl", models))
-    left_done = jnp.einsum("ab,bjc->ajc", inverse, row_tiles, precision=HIGH)
-    right_done = jnp.einsum("ajc,jdc->ajd", left_done, inverses, precision=HIGH)
-    cross_gram = right_done.reshape(basis_width, models * basis_width)
-    similarity = jnp.sum(right_done * right_done, axis=(0, 2)) / basis_width
+    right_done = jnp.dot(tile, inverse.T, precision=HIGH)
+    sent = jnp.concatenate([to_halves(right_done), pack_lower(inverse)], axis=0)
+    got = gather_all(sent, inner, models)
+    row = got[:, :2 * width].reshape(models, 2, width, half).transpose(2, 0, 1, 3).reshape(width, models, width)
+    inverses = unpack_lower(got[:, 2 * width:])
+    mine = lax.dynamic_index_in_dim(inverses, me, 0, keepdims=False)
+    done = jnp.einsum("ab,bkc->akc", mine, row, precision=HIGH)
+    cross_gram = done.reshape(width, models * width)
+    similarity = jnp.sum(done * done, axis=(0, 2)) / width
     return (cross_gram, similarity[None, :])
 
 

time: 276 us -> 318 us (1.15)
  blocking collectives: 118 us -> 83.1 us
  local copies, waits for them, and re-layouts: 19.6 us -> 49.2 us
  waiting for transfers between devices: 51.2 us -> 79.6 us
  starting transfers between devices: 11.2 us -> 21.5 us
  other arithmetic: 58.5 us -> 65.4 us
    all_to_all x2 -> x0, blocking collectives: 51 us -> none  [gather_all(): return lax.all_to_all(copies, axes, 0, 0, tiled=True)]
    all_to_all x2 -> x3, waiting for transfers between devices: 51.2 us -> 79.6 us  [gather_all(): return lax.all_to_all(copies, axes, 0, 0, tiled=True)]
    all_to_all x2, blocking collectives: 66.6 us -> 83.1 us  [scatter_sum(): return lax.all_to_all(chunks, axes, 0, 0, tiled=True).sum(axis=0)]
    slice x1 -> x5, local copies, waits for them, and re-layouts: 0.02 us -> 13.2 us  [the longest x2 7.4 us: pack_lower(): top, low_right = (m[:h, :h], m[h:, h:])]
    all_to_all x2 -> x3, starting transfers between devices: 11.2 us -> 21.5 us  [gather_all(): return lax.all_to_all(copies, axes, 0, 0, tiled=True)]
    unnamed x6 -> x25, local copies, waits for them, and re-layouts: 7.18 us -> 10.3 us
    dot_general x3 -> x4, matrix products: 10.6 us -> 9.01 us  [the longest x1 4.81 us: on_device(): done = jnp.einsum('ab,bkc->akc', mine, row, precision=HIGH)]
  transfers between devices with their start and end apart: 2 -> 3, of which waited for: 2 -> 3; matrix products, arithmetic and copies ran while one was open for 2% -> 0% of each run, Pallas kernels for 0% -> 0%
where the time goes in v3:
time: 318 us; the launch traced here: 317 us
  blocking collectives  83.1 us (26%)
  waiting for transfers between devices  79.6 us (25%)
  other arithmetic  65.4 us (21%)
  local copies, waits for them, and re-layouts  49.2 us (15%)
  starting transfers between devices  21.5 us (7%)
  matrix products  15.4 us (5%)
    all_to_all x2, blocking collectives, scatter_sum(): return lax.all_to_all(chunks, axes, 0, 0, tiled=True).sum(axis=0)  83.1 us
    all_to_all x3, waiting for transfers between devices, gather_all(): return lax.all_to_all(copies, axes, 0, 0, tiled=True)  79.6 us
    another operation x6, other arithmetic, on_device(): factor = jnp.linalg.cholesky(gram)  34.2 us
    all_to_all x3, starting transfers between devices, gather_all(): return lax.all_to_all(copies, axes, 0, 0, tiled=True)  21.5 us
    another operation x3, other arithmetic, on_device(): lax.linalg.triangular_solve(factor, eye, left_side=True, lower=True)  20.5 us
    unnamed x25, local copies, waits for them, and re-layouts  10.3 us
    slice x2, local copies, waits for them, and re-layouts, pack_lower(): top, low_right = (m[:h, :h], m[h:, h:])  7.4 us
  transfers between devices with their start and end apart: 3, of which 3 were waited for; matrix products, arithmetic and copies ran while one was open for 0% of the time, Pallas kernels for 0%

profile of v3, /device:TPU:1, one launch (start us, length us, event | category | flops | bytes accessed | tf_op | source)
XLA Modules:
  0.0 316.5 jit_solution(780189061156343787)
XLA Ops:
  0.6 1.7 copy-done
  2.4 2.6 fusion.2
  5.0 1.0 broadcast_in_dim.96
  6.0 7.7 %all-to-all-start = ((bf16[8,256,256]{2,1,0:T(8,128)(2,1)}), bf16[8,256,256]{2,1,0:T(8,128)(2,1)}, u32[]{:S(2)}, u32[]{:S(2)}) async-start(bf16[8,256,256]{2,1,0:T(8,128)(2,1)} %broadcast_in_dim.96), calls=%async_computation | async-start | bytes 2097152 | tf_op jit(solution)/shard_map/all_to_all | solution.py:16
  13.7 24.2 %all-to-all-done = bf16[8,256,256]{2,1,0:T(8,128)(2,1)} async-done(((bf16[8,256,256]{2,1,0:T(8,128)(2,1)}), bf16[8,256,256]{2,1,0:T(8,128)(2,1)}, u32[]{:S(2)}, u32[]{:S(2)}) %all-to-all-start) | async-done | bytes 1048608 | tf_op jit(solution)/shard_map/all_to_all | solution.py:16
  37.9 1.7 convolution_bitcast_fusion
  39.6 1.0 slice_dynamic-update-slice_fusion.1
  40.7 1.1 slice_dynamic-update-slice_fusion
  41.7 2.1 convolution_select_fusion
  43.8 1.3 copy-done.1
  45.1 1.1 fusion.41
  46.2 2.0 copy.70
  48.3 2.0 copy.67
  50.3 7.4 %copy.68 = f32[8,128,128]{0,2,1:T(8,128)} copy(f32[8,128,128]{1,2,0:T(8,128)S(1)} %get-tuple-element.41) | data formatting | bytes 1048576 | tf_op jit(solution)/shard_map/vmap()/slice | solution.py:35
  57.7 1.8 gather_fusion
  59.5 1.9 constant_dynamic-update-slice_fusion
  61.4 2.1 fusion.6
  63.5 1.4 dynamic-update-slice.20
  64.9 48.7 %all_to_all.25 = f32[8,769,128]{2,1,0:T(8,128)} all-to-all(f32[8,769,128]{2,1,0:T(8,128)} %dynamic-update-slice.20), channel_id=1, replica_groups=mesh['x'=4,'z'=12,'c'=2,'mdl'=8] {'x','c'}, dimensions={0} | all-to-all | bytes 6299648 | tf_op jit(solution)/shard_map/all_to_all | solution.py:11
  113.6 2.1 reduce_sum.27
  115.8 34.4 %all_to_all.26 = f32[12,65,128]{2,1,0:T(8,128)S(1)} all-to-all(f32[12,65,128]{2,1,0:T(8,128)S(1)} %reshape.61), channel_id=1, replica_groups=mesh['x'=4,'z'=12,'c'=2,'mdl'=8] {'z'}, dimensions={0} | all-to-all | bytes 798720 | tf_op jit(solution)/shard_map/all_to_all | solution.py:11
  150.2 0.8 broadcast_in_dim.101
  151.0 5.4 %all-to-all-start.3 = ((f32[12,65,128]{2,1,0:T(8,128)}), f32[12,65,128]{2,1,0:T(8,128)S(1)}, u32[]{:S(2)}, u32[]{:S(2)}) async-start(f32[12,65,128]{2,1,0:T(8,128)} %broadcast_in_dim.101), calls=%async_computation.3 | async-start | bytes 884736 | tf_op jit(solution)/shard_map/all_to_all | solution.py:16
  157.1 17.6 %all-to-all-done.3 = f32[12,65,128]{2,1,0:T(8,128)S(1)} async-done(((f32[12,65,128]{2,1,0:T(8,128)}), f32[12,65,128]{2,1,0:T(8,128)S(1)}, u32[]{:S(2)}, u32[]{:S(2)}) %all-to-all-start.3) | async-done | bytes 399392 | tf_op jit(solution)/shard_map/all_to_all | solution.py:16
  175.9 2.3 gather_fusion.1
  178.5 11.7 %cholesky.48 = f32[128,128]{1,0:T(8,128)S(1)} custom-call(f32[128,128]{1,0:T(8,128)S(1)} %cholesky.112), custom_call_target="Cholesky" | custom-call | tf_op jit(solution)/shard_map/jit(cholesky)/cholesky | solution.py:82
  190.5 9.8 %custom-call.14 = f32[1,128,128]{1,2,0:T(8,128)S(1)} custom-call(f32[1,128,128]{2,1,0:T(8,128)S(1)} %copy.77), custom_call_target="InvertDiagBlocksLowerTriangular" | custom-call | tf_op jit(solution)/shard_map/jit(cholesky)/cholesky | solution.py:82
  200.9 11.7 %cholesky.100 = f32[128,128]{1,0:T(8,128)S(1)} custom-call(f32[128,128]{1,0:T(8,128)S(1)} %convolution_subtract_fusion.1), custom_call_target="Cholesky" | custom-call | tf_op jit(solution)/shard_map/jit(cholesky)/cholesky | solution.py:82
  215.0 5.4 %while.1 = (s32[]{:T(128)}, f32[256,256]{0,1:T(8,128)S(1)}, s32[2,2]{1,0:T(2,128)S(1)}, f32[2,128,128]{2,1,0:T(8,128)}, s32[]{:T(128)}) while((s32[]{:T(128)}, f32[256,256]{0,1:T(8,128)S(1)}, s32[2,2]{1,0:T(2,128)S(1)}, f32[2,128,128]{2,1,0:T(8,128)}, s32[]{:T(128)}) %tuple.40), condition=%wide.while_cond, body=%wide.while_body.sunk | while | flops 2 | bytes 393329 | solution.py:84
  215.6 1.3 dynamic-slice.7
  218.3 1.3 dynamic-slice.7
  220.4 20.5 %custom-call.15 = f32[2,128,128]{1,2,0:T(8,128)S(1)} custom-call(f32[2,128,128]{2,1,0:T(8,128)} %get-tuple-element.9), custom_call_target="InvertDiagBlocksLowerTriangular" | custom-call | tf_op jit(solution)/shard_map/triangular_solve | solution.py:84
  240.9 1.1 fusion.26
  242.0 1.1 convolution_subtract_fusion
  243.1 1.2 fusion.30
  244.4 1.3 gather_fusion.2
  246.8 0.9 copy.85
  247.8 1.9 broadcast_in_dim.106
  249.7 8.4 %all-to-all-start.4 = ((f32[8,769,128]{2,1,0:T(8,128)}), f32[8,769,128]{2,1,0:T(8,128)}, u32[]{:S(2)}, u32[]{:S(2)}) async-start(f32[8,769,128]{2,1,0:T(8,128)} %broadcast_in_dim.106), calls=%async_computation.4 | async-start | bytes 6356992 | tf_op jit(solution)/shard_map/all_to_all | solution.py:16
  258.4 37.8 %all-to-all-done.4 = f32[8,769,128]{2,1,0:T(8,128)} async-done(((f32[8,769,128]{2,1,0:T(8,128)}), f32[8,769,128]{2,1,0:T(8,128)}, u32[]{:S(2)}, u32[]{:S(2)}) %all-to-all-start.4) | async-done | bytes 3149856 | tf_op jit(solution)/shard_map/all_to_all | solution.py:16
  296.2 3.1 slice.169
  299.2 2.9 copy.90
  302.1 0.8 slice.167
  302.9 2.3 multiply_add_fusion
  305.2 2.0 copy.89
  307.2 1.1 select_bitcast_fusion
  308.3 4.8 %multiply_reduce_fusion = (f32[8]{0:T(128)S(1)}, f32[256,8,256]{0,2,1:T(8,128)}) fusion(f32[256,8,256]{0,2,1:T(8,128)} %bitcast.86, s32[]{:T(128)S(6)} %select_n.61, f32[8,128,128]{2,1,0:T(8,128)} %get-tuple-element.39, f32[8,128,128]{2,1,0:T(8,128)S(1)} %select_bitcast_fusion, f32[8,128,128]{2,1,0:T(8,128)S(1)} %get-tuple-element.38), kind=kOutput, calls=%fused_computation.10 | convolution fusion | flops 1611923456 | bytes 5767204 | tf_op jit(solution)/shard_map/ab,bkc->akc/dot_general | solution.py:91
  313.1 2.9 copy.91
  (71 shorter events, 8.8 us)
Async XLA Ops:
  0.6 1.7 copy-start
  6.0 31.9 %all-to-all-start = ((bf16[8,256,256]{2,1,0:T(8,128)(2,1)}), bf16[8,256,256]{2,1,0:T(8,128)(2,1)}, u32[]{:S(2)}, u32[]{:S(2)}) async-start(bf16[8,256,256]{2,1,0:T(8,128)(2,1)} %broadcast_in_dim.96), calls=%async_computation | async-start | bytes 2097152 | tf_op jit(solution)/shard_map/all_to_all | solution.py:16
  13.7 30.1 %copy-start.4 = (pred[128,128]{0,1:T(8,128)(4,1)}, pred[128,128]{0,1:T(8,128)(4,1)S(1)}, u32[]{:S(2)}) copy-start(pred[128,128]{0,1:T(8,128)(4,1)S(1)} %iota_compare_fusion.7) | copy-start | bytes 49156
  43.8 1.3 copy-start.1
  151.0 23.7 %all-to-all-start.3 = ((f32[12,65,128]{2,1,0:T(8,128)}), f32[12,65,128]{2,1,0:T(8,128)S(1)}, u32[]{:S(2)}, u32[]{:S(2)}) async-start(f32[12,65,128]{2,1,0:T(8,128)} %broadcast_in_dim.101), calls=%async_computation.3 | async-start | bytes 884736 | tf_op jit(solution)/shard_map/all_to_all | solution.py:16
  200.8 45.5 %copy-start.2 = (f32[256,128]{1,0:T(8,128)S(1)}, f32[256,128]{1,0:T(8,128)}, u32[]{:S(2)}) copy-start(f32[256,128]{1,0:T(8,128)} %get-tuple-element.46) | copy-start | bytes 393220
  200.8 45.5 %copy-start.3 = (f32[256,128]{1,0:T(8,128)S(1)}, f32[256,128]{1,0:T(8,128)}, u32[]{:S(2)}) copy-start(f32[256,128]{1,0:T(8,128)} %get-tuple-element.47) | copy-start | bytes 393220
  240.9 2.2 copy-start.6
  249.7 8.5 %copy-start.5 = (pred[128,128]{0,1:T(8,128)(4,1)S(1)}, pred[128,128]{0,1:T(8,128)(4,1)}, u32[]{:S(2)}) copy-start(pred[128,128]{0,1:T(8,128)(4,1)} %copy-done.4) | copy-start | bytes 49156
  249.7 46.5 %all-to-all-start.4 = ((f32[8,769,128]{2,1,0:T(8,128)}), f32[8,769,128]{2,1,0:T(8,128)}, u32[]{:S(2)}, u32[]{:S(2)}) async-start(f32[8,769,128]{2,1,0:T(8,128)} %broadcast_in_dim.106), calls=%async_computation.4 | async-start | bytes 6356992 | tf_op jit(solution)/shard_map/all_to_all | solution.py:16

commit v4 on v2

--- a/solution.py
+++ b/solution.py
@@ -16,18 +16,34 @@
     return lax.all_to_all(copies, axes, 0, 0, tiled=True)
 
 
-def sum_over_tokens(row, inner, outer):
-    rows, cols = row.shape
-    n_in = lax.axis_size(inner)
+def swap_halves_sum(row, axis):
+    cols = row.shape[1]
+    side = lax.axis_index(axis)
+    halves = row.reshape(row.shape[0], 2, cols // 2)
+    mine = lax.dynamic_index_in_dim(halves, side, 1, keepdims=False)
+    theirs = lax.dynamic_index_in_dim(halves, 1 - side, 1, keepdims=False)
+    return mine + lax.ppermute(theirs, axis, [(0, 1), (1, 0)])
+
+
+def swap_halves_join(half, axis):
+    side = lax.axis_index(axis)
+    other = lax.ppermute(half, axis, [(0, 1), (1, 0)])
+    return jnp.where(side == 0, jnp.concatenate([half, other], 1), jnp.concatenate([other, half], 1))
+
+
+def sum_over_tokens(row, pair, ring, outer):
+    rows = row.shape[0]
+    n_ring = lax.axis_size(ring)
     n_out = lax.axis_size(outer)
-    width = cols // n_in
-    part = scatter_sum(row.reshape(rows, n_in, width).transpose(1, 0, 2), inner)
+    part = swap_halves_sum(row, pair)
+    width = part.shape[1] // n_ring
+    part = scatter_sum(part.reshape(rows, n_ring, width).transpose(1, 0, 2), ring)
     pad = (-rows) % n_out
     padded = jnp.pad(part, ((0, pad), (0, 0))).reshape(n_out, (rows + pad) // n_out, width)
     piece = scatter_sum(padded, outer)
     part = gather_all(piece, outer, n_out).reshape(rows + pad, width)[:rows]
-    full = gather_all(part, inner, n_in)
-    return full.transpose(1, 0, 2).reshape(rows, cols)
+    part = gather_all(part, ring, n_ring).transpose(1, 0, 2).reshape(rows, n_ring * width)
+    return swap_halves_join(part, pair)
 
 
 def pack_lower(m):
@@ -56,7 +72,7 @@
     everyone = gather_all(projected, "mdl", models)
     everyone = everyone.transpose(1, 0, 2).reshape(projected.shape[0], models * basis_width)
     local_row = jnp.dot(projected.T, everyone, preferred_element_type=jnp.float32)
-    row_sums = sum_over_tokens(local_row, ("x", "c"), "z")
+    row_sums = sum_over_tokens(local_row, "c", "x", "z")
     row_tiles = row_sums.reshape(basis_width, models, basis_width)
     gram_total = lax.dynamic_index_in_dim(row_tiles, me, 1, keepdims=False)
     factor = jnp.linalg.cholesky(gram_total)

time: 276 us -> 274 us (level); the launches traced: 275 us -> 269 us
  blocking collectives: 118 us -> 82.4 us
  starting transfers between devices: 11.2 us -> 26.1 us
  local copies, waits for them, and re-layouts: 19.6 us -> 27.3 us
  other arithmetic: 58.5 us -> 63.3 us
    all_to_all x2, blocking collectives: 66.6 us -> 47.6 us  [scatter_sum(): return lax.all_to_all(chunks, axes, 0, 0, tiled=True).sum(axis=0)]
    all_to_all x2, blocking collectives: 51 us -> 34.8 us  [gather_all(): return lax.all_to_all(copies, axes, 0, 0, tiled=True)]
    ppermute x0 -> x2, starting transfers between devices: none -> 14.2 us  [the longest x1 7.49 us: swap_halves_sum(): return mine + lax.ppermute(theirs, axis, [(0, 1), (1, 0)])]
    ppermute x0 -> x2, waiting for transfers between devices: none -> 4.95 us  [the longest x1 2.61 us: swap_halves_sum(): return mine + lax.ppermute(theirs, axis, [(0, 1), (1, 0)])]
    all_to_all x2, waiting for transfers between devices: 51.2 us -> 46.7 us  [gather_all(): return lax.all_to_all(copies, axes, 0, 0, tiled=True)]
    unnamed x6 -> x10, local copies, waits for them, and re-layouts: 7.18 us -> 9.8 us
  transfers between devices with their start and end apart: 2 -> 4, of which waited for: 2 -> 4; matrix products, arithmetic and copies ran while one was open for 2% -> 2% of each run, Pallas kernels for 0% -> 0%
where the time goes in v4:
time: 274 us; the launch traced here: 269 us
  blocking collectives  82.4 us (30%)
  other arithmetic  63.3 us (23%)
  waiting for transfers between devices  51.6 us (19%)
  local copies, waits for them, and re-layouts  27.3 us (10%)
  starting transfers between devices  26.1 us (10%)
  matrix products  15.8 us (6%)
    all_to_all x2, blocking collectives, scatter_sum(): return lax.all_to_all(chunks, axes, 0, 0, tiled=True).sum(axis=0)  47.6 us
    all_to_all x2, waiting for transfers between devices, gather_all(): return lax.all_to_all(copies, axes, 0, 0, tiled=True)  46.7 us
    all_to_all x2, blocking collectives, gather_all(): return lax.all_to_all(copies, axes, 0, 0, tiled=True)  34.8 us
    another operation x6, other arithmetic, on_device(): factor = jnp.linalg.cholesky(gram_total)  34 us
    another operation x3, other arithmetic, on_device(): lax.linalg.triangular_solve(factor, eye, left_side=True, lower=True)  19.7 us
    all_to_all x2, starting transfers between devices, gather_all(): return lax.all_to_all(copies, axes, 0, 0, tiled=True)  11.9 us
    unnamed x10, local copies, waits for them, and re-layouts  9.8 us
    ppermute x1, starting transfers between devices, swap_halves_sum(): return mine + lax.ppermute(theirs, axis, [(0, 1), (1, 0)])  7.49 us
  transfers between devices with their start and end apart: 4, of which 4 were waited for; matrix products, arithmetic and copies ran while one was open for 2% of the time, Pallas kernels for 0%

profile of v4, /device:TPU:1, one launch (start us, length us, event | category | flops | bytes accessed | tf_op | source)
XLA Modules:
  0.0 268.9 jit_solution(15904408606862776539)
XLA Ops:
  0.6 1.7 copy-done
  2.4 2.6 fusion.8
  5.1 1.0 broadcast_in_dim.31
  6.1 7.7 %all-to-all-start = ((bf16[8,256,256]{1,2,0:T(8,128)(2,1)}), bf16[8,256,256]{1,2,0:T(8,128)(2,1)}, u32[]{:S(2)}, u32[]{:S(2)}) async-start(bf16[8,256,256]{1,2,0:T(8,128)(2,1)} %broadcast_in_dim.31), calls=%async_computation | async-start | bytes 2097152 | tf_op jit(solution)/shard_map/all_to_all | solution.py:16
  13.8 24.2 %all-to-all-done = bf16[8,256,256]{1,2,0:T(8,128)(2,1)} async-done(((bf16[8,256,256]{1,2,0:T(8,128)(2,1)}), bf16[8,256,256]{1,2,0:T(8,128)(2,1)}, u32[]{:S(2)}, u32[]{:S(2)}) %all-to-all-start) | async-done | bytes 1048608 | tf_op jit(solution)/shard_map/all_to_all | solution.py:16
  38.0 1.7 fusion.17
  39.7 1.3 copy-done.2
  41.0 1.1 dynamic-slice_bitcast_fusion
  42.1 7.5 %collective-permute-start = (f32[256,1024]{1,0:T(8,128)}, f32[256,1024]{1,0:T(8,128)}, u32[]{:S(2)}, u32[]{:S(2)}) collective-permute-start(f32[256,1024]{1,0:T(8,128)} %dynamic-slice_bitcast_fusion), channel_id=1, source_target_pairs={{0,8},{8,0},{1,9},{9,1},{2,10},{10,2},{3,11},{11,3},{4,12},{12,4},... | collective-permute-start | bytes 3145736 | tf_op jit(solution)/shard_map/ppermute | solution.py:25
  49.6 2.6 collective-permute-done
  52.2 2.8 %bitcast_add_fusion = f32[256,1024]{1,0:T(8,128)} fusion(f32[256,1024]{1,0:T(8,128)} %collective-permute-done, f32[256,2,1024]{2,0,1:T(8,128)} %copy-done.2, s32[]{:T(128)S(6)} %select_n.41), kind=kLoop, calls=%fused_computation.20 | loop fusion | flops 262144 | bytes 3145732 | tf_op jit(solution)/shard_map/add | solution.py:25
  55.0 2.5 copy.66
  57.5 2.5 copy.67
  60.1 19.1 %all_to_all.30 = f32[4,256,256]{2,1,0:T(8,128)} all-to-all(f32[4,256,256]{2,1,0:T(8,128)} %copy.67), channel_id=1, replica_groups=mesh['x'=4,'z'=12,'c'=2,'mdl'=8] {'x'}, dimensions={0} | all-to-all | bytes 2097152 | tf_op jit(solution)/shard_map/all_to_all | solution.py:11
  79.2 1.3 reduce_sum.27
  80.6 28.5 %all_to_all.31 = f32[12,22,256]{2,1,0:T(8,128)S(1)} all-to-all(f32[12,22,256]{2,1,0:T(8,128)S(1)} %reshape.74), channel_id=1, replica_groups=mesh['x'=4,'z'=12,'c'=2,'mdl'=8] {'z'}, dimensions={0} | all-to-all | bytes 540672 | tf_op jit(solution)/shard_map/all_to_all | solution.py:11
  109.2 20.2 %all_to_all.32 = f32[12,22,256]{2,1,0:T(8,128)S(1)} all-to-all(f32[12,22,256]{2,1,0:T(8,128)S(1)} %broadcast_in_dim.32), channel_id=1, replica_groups=mesh['x'=4,'z'=12,'c'=2,'mdl'=8] {'z'}, dimensions={0} | all-to-all | bytes 540672 | tf_op jit(solution)/shard_map/all_to_all | solution.py:16
  129.7 14.5 %all_to_all.33 = f32[4,256,256]{1,2,0:T(8,128)} all-to-all(f32[4,256,256]{1,2,0:T(8,128)S(1)} %broadcast_in_dim.35), channel_id=1, replica_groups=mesh['x'=4,'z'=12,'c'=2,'mdl'=8] {'x'}, dimensions={0} | all-to-all | bytes 2097152 | tf_op jit(solution)/shard_map/all_to_all | solution.py:16
  144.2 6.7 %collective-permute-start.1 = (f32[256,1024]{0,1:T(8,128)}, f32[256,1024]{0,1:T(8,128)}, u32[]{:S(2)}, u32[]{:S(2)}) collective-permute-start(f32[256,1024]{0,1:T(8,128)} %bitcast.11), channel_id=1, source_target_pairs={{0,8},{8,0},{1,9},{9,1},{2,10},{10,2},{3,11},{11,3},{4,12},{12,4},... | collective-permute-start | bytes 3145736 | tf_op jit(solution)/shard_map/ppermute | solution.py:30
  151.0 2.3 collective-permute-done.1
  153.4 2.6 maximum_select_fusion
  156.0 1.3 copy-done.1
  157.5 1.0 fusion.16
  158.5 11.7 %cholesky.48 = f32[128,128]{1,0:T(8,128)S(1)} custom-call(f32[128,128]{1,0:T(8,128)S(1)} %cholesky.114), custom_call_target="Cholesky" | custom-call | tf_op jit(solution)/shard_map/jit(cholesky)/cholesky | solution.py:78
  170.3 9.8 %custom-call.14 = f32[1,128,128]{1,2,0:T(8,128)S(1)} custom-call(f32[1,128,128]{2,1,0:T(8,128)S(1)} %get-tuple-element.43), custom_call_target="InvertDiagBlocksLowerTriangular" | custom-call | tf_op jit(solution)/shard_map/jit(cholesky)/cholesky | solution.py:78
  180.3 0.3 convolution_subtract_fusion.1
  180.6 11.7 %cholesky.101 = f32[128,128]{1,0:T(8,128)S(1)} custom-call(f32[128,128]{1,0:T(8,128)S(1)} %convolution_subtract_fusion.1), custom_call_target="Cholesky" | custom-call | tf_op jit(solution)/shard_map/jit(cholesky)/cholesky | solution.py:78
  192.3 0.7 compare_reduce_fusion
  194.4 4.2 %while.1 = (s32[]{:T(128)}, f32[256,256]{1,0:T(8,128)S(1)}, s32[2,2]{1,0:T(2,128)S(1)}, f32[2,128,128]{2,1,0:T(8,128)S(1)}, s32[]{:T(128)}) while((s32[]{:T(128)}, f32[256,256]{1,0:T(8,128)S(1)}, s32[2,2]{1,0:T(2,128)S(1)}, f32[2,128,128]{2,1,0:T(8,128)S(1)}, s32[]{:T(128)}) %tuple.38), condition=%wide.while_cond, body=%wide.while_body.sunk | while | flops 2 | bytes 131189 | solution.py:80
  194.6 0.7 fusion.43
  195.3 1.3 bitcast_dynamic-update-slice_fusion.2
  196.6 0.7 fusion.43
  197.3 1.3 bitcast_dynamic-update-slice_fusion.2
  198.6 19.7 %custom-call.15 = f32[2,128,128]{1,2,0:T(8,128)S(1)} custom-call(f32[2,128,128]{2,1,0:T(8,128)S(1)} %get-tuple-element.9), custom_call_target="InvertDiagBlocksLowerTriangular" | custom-call | tf_op jit(solution)/shard_map/triangular_solve | solution.py:80
  218.9 0.3 fusion.22
  219.4 1.2 gather_fusion
  220.7 1.1 broadcast_in_dim.57
  221.7 4.3 %all-to-all-start.5 = ((f32[8,257,128]{2,1,0:T(8,128)}), f32[8,257,128]{2,1,0:T(8,128)}, u32[]{:S(2)}, u32[]{:S(2)}) async-start(f32[8,257,128]{2,1,0:T(8,128)} %broadcast_in_dim.57), calls=%async_computation.5 | async-start | bytes 2162688 | tf_op jit(solution)/shard_map/all_to_all | solution.py:16
  226.3 4.9 %fusion.13 = f32[256,8,256]{2,0,1:T(8,128)} fusion(f32[256,8,256]{0,2,1:T(8,128)} %copy-done.1, f32[128,256]{1,0:T(8,128)S(1)} %fusion.22, f32[128,256]{1,0:T(8,128)S(1)} %fusion.19), kind=kOutput, calls=%fused_computation.26 | convolution fusion | flops 1610678272 | bytes 4456448 | tf_op jit(solution)/shard_map/ab,bjc->ajc/dot_general | solution.py:82
  231.2 22.4 %all-to-all-done.5 = f32[8,257,128]{2,1,0:T(8,128)} async-done(((f32[8,257,128]{2,1,0:T(8,128)}), f32[8,257,128]{2,1,0:T(8,128)}, u32[]{:S(2)}, u32[]{:S(2)}) %all-to-all-start.5) | async-done | bytes 1052704 | tf_op jit(solution)/shard_map/all_to_all | solution.py:16
  253.6 2.3 fusion.32
  255.9 1.2 copy.81
  257.1 0.8 slice.92
  257.9 1.1 select_bitcast_fusion
  259.0 1.2 copy.83
  260.2 5.3 %fusion.7 = (f32[8]{0:T(128)S(1)}, f32[8,256,256]{2,1,0:T(8,128)}) fusion(f32[256,8,256]{2,0,1:T(8,128)} %fusion.13, f32[8,128,128]{2,1,0:T(8,128)S(1)} %copy.83, f32[8,128,128]{2,1,0:T(8,128)} %get-tuple-element.34, f32[8,128,128]{2,1,0:T(8,128)} %get-tuple-element.32), kind=kOutput, calls=%fused_computation.14 | convolution fusion | flops 1613758464 | bytes 5767200 | tf_op jit(solution)/shard_map/ajc,jdc->ajd/dot_general | solution.py:83
  265.5 0.5 multiply_bitcast_fusion
  266.0 2.9 %copy.76 = f32[256,2048]{1,0:T(8,128)} copy(f32[256,2048]{0,1:T(8,128)} %bitcast.86) | data formatting | bytes 4194304
  (38 shorter events, 2.1 us)
Async XLA Ops:
  0.6 1.7 copy-start
  6.1 31.9 %all-to-all-start = ((bf16[8,256,256]{1,2,0:T(8,128)(2,1)}), bf16[8,256,256]{1,2,0:T(8,128)(2,1)}, u32[]{:S(2)}, u32[]{:S(2)}) async-start(bf16[8,256,256]{1,2,0:T(8,128)(2,1)} %broadcast_in_dim.31), calls=%async_computation | async-start | bytes 2097152 | tf_op jit(solution)/shard_map/all_to_all | solution.py:16
  39.7 1.3 copy-start.2
  42.1 10.1 %collective-permute-start = (f32[256,1024]{1,0:T(8,128)}, f32[256,1024]{1,0:T(8,128)}, u32[]{:S(2)}, u32[]{:S(2)}) collective-permute-start(f32[256,1024]{1,0:T(8,128)} %dynamic-slice_bitcast_fusion), channel_id=1, source_target_pairs={{0,8},{8,0},{1,9},{9,1},{2,10},{10,2},{3,11},{11,3},{4,12},{12,4},... | collective-permute-start | bytes 3145736 | tf_op jit(solution)/shard_map/ppermute | solution.py:25
  144.2 9.2 %collective-permute-start.1 = (f32[256,1024]{0,1:T(8,128)}, f32[256,1024]{0,1:T(8,128)}, u32[]{:S(2)}, u32[]{:S(2)}) collective-permute-start(f32[256,1024]{0,1:T(8,128)} %bitcast.11), channel_id=1, source_target_pairs={{0,8},{8,0},{1,9},{9,1},{2,10},{10,2},{3,11},{11,3},{4,12},{12,4},... | collective-permute-start | bytes 3145736 | tf_op jit(solution)/shard_map/ppermute | solution.py:30
  156.0 1.3 copy-start.1
  221.7 31.9 %all-to-all-start.5 = ((f32[8,257,128]{2,1,0:T(8,128)}), f32[8,257,128]{2,1,0:T(8,128)}, u32[]{:S(2)}, u32[]{:S(2)}) async-start(f32[8,257,128]{2,1,0:T(8,128)} %broadcast_in_dim.57), calls=%async_computation.5 | async-start | bytes 2162688 | tf_op jit(solution)/shard_map/all_to_all | solution.py:16

commit v5 on v4

--- a/solution.py
+++ b/solution.py
@@ -63,6 +63,21 @@
     return jnp.concatenate([upper, lower], axis=-2)
 
 
+def factor_inverse(gram):
+    h = gram.shape[0] // 2
+    eye = jnp.eye(h, dtype=gram.dtype)
+    top = jnp.linalg.cholesky(gram[:h, :h])
+    top_inv = lax.linalg.triangular_solve(top, eye, left_side=True, lower=True)
+    low_left = jnp.dot(gram[h:, :h], top_inv.T, precision=HIGH)
+    rest = gram[h:, h:] - jnp.dot(low_left, low_left.T, precision=HIGH)
+    low = jnp.linalg.cholesky(rest)
+    low_inv = lax.linalg.triangular_solve(low, eye, left_side=True, lower=True)
+    mixed = -jnp.dot(low_inv, jnp.dot(low_left, top_inv, precision=HIGH), precision=HIGH)
+    upper = jnp.concatenate([top_inv, jnp.zeros_like(top_inv)], axis=1)
+    lower = jnp.concatenate([mixed, low_inv], axis=1)
+    return jnp.concatenate([upper, lower], axis=0)
+
+
 def on_device(hidden, sketch):
     states = hidden[0]
     projected = jnp.dot(states, sketch, preferred_element_type=jnp.float32).astype(jnp.bfloat16)
@@ -75,9 +90,7 @@
     row_sums = sum_over_tokens(local_row, "c", "x", "z")
     row_tiles = row_sums.reshape(basis_width, models, basis_width)
     gram_total = lax.dynamic_index_in_dim(row_tiles, me, 1, keepdims=False)
-    factor = jnp.linalg.cholesky(gram_total)
-    eye = jnp.eye(basis_width, dtype=jnp.float32)
-    inverse = lax.linalg.triangular_solve(factor, eye, left_side=True, lower=True)
+    inverse = factor_inverse(gram_total)
     inverses = unpack_lower(gather_all(pack_lower(inverse), "mdl", models))
     left_done = jnp.einsum("ab,bjc->ajc", inverse, row_tiles, precision=HIGH)
     right_done = jnp.einsum("ajc,jdc->ajd", left_done, inverses, precision=HIGH)

time: 274 us -> 258 us (0.942)
  other arithmetic: 63.3 us -> 54.2 us
  local copies, waits for them, and re-layouts: 27.3 us -> 23.3 us
    another operation x9 -> x10, other arithmetic: 53.7 us -> 45.7 us  [the longest x3 12.4 us: factor_inverse(): top = jnp.linalg.cholesky(gram[:h, :h])]
    another operation x9 -> x1, local copies, waits for them, and re-layouts: 4.12 us -> 0.09 us  [factor_inverse(): low_inv = lax.linalg.triangular_solve(low, eye, left_side=True, lower=True)]
    unnamed x10 -> x9, local copies, waits for them, and re-layouts: 9.8 us -> 9.72 us
where the time goes in v5:
time: 258 us; the launch traced here: 255 us
  blocking collectives  82.4 us (32%)
  other arithmetic  54.2 us (21%)
  waiting for transfers between devices  52.1 us (20%)
  starting transfers between devices  26.2 us (10%)
  local copies, waits for them, and re-layouts  23.3 us (9%)
  matrix products  16 us (6%)
    all_to_all x2, blocking collectives, scatter_sum(): return lax.all_to_all(chunks, axes, 0, 0, tiled=True).sum(axis=0)  47.6 us
    all_to_all x2, waiting for transfers between devices, gather_all(): return lax.all_to_all(copies, axes, 0, 0, tiled=True)  46.9 us
    all_to_all x2, blocking collectives, gather_all(): return lax.all_to_all(copies, axes, 0, 0, tiled=True)  34.8 us
    another operation x3, other arithmetic, factor_inverse(): top = jnp.linalg.cholesky(gram[:h, :h])  12.4 us
    another operation x3, other arithmetic, factor_inverse(): low = jnp.linalg.cholesky(rest)  12.4 us
    all_to_all x2, starting transfers between devices, gather_all(): return lax.all_to_all(copies, axes, 0, 0, tiled=True)  12.1 us
    another operation x2, other arithmetic, factor_inverse(): top_inv = lax.linalg.triangular_solve(top, eye, left_side=True, lower=True)  10.5 us
    another operation x2, other arithmetic, factor_inverse(): low_inv = lax.linalg.triangular_solve(low, eye, left_side=True, lower=True)  10.5 us
  transfers between devices with their start and end apart: 4, of which 4 were waited for; matrix products, arithmetic and copies ran while one was open for 2% of the time, Pallas kernels for 0%

profile of v5, /device:TPU:1, one launch (start us, length us, event | category | flops | bytes accessed | tf_op | source)
XLA Modules:
  0.0 255.1 jit_solution(11843241347504492425)
XLA Ops:
  0.6 1.7 copy-done
  2.4 2.6 %fusion.8 = bf16[256,256]{1,0:T(8,128)(2,1)S(1)} fusion(bf16[5120,256]{1,0:T(8,128)(2,1)S(1)} %copy-done, bf16[1,256,5120]{2,1,0:T(8,128)(2,1)} %param.5), kind=kOutput, calls=%fused_computation.13 | convolution fusion | flops 671154176 | bytes 5373952 | tf_op jit(solution)/shard_map/dot_general | solution.py:83
  5.1 1.0 broadcast_in_dim.32
  6.1 7.7 %all-to-all-start = ((bf16[8,256,256]{1,2,0:T(8,128)(2,1)}), bf16[8,256,256]{1,2,0:T(8,128)(2,1)}, u32[]{:S(2)}, u32[]{:S(2)}) async-start(bf16[8,256,256]{1,2,0:T(8,128)(2,1)} %broadcast_in_dim.32), calls=%async_computation | async-start | bytes 2097152 | tf_op jit(solution)/shard_map/all_to_all | solution.py:16
  13.8 24.2 %all-to-all-done = bf16[8,256,256]{1,2,0:T(8,128)(2,1)} async-done(((bf16[8,256,256]{1,2,0:T(8,128)(2,1)}), bf16[8,256,256]{1,2,0:T(8,128)(2,1)}, u32[]{:S(2)}, u32[]{:S(2)}) %all-to-all-start) | async-done | bytes 1048608 | tf_op jit(solution)/shard_map/all_to_all | solution.py:16
  38.0 1.7 fusion.22
  39.7 1.3 copy-done.2
  41.0 1.1 dynamic-slice_bitcast_fusion
  42.1 7.5 %collective-permute-start = (f32[256,1024]{1,0:T(8,128)}, f32[256,1024]{1,0:T(8,128)}, u32[]{:S(2)}, u32[]{:S(2)}) collective-permute-start(f32[256,1024]{1,0:T(8,128)} %dynamic-slice_bitcast_fusion), channel_id=1, source_target_pairs={{0,8},{8,0},{1,9},{9,1},{2,10},{10,2},{3,11},{11,3},{4,12},{12,4},... | collective-permute-start | bytes 3145736 | tf_op jit(solution)/shard_map/ppermute | solution.py:25
  49.6 2.6 %collective-permute-done = f32[256,1024]{1,0:T(8,128)} collective-permute-done((f32[256,1024]{1,0:T(8,128)}, f32[256,1024]{1,0:T(8,128)}, u32[]{:S(2)}, u32[]{:S(2)}) %collective-permute-start) | collective-permute-done | bytes 1048608 | tf_op jit(solution)/shard_map/ppermute | solution.py:25
  52.2 2.8 %bitcast_add_fusion = f32[256,1024]{1,0:T(8,128)} fusion(f32[256,1024]{1,0:T(8,128)} %collective-permute-done, f32[256,2,1024]{2,0,1:T(8,128)} %copy-done.2, s32[]{:T(128)S(6)} %select_n.40), kind=kLoop, calls=%fused_computation.17 | loop fusion | flops 262144 | bytes 3145732 | tf_op jit(solution)/shard_map/add | solution.py:25
  55.0 2.5 copy.71
  57.5 2.5 copy.72
  60.1 19.1 %all_to_all.30 = f32[4,256,256]{2,1,0:T(8,128)} all-to-all(f32[4,256,256]{2,1,0:T(8,128)} %copy.72), channel_id=1, replica_groups=mesh['x'=4,'z'=12,'c'=2,'mdl'=8] {'x'}, dimensions={0} | all-to-all | bytes 2097152 | tf_op jit(solution)/shard_map/all_to_all | solution.py:11
  79.2 1.3 reduce_sum.27
  80.6 28.5 %all_to_all.31 = f32[12,22,256]{2,1,0:T(8,128)S(1)} all-to-all(f32[12,22,256]{2,1,0:T(8,128)S(1)} %reshape.68), channel_id=1, replica_groups=mesh['x'=4,'z'=12,'c'=2,'mdl'=8] {'z'}, dimensions={0} | all-to-all | bytes 540672 | tf_op jit(solution)/shard_map/all_to_all | solution.py:11
  109.2 20.2 %all_to_all.32 = f32[12,22,256]{2,1,0:T(8,128)S(1)} all-to-all(f32[12,22,256]{2,1,0:T(8,128)S(1)} %broadcast_in_dim.33), channel_id=1, replica_groups=mesh['x'=4,'z'=12,'c'=2,'mdl'=8] {'z'}, dimensions={0} | all-to-all | bytes 540672 | tf_op jit(solution)/shard_map/all_to_all | solution.py:16
  129.7 14.5 %all_to_all.33 = f32[4,256,256]{1,2,0:T(8,128)} all-to-all(f32[4,256,256]{1,2,0:T(8,128)S(1)} %broadcast_in_dim.36), channel_id=1, replica_groups=mesh['x'=4,'z'=12,'c'=2,'mdl'=8] {'x'}, dimensions={0} | all-to-all | bytes 2097152 | tf_op jit(solution)/shard_map/all_to_all | solution.py:16
  144.2 6.5 %collective-permute-start.1 = (f32[256,1024]{0,1:T(8,128)}, f32[256,1024]{0,1:T(8,128)}, u32[]{:S(2)}, u32[]{:S(2)}) collective-permute-start(f32[256,1024]{0,1:T(8,128)} %bitcast.11), channel_id=1, source_target_pairs={{0,8},{8,0},{1,9},{9,1},{2,10},{10,2},{3,11},{11,3},{4,12},{12,4},... | collective-permute-start | bytes 3145736 | tf_op jit(solution)/shard_map/ppermute | solution.py:30
  150.8 2.6 %collective-permute-done.1 = f32[256,1024]{0,1:T(8,128)} collective-permute-done((f32[256,1024]{0,1:T(8,128)}, f32[256,1024]{0,1:T(8,128)}, u32[]{:S(2)}, u32[]{:S(2)}) %collective-permute-start.1) | collective-permute-done | bytes 1048608 | tf_op jit(solution)/shard_map/ppermute | solution.py:30
  153.4 2.6 %maximum_select_fusion = f32[256,8,256]{0,2,1:T(8,128)S(1)} fusion(f32[256,4,256]{0,2,1:T(8,128)} %bitcast.12, f32[256,4,256]{0,2,1:T(8,128)} %bitcast.10, pred[]{:T(512)S(6)} %eq.15), kind=kLoop, calls=%fused_computation.7 | loop fusion | flops 1572864 | bytes 4194305 | tf_op jit(solution)/shard_map/jit(_where)/select_n | solution.py:31
  156.0 1.3 copy-done.1
  157.5 11.7 %cholesky.44 = f32[128,128]{1,0:T(8,128)S(1)} custom-call(f32[128,128]{1,0:T(8,128)S(1)} %fusion.33), custom_call_target="Cholesky" | custom-call | tf_op jit(solution)/shard_map/jit(cholesky)/cholesky | solution.py:69
  169.2 0.6 compare_reduce_fusion.1
  169.9 0.7 fusion.24
  170.5 9.8 %custom-call.8 = f32[1,128,128]{1,2,0:T(8,128)S(1)} custom-call(f32[1,128,128]{2,1,0:T(8,128)S(1)} %fusion.24), custom_call_target="InvertDiagBlocksLowerTriangular" | custom-call | tf_op jit(solution)/shard_map/triangular_solve/custom-call.0 | solution.py:70
  180.3 0.3 fusion.31
  180.6 0.3 fusion.26
  180.9 0.3 slice_subtract_fusion
  181.4 1.4 gather_fusion
  183.0 11.7 %cholesky.55 = f32[128,128]{1,0:T(8,128)S(1)} custom-call(f32[128,128]{1,0:T(8,128)S(1)} %fusion.30), custom_call_target="Cholesky" | custom-call | tf_op jit(solution)/shard_map/jit(cholesky)/cholesky | solution.py:73
  194.7 0.6 compare_reduce_fusion
  195.4 0.7 fusion.25
  196.0 9.8 %custom-call.9 = f32[1,128,128]{1,2,0:T(8,128)S(1)} custom-call(f32[1,128,128]{2,1,0:T(8,128)S(1)} %fusion.25), custom_call_target="InvertDiagBlocksLowerTriangular" | custom-call | tf_op jit(solution)/shard_map/triangular_solve/custom-call.0 | solution.py:74
  205.8 0.2 bitcast_add_fusion.1
  206.0 0.3 convolution_negate_fusion
  206.4 1.1 broadcast_in_dim.60
  207.4 4.5 %all-to-all-start.5 = ((f32[8,257,128]{2,1,0:T(8,128)}), f32[8,257,128]{2,1,0:T(8,128)}, u32[]{:S(2)}, u32[]{:S(2)}) async-start(f32[8,257,128]{2,1,0:T(8,128)} %broadcast_in_dim.60), calls=%async_computation.5 | async-start | bytes 2162688 | tf_op jit(solution)/shard_map/all_to_all | solution.py:16
  212.2 4.9 %fusion.14 = f32[256,8,256]{2,0,1:T(8,128)} fusion(f32[256,8,256]{0,2,1:T(8,128)} %copy-done.1, f32[128,128]{1,0:T(8,128)S(1)} %fusion.31, f32[128,128]{1,0:T(8,128)S(1)} %copy.80, f32[128,128]{1,0:T(8,128)S(1)} %convolution_negate_fusion), kind=kOutput, calls=%fused_computation.23 | convolution fusion | flops 1610874880 | bytes 4390912 | tf_op jit(solution)/shard_map/ab,bjc->ajc/dot_general | solution.py:95
  217.1 22.7 %all-to-all-done.5 = f32[8,257,128]{2,1,0:T(8,128)} async-done(((f32[8,257,128]{2,1,0:T(8,128)}), f32[8,257,128]{2,1,0:T(8,128)}, u32[]{:S(2)}, u32[]{:S(2)}) %all-to-all-start.5) | async-done | bytes 1052704 | tf_op jit(solution)/shard_map/all_to_all | solution.py:16
  239.8 2.3 fusion.45
  242.0 1.2 copy.87
  243.3 0.8 slice.41
  244.0 1.1 select_bitcast_fusion
  245.1 1.2 copy.89
  246.4 5.3 %fusion.7 = (f32[8]{0:T(128)S(1)}, f32[8,256,256]{2,1,0:T(8,128)}) fusion(f32[256,8,256]{2,0,1:T(8,128)} %fusion.14, f32[8,128,128]{2,1,0:T(8,128)S(1)} %copy.89, f32[8,128,128]{2,1,0:T(8,128)} %get-tuple-element.18, f32[8,128,128]{2,1,0:T(8,128)} %get-tuple-element.16), kind=kOutput, calls=%fused_computation.12 | convolution fusion | flops 1613758464 | bytes 5767200 | tf_op jit(solution)/shard_map/ajc,jdc->ajd/dot_general | solution.py:96
  251.7 0.5 multiply_bitcast_fusion
  252.2 2.9 %copy.82 = f32[256,2048]{1,0:T(8,128)} copy(f32[256,2048]{0,1:T(8,128)} %bitcast.81) | data formatting | bytes 4194304
  (28 shorter events, 1.3 us)
Async XLA Ops:
  0.6 1.7 copy-start
  6.1 31.9 %all-to-all-start = ((bf16[8,256,256]{1,2,0:T(8,128)(2,1)}), bf16[8,256,256]{1,2,0:T(8,128)(2,1)}, u32[]{:S(2)}, u32[]{:S(2)}) async-start(bf16[8,256,256]{1,2,0:T(8,128)(2,1)} %broadcast_in_dim.32), calls=%async_computation | async-start | bytes 2097152 | tf_op jit(solution)/shard_map/all_to_all | solution.py:16
  39.7 1.3 copy-start.2
  42.1 10.1 %collective-permute-start = (f32[256,1024]{1,0:T(8,128)}, f32[256,1024]{1,0:T(8,128)}, u32[]{:S(2)}, u32[]{:S(2)}) collective-permute-start(f32[256,1024]{1,0:T(8,128)} %dynamic-slice_bitcast_fusion), channel_id=1, source_target_pairs={{0,8},{8,0},{1,9},{9,1},{2,10},{10,2},{3,11},{11,3},{4,12},{12,4},... | collective-permute-start | bytes 3145736 | tf_op jit(solution)/shard_map/ppermute | solution.py:25
  144.2 9.2 %collective-permute-start.1 = (f32[256,1024]{0,1:T(8,128)}, f32[256,1024]{0,1:T(8,128)}, u32[]{:S(2)}, u32[]{:S(2)}) collective-permute-start(f32[256,1024]{0,1:T(8,128)} %bitcast.11), channel_id=1, source_target_pairs={{0,8},{8,0},{1,9},{9,1},{2,10},{10,2},{3,11},{11,3},{4,12},{12,4},... | collective-permute-start | bytes 3145736 | tf_op jit(solution)/shard_map/ppermute | solution.py:30
  156.0 1.3 copy-start.1
  207.4 32.3 %all-to-all-start.5 = ((f32[8,257,128]{2,1,0:T(8,128)}), f32[8,257,128]{2,1,0:T(8,128)}, u32[]{:S(2)}, u32[]{:S(2)}) async-start(f32[8,257,128]{2,1,0:T(8,128)} %broadcast_in_dim.60), calls=%async_computation.5 | async-start | bytes 2162688 | tf_op jit(solution)/shard_map/all_to_all | solution.py:16

commit v6 on v5

--- a/solution.py
+++ b/solution.py
@@ -17,32 +17,32 @@
 
 
 def swap_halves_sum(row, axis):
-    cols = row.shape[1]
     side = lax.axis_index(axis)
-    halves = row.reshape(row.shape[0], 2, cols // 2)
-    mine = lax.dynamic_index_in_dim(halves, side, 1, keepdims=False)
-    theirs = lax.dynamic_index_in_dim(halves, 1 - side, 1, keepdims=False)
+    halves = row.reshape(2, row.shape[0] // 2, row.shape[1])
+    mine = lax.dynamic_index_in_dim(halves, side, 0, keepdims=False)
+    theirs = lax.dynamic_index_in_dim(halves, 1 - side, 0, keepdims=False)
     return mine + lax.ppermute(theirs, axis, [(0, 1), (1, 0)])
 
 
 def swap_halves_join(half, axis):
     side = lax.axis_index(axis)
     other = lax.ppermute(half, axis, [(0, 1), (1, 0)])
-    return jnp.where(side == 0, jnp.concatenate([half, other], 1), jnp.concatenate([other, half], 1))
+    return jnp.where(side == 0, jnp.concatenate([half, other], 0), jnp.concatenate([other, half], 0))
 
 
-def sum_over_tokens(row, pair, ring, outer):
-    rows = row.shape[0]
+def sum_over_tokens(row, pair, ring, outer, lanes=128):
+    cols = row.shape[1]
     n_ring = lax.axis_size(ring)
     n_out = lax.axis_size(outer)
     part = swap_halves_sum(row, pair)
-    width = part.shape[1] // n_ring
-    part = scatter_sum(part.reshape(rows, n_ring, width).transpose(1, 0, 2), ring)
-    pad = (-rows) % n_out
-    padded = jnp.pad(part, ((0, pad), (0, 0))).reshape(n_out, (rows + pad) // n_out, width)
+    rows = part.shape[0] // n_ring
+    part = scatter_sum(part.reshape(n_ring, rows, cols), ring)
+    flat = part.reshape(rows * cols // lanes, lanes)
+    pad = (-flat.shape[0]) % n_out
+    padded = jnp.pad(flat, ((0, pad), (0, 0))).reshape(n_out, -1, lanes)
     piece = scatter_sum(padded, outer)
-    part = gather_all(piece, outer, n_out).reshape(rows + pad, width)[:rows]
-    part = gather_all(part, ring, n_ring).transpose(1, 0, 2).reshape(rows, n_ring * width)
+    flat = gather_all(piece, outer, n_out).reshape(-1, lanes)[: flat.shape[0]]
+    part = gather_all(flat.reshape(rows, cols), ring, n_ring).reshape(n_ring * rows, cols)
     return swap_halves_join(part, pair)
 
 
@@ -92,8 +92,8 @@
     gram_total = lax.dynamic_index_in_dim(row_tiles, me, 1, keepdims=False)
     inverse = factor_inverse(gram_total)
     inverses = unpack_lower(gather_all(pack_lower(inverse), "mdl", models))
-    left_done = jnp.einsum("ab,bjc->ajc", inverse, row_tiles, precision=HIGH)
-    right_done = jnp.einsum("ajc,jdc->ajd", left_done, inverses, precision=HIGH)
+    left_done = jnp.einsum("ab,bjc->ajc", inverse, row_tiles, precision=lax.Precision.HIGH)
+    right_done = jnp.einsum("ajc,jdc->ajd", left_done, inverses, precision=lax.Precision.HIGH)
     cross_gram = right_done.reshape(basis_width, models * basis_width)
     similarity = jnp.sum(right_done * right_done, axis=(0, 2)) / basis_width
     return (cross_gram, similarity[None, :])

time: 258 us -> 254 us (0.984)
  other arithmetic: 54.2 us -> 50.7 us
  local copies, waits for them, and re-layouts: 23.3 us -> 26.8 us
  blocking collectives: 82.4 us -> 79 us
    unnamed x9 -> x11, local copies, waits for them, and re-layouts: 9.72 us -> 12.8 us
  transfers between devices with their start and end apart: 4 -> 4, of which waited for: 4 -> 4; matrix products, arithmetic and copies ran while one was open for 2% -> 3% of each run, Pallas kernels for 0% -> 0%
where the time goes in v6:
time: 254 us; the launch traced here: 250 us
  blocking collectives  79 us (31%)
  other arithmetic  50.7 us (20%)
  waiting for transfers between devices  50.5 us (20%)
  local copies, waits for them, and re-layouts  26.8 us (11%)
  starting transfers between devices  26.8 us (11%)
  matrix products  14.9 us (6%)
    all_to_all x2, waiting for transfers between devices, gather_all(): return lax.all_to_all(copies, axes, 0, 0, tiled=True)  47 us
    all_to_all x2, blocking collectives, scatter_sum(): return lax.all_to_all(chunks, axes, 0, 0, tiled=True).sum(axis=0)  46.7 us
    all_to_all x2, blocking collectives, gather_all(): return lax.all_to_all(copies, axes, 0, 0, tiled=True)  32.3 us
    unnamed x11, local copies, waits for them, and re-layouts  12.8 us
    another operation x3, other arithmetic, factor_inverse(): top = jnp.linalg.cholesky(gram[:h, :h])  12.4 us
    another operation x3, other arithmetic, factor_inverse(): low = jnp.linalg.cholesky(rest)  12.4 us
    all_to_all x2, starting transfers between devices, gather_all(): return lax.all_to_all(copies, axes, 0, 0, tiled=True)  11.9 us
    another operation x2, other arithmetic, factor_inverse(): top_inv = lax.linalg.triangular_solve(top, eye, left_side=True, lower=True)  10.5 us
  transfers between devices with their start and end apart: 4, of which 4 were waited for; matrix products, arithmetic and copies ran while one was open for 3% of the time, Pallas kernels for 0%

profile of v6, /device:TPU:1, one launch (start us, length us, event | category | flops | bytes accessed | tf_op | source)
XLA Modules:
  0.0 249.6 jit_solution(9766758459884368367)
XLA Ops:
  0.6 1.7 copy-done
  2.4 2.9 %fusion.10 = bf16[256,256]{0,1:T(8,128)(2,1)S(1)} fusion(bf16[5120,256]{1,0:T(8,128)(2,1)S(1)} %copy-done, bf16[1,256,5120]{2,1,0:T(8,128)(2,1)} %param.5), kind=kOutput, calls=%fused_computation.15 | convolution fusion | flops 671154176 | bytes 5373952 | tf_op jit(solution)/shard_map/dot_general | solution.py:83
  5.4 1.0 broadcast_in_dim.56
  6.4 7.7 %all-to-all-start = ((bf16[8,256,256]{2,1,0:T(8,128)(2,1)}), bf16[8,256,256]{2,1,0:T(8,128)(2,1)}, u32[]{:S(2)}, u32[]{:S(2)}) async-start(bf16[8,256,256]{2,1,0:T(8,128)(2,1)} %broadcast_in_dim.56), calls=%async_computation | async-start | bytes 2097152 | tf_op jit(solution)/shard_map/all_to_all | solution.py:16
  14.0 24.2 %all-to-all-done = bf16[8,256,256]{2,1,0:T(8,128)(2,1)} async-done(((bf16[8,256,256]{2,1,0:T(8,128)(2,1)}), bf16[8,256,256]{2,1,0:T(8,128)(2,1)}, u32[]{:S(2)}, u32[]{:S(2)}) %all-to-all-start) | async-done | bytes 1048608 | tf_op jit(solution)/shard_map/all_to_all | solution.py:16
  38.3 2.8 %copy.40 = bf16[256,8,256]{2,1,0:T(8,128)(2,1)} copy(bf16[256,8,256]{2,0,1:T(8,128)(2,1)} %bitcast.3) | data formatting | bytes 2097152 | tf_op jit(solution)/shard_map/transpose | solution.py:88
  41.1 2.3 reshape.88
  43.4 1.7 fusion.45
  45.1 1.3 copy-done.2
  46.4 1.1 dynamic-slice_bitcast_fusion
  47.5 7.5 %collective-permute-start = (f32[128,2048]{1,0:T(8,128)}, f32[128,2048]{1,0:T(8,128)}, u32[]{:S(2)}, u32[]{:S(2)}) collective-permute-start(f32[128,2048]{1,0:T(8,128)} %dynamic-slice_bitcast_fusion), channel_id=1, source_target_pairs={{0,8},{8,0},{1,9},{9,1},{2,10},{10,2},{3,11},{11,3},{4,12},{12,4},... | collective-permute-start | bytes 3145736 | tf_op jit(solution)/shard_map/ppermute | solution.py:24
  55.0 2.6 %collective-permute-done = f32[128,2048]{1,0:T(8,128)} collective-permute-done((f32[128,2048]{1,0:T(8,128)}, f32[128,2048]{1,0:T(8,128)}, u32[]{:S(2)}, u32[]{:S(2)}) %collective-permute-start) | collective-permute-done | bytes 1048608 | tf_op jit(solution)/shard_map/ppermute | solution.py:24
  57.6 1.7 bitcast_add_fusion
  59.3 18.1 %all_to_all.30 = f32[4,32,2048]{2,1,0:T(8,128)} all-to-all(f32[4,32,2048]{2,1,0:T(8,128)S(1)} %bitcast.75), channel_id=1, replica_groups=mesh['x'=4,'z'=12,'c'=2,'mdl'=8] {'x'}, dimensions={0} | all-to-all | bytes 2097152 | tf_op jit(solution)/shard_map/all_to_all | solution.py:11
  77.4 1.3 reduce_sum.27
  78.8 28.6 %all_to_all.31 = f32[12,43,128]{2,1,0:T(8,128)S(1)} all-to-all(f32[12,43,128]{2,1,0:T(8,128)S(1)} %reshape.72), channel_id=1, replica_groups=mesh['x'=4,'z'=12,'c'=2,'mdl'=8] {'z'}, dimensions={0} | all-to-all | bytes 528384 | tf_op jit(solution)/shard_map/all_to_all | solution.py:11
  107.4 17.6 %all_to_all.32 = f32[12,43,128]{2,1,0:T(8,128)S(1)} all-to-all(f32[12,43,128]{2,1,0:T(8,128)S(1)} %broadcast_in_dim.57), channel_id=1, replica_groups=mesh['x'=4,'z'=12,'c'=2,'mdl'=8] {'z'}, dimensions={0} | all-to-all | bytes 528384 | tf_op jit(solution)/shard_map/all_to_all | solution.py:16
  125.3 14.7 %all_to_all.33 = f32[4,32,2048]{2,1,0:T(8,128)} all-to-all(f32[4,32,2048]{2,1,0:T(8,128)S(1)} %broadcast_in_dim.59), channel_id=1, replica_groups=mesh['x'=4,'z'=12,'c'=2,'mdl'=8] {'x'}, dimensions={0} | all-to-all | bytes 2097152 | tf_op jit(solution)/shard_map/all_to_all | solution.py:16
  139.9 7.4 %collective-permute-start.1 = (f32[128,2048]{1,0:T(8,128)}, f32[128,2048]{1,0:T(8,128)}, u32[]{:S(2)}, u32[]{:S(2)}) collective-permute-start(f32[128,2048]{1,0:T(8,128)} %bitcast.7), channel_id=1, source_target_pairs={{0,8},{8,0},{1,9},{9,1},{2,10},{10,2},{3,11},{11,3},{4,12},{12,4},... | collective-permute-start | bytes 3145736 | tf_op jit(solution)/shard_map/ppermute | solution.py:29
  147.4 1.6 copy.55
  148.9 0.8 collective-permute-done.1
  149.7 1.6 copy.56
  151.6 1.3 copy-done.1
  153.4 11.7 %cholesky.44 = f32[128,128]{1,0:T(8,128)S(1)} custom-call(f32[128,128]{1,0:T(8,128)S(1)} %fusion.32), custom_call_target="Cholesky" | custom-call | tf_op jit(solution)/shard_map/jit(cholesky)/cholesky | solution.py:69
  165.1 0.6 compare_reduce_fusion.1
  165.7 0.7 fusion.23
  166.4 9.8 %custom-call.8 = f32[1,128,128]{1,2,0:T(8,128)S(1)} custom-call(f32[1,128,128]{2,1,0:T(8,128)S(1)} %fusion.23), custom_call_target="InvertDiagBlocksLowerTriangular" | custom-call | tf_op jit(solution)/shard_map/triangular_solve/custom-call.0 | solution.py:70
  176.2 0.3 fusion.30
  176.5 0.3 fusion.25
  176.8 0.3 convolution_subtract_fusion
  177.3 1.5 gather_fusion
  178.9 11.7 %cholesky.55 = f32[128,128]{1,0:T(8,128)S(1)} custom-call(f32[128,128]{1,0:T(8,128)S(1)} %fusion.29), custom_call_target="Cholesky" | custom-call | tf_op jit(solution)/shard_map/jit(cholesky)/cholesky | solution.py:73
  190.6 0.6 compare_reduce_fusion
  191.3 0.7 fusion.24
  191.9 9.8 %custom-call.9 = f32[1,128,128]{1,2,0:T(8,128)S(1)} custom-call(f32[1,128,128]{2,1,0:T(8,128)S(1)} %fusion.24), custom_call_target="InvertDiagBlocksLowerTriangular" | custom-call | tf_op jit(solution)/shard_map/triangular_solve/custom-call.0 | solution.py:74
  202.0 0.3 convolution_negate_fusion
  202.3 1.1 broadcast_in_dim.62
  203.3 4.3 %all-to-all-start.5 = ((f32[8,257,128]{2,1,0:T(8,128)}), f32[8,257,128]{2,1,0:T(8,128)}, u32[]{:S(2)}, u32[]{:S(2)}) async-start(f32[8,257,128]{2,1,0:T(8,128)} %broadcast_in_dim.62), calls=%async_computation.5 | async-start | bytes 2162688 | tf_op jit(solution)/shard_map/all_to_all | solution.py:16
  207.9 4.5 %fusion.8 = f32[256,8,256]{2,0,1:T(8,128)} fusion(f32[256,8,256]{2,1,0:T(8,128)} %copy-done.1, f32[128,128]{1,0:T(8,128)S(1)} %fusion.30, f32[128,128]{1,0:T(8,128)S(1)} %copy.48, f32[128,128]{1,0:T(8,128)S(1)} %convolution_negate_fusion), kind=kOutput, calls=%fused_computation.13 | convolution fusion | flops 805568512 | bytes 4390912 | tf_op jit(solution)/shard_map/ab,bjc->ajc/dot_general | solution.py:95
  212.5 22.8 %all-to-all-done.5 = f32[8,257,128]{2,1,0:T(8,128)} async-done(((f32[8,257,128]{2,1,0:T(8,128)}), f32[8,257,128]{2,1,0:T(8,128)}, u32[]{:S(2)}, u32[]{:S(2)}) %all-to-all-start.5) | async-done | bytes 1052704 | tf_op jit(solution)/shard_map/all_to_all | solution.py:16
  235.2 2.3 fusion.44
  237.5 1.2 copy.52
  238.8 0.8 slice.41
  239.5 1.1 select_bitcast_fusion
  240.6 1.2 copy.54
  241.8 4.3 %fusion.7 = (f32[8]{0:T(128)S(1)}, f32[8,256,256]{2,1,0:T(8,128)}) fusion(f32[256,8,256]{2,0,1:T(8,128)} %fusion.8, f32[8,128,128]{2,1,0:T(8,128)S(1)} %copy.54, f32[8,128,128]{2,1,0:T(8,128)} %get-tuple-element.14, f32[8,128,128]{2,1,0:T(8,128)} %get-tuple-element.12), kind=kOutput, calls=%fused_computation.12 | convolution fusion | flops 808452096 | bytes 5767200 | tf_op jit(solution)/shard_map/ajc,jdc->ajd/dot_general | solution.py:96
  246.2 0.5 multiply_bitcast_fusion
  246.7 2.9 %copy.50 = f32[256,2048]{1,0:T(8,128)} copy(f32[256,2048]{0,1:T(8,128)} %bitcast.76) | data formatting | bytes 4194304
  (32 shorter events, 2.0 us)
Async XLA Ops:
  0.6 1.7 copy-start
  6.4 31.9 %all-to-all-start = ((bf16[8,256,256]{2,1,0:T(8,128)(2,1)}), bf16[8,256,256]{2,1,0:T(8,128)(2,1)}, u32[]{:S(2)}, u32[]{:S(2)}) async-start(bf16[8,256,256]{2,1,0:T(8,128)(2,1)} %broadcast_in_dim.56), calls=%async_computation | async-start | bytes 2097152 | tf_op jit(solution)/shard_map/all_to_all | solution.py:16
  45.1 1.3 copy-start.2
  47.5 10.1 %collective-permute-start = (f32[128,2048]{1,0:T(8,128)}, f32[128,2048]{1,0:T(8,128)}, u32[]{:S(2)}, u32[]{:S(2)}) collective-permute-start(f32[128,2048]{1,0:T(8,128)} %dynamic-slice_bitcast_fusion), channel_id=1, source_target_pairs={{0,8},{8,0},{1,9},{9,1},{2,10},{10,2},{3,11},{11,3},{4,12},{12,4},... | collective-permute-start | bytes 3145736 | tf_op jit(solution)/shard_map/ppermute | solution.py:24
  139.9 9.8 %collective-permute-start.1 = (f32[128,2048]{1,0:T(8,128)}, f32[128,2048]{1,0:T(8,128)}, u32[]{:S(2)}, u32[]{:S(2)}) collective-permute-start(f32[128,2048]{1,0:T(8,128)} %bitcast.7), channel_id=1, source_target_pairs={{0,8},{8,0},{1,9},{9,1},{2,10},{10,2},{3,11},{11,3},{4,12},{12,4},... | collective-permute-start | bytes 3145736 | tf_op jit(solution)/shard_map/ppermute | solution.py:29
  151.6 1.3 copy-start.1
  203.3 31.9 %all-to-all-start.5 = ((f32[8,257,128]{2,1,0:T(8,128)}), f32[8,257,128]{2,1,0:T(8,128)}, u32[]{:S(2)}, u32[]{:S(2)}) async-start(f32[8,257,128]{2,1,0:T(8,128)} %broadcast_in_dim.62), calls=%async_computation.5 | async-start | bytes 2162688 | tf_op jit(solution)/shard_map/all_to_all | solution.py:16

commit v7 on v6

--- a/solution.py
+++ b/solution.py
@@ -16,9 +16,9 @@
     return lax.all_to_all(copies, axes, 0, 0, tiled=True)
 
 
-def swap_halves_sum(row, axis):
+def swap_halves_sum(tiles, axis):
     side = lax.axis_index(axis)
-    halves = row.reshape(2, row.shape[0] // 2, row.shape[1])
+    halves = tiles.reshape((2, tiles.shape[0] // 2) + tiles.shape[1:])
     mine = lax.dynamic_index_in_dim(halves, side, 0, keepdims=False)
     theirs = lax.dynamic_index_in_dim(halves, 1 - side, 0, keepdims=False)
     return mine + lax.ppermute(theirs, axis, [(0, 1), (1, 0)])
@@ -30,19 +30,18 @@
     return jnp.where(side == 0, jnp.concatenate([half, other], 0), jnp.concatenate([other, half], 0))
 
 
-def sum_over_tokens(row, pair, ring, outer, lanes=128):
-    cols = row.shape[1]
+def sum_over_tokens(tiles, pair, ring, outer, lanes=128):
     n_ring = lax.axis_size(ring)
     n_out = lax.axis_size(outer)
-    part = swap_halves_sum(row, pair)
-    rows = part.shape[0] // n_ring
-    part = scatter_sum(part.reshape(n_ring, rows, cols), ring)
-    flat = part.reshape(rows * cols // lanes, lanes)
+    part = swap_halves_sum(tiles, pair)
+    each = part.shape[0] // n_ring
+    part = scatter_sum(part.reshape((n_ring, each) + part.shape[1:]), ring)
+    flat = part.reshape(-1, lanes)
     pad = (-flat.shape[0]) % n_out
     padded = jnp.pad(flat, ((0, pad), (0, 0))).reshape(n_out, -1, lanes)
     piece = scatter_sum(padded, outer)
     flat = gather_all(piece, outer, n_out).reshape(-1, lanes)[: flat.shape[0]]
-    part = gather_all(flat.reshape(rows, cols), ring, n_ring).reshape(n_ring * rows, cols)
+    part = gather_all(flat.reshape(part.shape), ring, n_ring).reshape((n_ring * each,) + part.shape[1:])
     return swap_halves_join(part, pair)
 
 
@@ -85,17 +84,15 @@
     models = lax.axis_size("mdl")
     me = lax.axis_index("mdl")
     everyone = gather_all(projected, "mdl", models)
-    everyone = everyone.transpose(1, 0, 2).reshape(projected.shape[0], models * basis_width)
-    local_row = jnp.dot(projected.T, everyone, preferred_element_type=jnp.float32)
-    row_sums = sum_over_tokens(local_row, "c", "x", "z")
-    row_tiles = row_sums.reshape(basis_width, models, basis_width)
-    gram_total = lax.dynamic_index_in_dim(row_tiles, me, 1, keepdims=False)
+    local_tiles = jnp.einsum("ta,jtc->jac", projected, everyone, preferred_element_type=jnp.float32)
+    tiles = sum_over_tokens(local_tiles, "c", "x", "z")
+    gram_total = lax.dynamic_index_in_dim(tiles, me, 0, keepdims=False)
     inverse = factor_inverse(gram_total)
     inverses = unpack_lower(gather_all(pack_lower(inverse), "mdl", models))
-    left_done = jnp.einsum("ab,bjc->ajc", inverse, row_tiles, precision=lax.Precision.HIGH)
-    right_done = jnp.einsum("ajc,jdc->ajd", left_done, inverses, precision=lax.Precision.HIGH)
-    cross_gram = right_done.reshape(basis_width, models * basis_width)
-    similarity = jnp.sum(right_done * right_done, axis=(0, 2)) / basis_width
+    left_done = jnp.einsum("ab,jbc->jac", inverse, tiles, precision=lax.Precision.HIGH)
+    right_done = jnp.einsum("jac,jdc->jad", left_done, inverses, precision=lax.Precision.HIGH)
+    cross_gram = right_done.transpose(1, 0, 2).reshape(basis_width, models * basis_width)
+    similarity = jnp.sum(right_done * right_done, axis=(1, 2)) / basis_width
     return (cross_gram, similarity[None, :])
 
 

time: 254 us -> 248 us (0.976)
  local copies, waits for them, and re-layouts: 26.8 us -> 18.4 us
    unnamed x11 -> x9, local copies, waits for them, and re-layouts: 12.8 us -> 9.72 us
    transpose x1 -> x0, local copies, waits for them, and re-layouts: 2.78 us -> none  [on_device(): everyone.transpose(1, 0, 2)]
  transfers between devices with their start and end apart: 4 -> 4, of which waited for: 4 -> 4; matrix products, arithmetic and copies ran while one was open for 3% -> 2% of each run, Pallas kernels for 0% -> 0%
where the time goes in v7:
time: 248 us; the launch traced here: 243 us
  blocking collectives  78.9 us (32%)
  waiting for transfers between devices  52.8 us (21%)
  other arithmetic  51.8 us (21%)
  starting transfers between devices  26.6 us (11%)
  local copies, waits for them, and re-layouts  18.4 us (7%)
  matrix products  14 us (6%)
    all_to_all x2, waiting for transfers between devices, gather_all(): return lax.all_to_all(copies, axes, 0, 0, tiled=True)  47.6 us
    all_to_all x2, blocking collectives, scatter_sum(): return lax.all_to_all(chunks, axes, 0, 0, tiled=True).sum(axis=0)  46.6 us
    all_to_all x2, blocking collectives, gather_all(): return lax.all_to_all(copies, axes, 0, 0, tiled=True)  32.3 us
    another operation x3, other arithmetic, factor_inverse(): top = jnp.linalg.cholesky(gram[:h, :h])  12.4 us
    another operation x3, other arithmetic, factor_inverse(): low = jnp.linalg.cholesky(rest)  12.4 us
    all_to_all x2, starting transfers between devices, gather_all(): return lax.all_to_all(copies, axes, 0, 0, tiled=True)  11.9 us
    another operation x2, other arithmetic, factor_inverse(): top_inv = lax.linalg.triangular_solve(top, eye, left_side=True, lower=True)  10.5 us
    another operation x2, other arithmetic, factor_inverse(): low_inv = lax.linalg.triangular_solve(low, eye, left_side=True, lower=True)  10.5 us
  transfers between devices with their start and end apart: 4, of which 4 were waited for; matrix products, arithmetic and copies ran while one was open for 2% of the time, Pallas kernels for 0%

profile of v7, /device:TPU:1, one launch (start us, length us, event | category | flops | bytes accessed | tf_op | source)
XLA Modules:
  0.0 243.4 jit_solution(10723068715899961285)
XLA Ops:
  0.6 1.7 copy-done
  2.4 2.6 %fusion.7 = bf16[256,256]{1,0:T(8,128)(2,1)S(1)} fusion(bf16[5120,256]{1,0:T(8,128)(2,1)S(1)} %copy-done, bf16[1,256,5120]{2,1,0:T(8,128)(2,1)} %param.5), kind=kOutput, calls=%fused_computation.12 | convolution fusion | flops 671154176 | bytes 5373952 | tf_op jit(solution)/shard_map/dot_general | solution.py:82
  5.1 1.0 broadcast_in_dim.35
  6.1 7.7 %all-to-all-start = ((bf16[8,256,256]{1,2,0:T(8,128)(2,1)}), bf16[8,256,256]{1,2,0:T(8,128)(2,1)}, u32[]{:S(2)}, u32[]{:S(2)}) async-start(bf16[8,256,256]{1,2,0:T(8,128)(2,1)} %broadcast_in_dim.35), calls=%async_computation | async-start | bytes 2097152 | tf_op jit(solution)/shard_map/all_to_all | solution.py:16
  13.8 24.2 %all-to-all-done = bf16[8,256,256]{1,2,0:T(8,128)(2,1)} async-done(((bf16[8,256,256]{1,2,0:T(8,128)(2,1)}), bf16[8,256,256]{1,2,0:T(8,128)(2,1)}, u32[]{:S(2)}, u32[]{:S(2)}) %all-to-all-start) | async-done | bytes 1048608 | tf_op jit(solution)/shard_map/all_to_all | solution.py:16
  38.0 1.7 fusion.22
  39.7 1.3 copy-done.2
  41.0 1.1 dynamic-slice_bitcast_fusion
  42.1 7.5 %collective-permute-start = (f32[4,256,256]{1,2,0:T(8,128)}, f32[4,256,256]{1,2,0:T(8,128)}, u32[]{:S(2)}, u32[]{:S(2)}) collective-permute-start(f32[4,256,256]{1,2,0:T(8,128)} %dynamic-slice_bitcast_fusion), channel_id=1, source_target_pairs={{0,8},{8,0},{1,9},{9,1},{2,10},{10,2},{3,11},{11,3},{4,12},{12,4},... | collective-permute-start | bytes 3145736 | tf_op jit(solution)/shard_map/ppermute | solution.py:24
  49.6 2.6 %collective-permute-done = f32[4,256,256]{1,2,0:T(8,128)} collective-permute-done((f32[4,256,256]{1,2,0:T(8,128)}, f32[4,256,256]{1,2,0:T(8,128)}, u32[]{:S(2)}, u32[]{:S(2)}) %collective-permute-start) | collective-permute-done | bytes 1048608 | tf_op jit(solution)/shard_map/ppermute | solution.py:24
  52.2 1.7 fusion.12
  53.8 18.0 %all_to_all.30 = f32[4,1,256,256]{2,3,1,0:T(8,128)S(1)} all-to-all(f32[4,1,256,256]{2,3,1,0:T(8,128)S(1)} %fusion.12), channel_id=1, replica_groups=mesh['x'=4,'z'=12,'c'=2,'mdl'=8] {'x'}, dimensions={0} | all-to-all | bytes 2097152 | tf_op jit(solution)/shard_map/all_to_all | solution.py:11
  71.9 0.1 copy.39
  72.1 28.6 %all_to_all.31 = f32[12,43,128]{2,1,0:T(8,128)S(1)} all-to-all(f32[12,43,128]{2,1,0:T(8,128)S(1)} %reshape.67), channel_id=1, replica_groups=mesh['x'=4,'z'=12,'c'=2,'mdl'=8] {'z'}, dimensions={0} | all-to-all | bytes 528384 | tf_op jit(solution)/shard_map/all_to_all | solution.py:11
  100.8 17.6 %all_to_all.32 = f32[12,43,128]{2,1,0:T(8,128)S(1)} all-to-all(f32[12,43,128]{2,1,0:T(8,128)S(1)} %broadcast_in_dim.56), channel_id=1, replica_groups=mesh['x'=4,'z'=12,'c'=2,'mdl'=8] {'z'}, dimensions={0} | all-to-all | bytes 528384 | tf_op jit(solution)/shard_map/all_to_all | solution.py:16
  118.6 0.1 copy.40
  118.8 14.7 %all_to_all.33 = f32[4,1,256,256]{2,3,1,0:T(8,128)} all-to-all(f32[4,1,256,256]{2,3,1,0:T(8,128)S(1)} %broadcast_in_dim.58), channel_id=1, replica_groups=mesh['x'=4,'z'=12,'c'=2,'mdl'=8] {'x'}, dimensions={0} | all-to-all | bytes 2097152 | tf_op jit(solution)/shard_map/all_to_all | solution.py:16
  133.4 7.2 %collective-permute-start.1 = (f32[4,256,256]{1,2,0:T(8,128)}, f32[4,256,256]{1,2,0:T(8,128)}, u32[]{:S(2)}, u32[]{:S(2)}) collective-permute-start(f32[4,256,256]{1,2,0:T(8,128)} %bitcast.9), channel_id=1, source_target_pairs={{0,8},{8,0},{1,9},{9,1},{2,10},{10,2},{3,11},{11,3},{4,12},{12,4},... | collective-permute-start | bytes 3145736 | tf_op jit(solution)/shard_map/ppermute | solution.py:29
  140.7 2.6 %collective-permute-done.1 = f32[4,256,256]{1,2,0:T(8,128)} collective-permute-done((f32[4,256,256]{1,2,0:T(8,128)}, f32[4,256,256]{1,2,0:T(8,128)}, u32[]{:S(2)}, u32[]{:S(2)}) %collective-permute-start.1) | collective-permute-done | bytes 1048608 | tf_op jit(solution)/shard_map/ppermute | solution.py:29
  143.3 2.6 %maximum_select_fusion = f32[8,256,256]{1,2,0:T(8,128)S(1)} fusion(f32[4,256,256]{1,2,0:T(8,128)} %collective-permute-done.1, f32[4,256,256]{1,2,0:T(8,128)} %bitcast.9, pred[]{:T(512)S(6)} %eq.15), kind=kLoop, calls=%fused_computation.7 | loop fusion | flops 1572864 | bytes 4194305 | tf_op jit(solution)/shard_map/jit(_where)/select_n | solution.py:30
  145.9 1.3 copy-done.1
  147.4 11.7 %cholesky.44 = f32[128,128]{1,0:T(8,128)S(1)} custom-call(f32[128,128]{1,0:T(8,128)S(1)} %fusion.33), custom_call_target="Cholesky" | custom-call | tf_op jit(solution)/shard_map/jit(cholesky)/cholesky | solution.py:68
  159.1 0.6 compare_reduce_fusion.1
  159.8 0.7 fusion.24
  160.4 9.8 %custom-call.8 = f32[1,128,128]{1,2,0:T(8,128)S(1)} custom-call(f32[1,128,128]{2,1,0:T(8,128)S(1)} %fusion.24), custom_call_target="InvertDiagBlocksLowerTriangular" | custom-call | tf_op jit(solution)/shard_map/triangular_solve/custom-call.0 | solution.py:69
  170.2 0.3 fusion.31
  170.5 0.3 fusion.26
  170.8 0.3 slice_subtract_fusion
  171.1 0.2 fusion.44
  171.3 1.4 gather_fusion
  172.8 11.7 %cholesky.55 = f32[128,128]{1,0:T(8,128)S(1)} custom-call(f32[128,128]{1,0:T(8,128)S(1)} %fusion.30), custom_call_target="Cholesky" | custom-call | tf_op jit(solution)/shard_map/jit(cholesky)/cholesky | solution.py:72
  184.6 0.6 compare_reduce_fusion
  185.2 0.7 fusion.25
  185.9 9.8 %custom-call.9 = f32[1,128,128]{1,2,0:T(8,128)S(1)} custom-call(f32[1,128,128]{2,1,0:T(8,128)S(1)} %fusion.25), custom_call_target="InvertDiagBlocksLowerTriangular" | custom-call | tf_op jit(solution)/shard_map/triangular_solve/custom-call.0 | solution.py:73
  195.7 0.2 bitcast_add_fusion.1
  195.9 0.3 convolution_negate_fusion
  196.2 1.1 broadcast_in_dim.62
  197.3 4.3 %all-to-all-start.5 = ((f32[8,257,128]{2,1,0:T(8,128)}), f32[8,257,128]{2,1,0:T(8,128)}, u32[]{:S(2)}, u32[]{:S(2)}) async-start(f32[8,257,128]{2,1,0:T(8,128)} %broadcast_in_dim.62), calls=%async_computation.5 | async-start | bytes 2162688 | tf_op jit(solution)/shard_map/all_to_all | solution.py:16
  201.9 4.0 %fusion.14 = f32[8,256,256]{2,1,0:T(8,128)} fusion(f32[8,256,256]{1,2,0:T(8,128)} %copy-done.1, f32[128,128]{1,0:T(8,128)S(1)} %fusion.31, f32[128,128]{1,0:T(8,128)S(1)} %copy.44, f32[128,128]{1,0:T(8,128)S(1)} %convolution_negate_fusion), kind=kOutput, calls=%fused_computation.24 | convolution fusion | flops 805568512 | bytes 4390912 | tf_op jit(solution)/shard_map/ab,jbc->jac/dot_general | solution.py:92
  205.9 23.3 %all-to-all-done.5 = f32[8,257,128]{2,1,0:T(8,128)} async-done(((f32[8,257,128]{2,1,0:T(8,128)}), f32[8,257,128]{2,1,0:T(8,128)}, u32[]{:S(2)}, u32[]{:S(2)}) %all-to-all-start.5) | async-done | bytes 1052704 | tf_op jit(solution)/shard_map/all_to_all | solution.py:16
  229.2 2.3 fusion.43
  231.5 1.2 copy.51
  232.7 0.8 slice.41
  233.5 1.1 select_bitcast_fusion
  234.6 1.2 copy.53
  235.8 4.2 %multiply_reduce_fusion = (f32[8]{0:T(128)S(1)}, f32[8,256,256]{1,2,0:T(8,128)}) fusion(f32[8,256,256]{2,1,0:T(8,128)} %fusion.14, f32[8,128,128]{2,1,0:T(8,128)S(1)} %copy.53, f32[8,128,128]{2,1,0:T(8,128)} %get-tuple-element.14, f32[8,128,128]{2,1,0:T(8,128)} %get-tuple-element.12), kind=kOutput, calls=%fused_computation.11 | convolution fusion | flops 808452096 | bytes 5767200 | tf_op jit(solution)/shard_map/jac,jdc->jad/dot_general | solution.py:93
  240.0 0.5 multiply_bitcast_fusion
  240.5 2.9 %copy.49 = f32[256,2048]{1,0:T(8,128)} copy(f32[256,2048]{0,1:T(8,128)} %bitcast.75) | data formatting | bytes 4194304
  (29 shorter events, 1.1 us)
Async XLA Ops:
  0.6 1.7 copy-start
  6.1 31.9 %all-to-all-start = ((bf16[8,256,256]{1,2,0:T(8,128)(2,1)}), bf16[8,256,256]{1,2,0:T(8,128)(2,1)}, u32[]{:S(2)}, u32[]{:S(2)}) async-start(bf16[8,256,256]{1,2,0:T(8,128)(2,1)} %broadcast_in_dim.35), calls=%async_computation | async-start | bytes 2097152 | tf_op jit(solution)/shard_map/all_to_all | solution.py:16
  39.7 1.3 copy-start.2
  42.1 10.1 %collective-permute-start = (f32[4,256,256]{1,2,0:T(8,128)}, f32[4,256,256]{1,2,0:T(8,128)}, u32[]{:S(2)}, u32[]{:S(2)}) collective-permute-start(f32[4,256,256]{1,2,0:T(8,128)} %dynamic-slice_bitcast_fusion), channel_id=1, source_target_pairs={{0,8},{8,0},{1,9},{9,1},{2,10},{10,2},{3,11},{11,3},{4,12},{12,4},... | collective-permute-start | bytes 3145736 | tf_op jit(solution)/shard_map/ppermute | solution.py:24
  133.4 9.8 %collective-permute-start.1 = (f32[4,256,256]{1,2,0:T(8,128)}, f32[4,256,256]{1,2,0:T(8,128)}, u32[]{:S(2)}, u32[]{:S(2)}) collective-permute-start(f32[4,256,256]{1,2,0:T(8,128)} %bitcast.9), channel_id=1, source_target_pairs={{0,8},{8,0},{1,9},{9,1},{2,10},{10,2},{3,11},{11,3},{4,12},{12,4},... | collective-permute-start | bytes 3145736 | tf_op jit(solution)/shard_map/ppermute | solution.py:29
  145.9 1.3 copy-start.1
  197.3 31.9 %all-to-all-start.5 = ((f32[8,257,128]{2,1,0:T(8,128)}), f32[8,257,128]{2,1,0:T(8,128)}, u32[]{:S(2)}, u32[]{:S(2)}) async-start(f32[8,257,128]{2,1,0:T(8,128)} %broadcast_in_dim.62), calls=%async_computation.5 | async-start | bytes 2162688 | tf_op jit(solution)/shard_map/all_to_all | solution.py:16

commit v8 on v7

--- a/solution.py
+++ b/solution.py
@@ -88,9 +88,17 @@
     tiles = sum_over_tokens(local_tiles, "c", "x", "z")
     gram_total = lax.dynamic_index_in_dim(tiles, me, 0, keepdims=False)
     inverse = factor_inverse(gram_total)
-    inverses = unpack_lower(gather_all(pack_lower(inverse), "mdl", models))
+    packed = gather_all(pack_lower(inverse), "mdl", models)
+    half = packed.shape[-1]
+    low_left, folded, diag = packed[:, :half], packed[:, half:2 * half], packed[:, 2 * half]
+    top = jnp.tril(folded, -1) + diag[:, :, None] * jnp.eye(half, dtype=packed.dtype)
+    low_right_t = jnp.triu(folded)
     left_done = jnp.einsum("ab,jbc->jac", inverse, tiles, precision=lax.Precision.HIGH)
-    right_done = jnp.einsum("jac,jdc->jad", left_done, inverses, precision=lax.Precision.HIGH)
+    first, second = left_done[..., :half], left_done[..., half:]
+    out_first = jnp.einsum("jac,jdc->jad", first, top, precision=lax.Precision.HIGH)
+    out_second = jnp.einsum("jac,jdc->jad", first, low_left, precision=lax.Precision.HIGH) + jnp.einsum(
+        "jac,jcd->jad", second, low_right_t, precision=lax.Precision.HIGH)
+    right_done = jnp.concatenate([out_first, out_second], axis=-1)
     cross_gram = right_done.transpose(1, 0, 2).reshape(basis_width, models * basis_width)
     similarity = jnp.sum(right_done * right_done, axis=(1, 2)) / basis_width
     return (cross_gram, similarity[None, :])

time: 248 us -> 245 us (0.988)
  local copies, waits for them, and re-layouts: 18.4 us -> 13.7 us
    dot_general x1 -> x3, matrix products: 4.21 us -> 5.32 us  [the longest x1 1.93 us: on_device(): jnp.einsum('jac,jdc->jad', first, low_left, precision=lax.Precision.HIGH)]
where the time goes in v8:
time: 245 us; the launch traced here: 241 us
  blocking collectives  78.9 us (32%)
  waiting for transfers between devices  52.9 us (22%)
  other arithmetic  52.3 us (21%)
  starting transfers between devices  26.6 us (11%)
  matrix products  15.1 us (6%)
  local copies, waits for them, and re-layouts  13.7 us (6%)
    all_to_all x2, waiting for transfers between devices, gather_all(): return lax.all_to_all(copies, axes, 0, 0, tiled=True)  47.7 us
    all_to_all x2, blocking collectives, scatter_sum(): return lax.all_to_all(chunks, axes, 0, 0, tiled=True).sum(axis=0)  46.6 us
    all_to_all x2, blocking collectives, gather_all(): return lax.all_to_all(copies, axes, 0, 0, tiled=True)  32.3 us
    another operation x3, other arithmetic, factor_inverse(): top = jnp.linalg.cholesky(gram[:h, :h])  12.4 us
    another operation x3, other arithmetic, factor_inverse(): low = jnp.linalg.cholesky(rest)  12.4 us
    all_to_all x2, starting transfers between devices, gather_all(): return lax.all_to_all(copies, axes, 0, 0, tiled=True)  11.9 us
    another operation x2, other arithmetic, factor_inverse(): top_inv = lax.linalg.triangular_solve(top, eye, left_side=True, lower=True)  10.5 us
    another operation x2, other arithmetic, factor_inverse(): low_inv = lax.linalg.triangular_solve(low, eye, left_side=True, lower=True)  10.5 us
  transfers between devices with their start and end apart: 4, of which 4 were waited for; matrix products, arithmetic and copies ran while one was open for 2% of the time, Pallas kernels for 0%

profile of v8, /device:TPU:1, one launch (start us, length us, event | category | flops | bytes accessed | tf_op | source)
XLA Modules:
  0.0 240.5 jit_solution(12294795300660752646)
XLA Ops:
  0.6 1.7 copy-done
  2.4 2.6 %fusion.2 = bf16[256,256]{1,0:T(8,128)(2,1)S(1)} fusion(bf16[5120,256]{1,0:T(8,128)(2,1)S(1)} %copy-done, bf16[1,256,5120]{2,1,0:T(8,128)(2,1)} %param.5), kind=kOutput, calls=%fused_computation.8 | convolution fusion | flops 671154176 | bytes 5373952 | tf_op jit(solution)/shard_map/dot_general | solution.py:82
  5.0 0.1 copy.37
  5.1 1.0 broadcast_in_dim.54
  6.1 7.7 %all-to-all-start = ((bf16[8,256,256]{1,2,0:T(8,128)(2,1)}), bf16[8,256,256]{1,2,0:T(8,128)(2,1)}, u32[]{:S(2)}, u32[]{:S(2)}) async-start(bf16[8,256,256]{1,2,0:T(8,128)(2,1)} %broadcast_in_dim.54), calls=%async_computation | async-start | bytes 2097152 | tf_op jit(solution)/shard_map/all_to_all | solution.py:16
  13.8 24.2 %all-to-all-done = bf16[8,256,256]{1,2,0:T(8,128)(2,1)} async-done(((bf16[8,256,256]{1,2,0:T(8,128)(2,1)}), bf16[8,256,256]{1,2,0:T(8,128)(2,1)}, u32[]{:S(2)}, u32[]{:S(2)}) %all-to-all-start) | async-done | bytes 1048608 | tf_op jit(solution)/shard_map/all_to_all | solution.py:16
  38.0 1.7 fusion.32
  39.7 1.3 copy-done.3
  41.0 1.1 dynamic-slice_bitcast_fusion
  42.1 7.5 %collective-permute-start = (f32[4,256,256]{1,2,0:T(8,128)}, f32[4,256,256]{1,2,0:T(8,128)}, u32[]{:S(2)}, u32[]{:S(2)}) collective-permute-start(f32[4,256,256]{1,2,0:T(8,128)} %dynamic-slice_bitcast_fusion), channel_id=1, source_target_pairs={{0,8},{8,0},{1,9},{9,1},{2,10},{10,2},{3,11},{11,3},{4,12},{12,4},... | collective-permute-start | bytes 3145736 | tf_op jit(solution)/shard_map/ppermute | solution.py:24
  49.6 2.6 %collective-permute-done = f32[4,256,256]{1,2,0:T(8,128)} collective-permute-done((f32[4,256,256]{1,2,0:T(8,128)}, f32[4,256,256]{1,2,0:T(8,128)}, u32[]{:S(2)}, u32[]{:S(2)}) %collective-permute-start) | collective-permute-done | bytes 1048608 | tf_op jit(solution)/shard_map/ppermute | solution.py:24
  52.2 1.7 fusion.6
  53.8 18.0 %all_to_all.30 = f32[4,1,256,256]{2,3,1,0:T(8,128)S(1)} all-to-all(f32[4,1,256,256]{2,3,1,0:T(8,128)S(1)} %fusion.6), channel_id=1, replica_groups=mesh['x'=4,'z'=12,'c'=2,'mdl'=8] {'x'}, dimensions={0} | all-to-all | bytes 2097152 | tf_op jit(solution)/shard_map/all_to_all | solution.py:11
  71.9 0.1 copy.39
  72.1 28.6 %all_to_all.31 = f32[12,43,128]{2,1,0:T(8,128)S(1)} all-to-all(f32[12,43,128]{2,1,0:T(8,128)S(1)} %reshape.67), channel_id=1, replica_groups=mesh['x'=4,'z'=12,'c'=2,'mdl'=8] {'z'}, dimensions={0} | all-to-all | bytes 528384 | tf_op jit(solution)/shard_map/all_to_all | solution.py:11
  100.8 17.6 %all_to_all.32 = f32[12,43,128]{2,1,0:T(8,128)S(1)} all-to-all(f32[12,43,128]{2,1,0:T(8,128)S(1)} %broadcast_in_dim.55), channel_id=1, replica_groups=mesh['x'=4,'z'=12,'c'=2,'mdl'=8] {'z'}, dimensions={0} | all-to-all | bytes 528384 | tf_op jit(solution)/shard_map/all_to_all | solution.py:16
  118.6 0.1 copy.40
  118.8 14.7 %all_to_all.33 = f32[4,1,256,256]{2,3,1,0:T(8,128)} all-to-all(f32[4,1,256,256]{2,3,1,0:T(8,128)S(1)} %broadcast_in_dim.57), channel_id=1, replica_groups=mesh['x'=4,'z'=12,'c'=2,'mdl'=8] {'x'}, dimensions={0} | all-to-all | bytes 2097152 | tf_op jit(solution)/shard_map/all_to_all | solution.py:16
  133.4 7.2 %collective-permute-start.1 = (f32[4,256,256]{1,2,0:T(8,128)}, f32[4,256,256]{1,2,0:T(8,128)}, u32[]{:S(2)}, u32[]{:S(2)}) collective-permute-start(f32[4,256,256]{1,2,0:T(8,128)} %bitcast.9), channel_id=1, source_target_pairs={{0,8},{8,0},{1,9},{9,1},{2,10},{10,2},{3,11},{11,3},{4,12},{12,4},... | collective-permute-start | bytes 3145736 | tf_op jit(solution)/shard_map/ppermute | solution.py:29
  140.7 2.6 %collective-permute-done.1 = f32[4,256,256]{1,2,0:T(8,128)} collective-permute-done((f32[4,256,256]{1,2,0:T(8,128)}, f32[4,256,256]{1,2,0:T(8,128)}, u32[]{:S(2)}, u32[]{:S(2)}) %collective-permute-start.1) | collective-permute-done | bytes 1048608 | tf_op jit(solution)/shard_map/ppermute | solution.py:29
  143.3 2.6 %maximum_select_fusion = f32[8,256,256]{1,2,0:T(8,128)S(1)} fusion(f32[4,256,256]{1,2,0:T(8,128)} %collective-permute-done.1, f32[4,256,256]{1,2,0:T(8,128)} %bitcast.9, pred[]{:T(512)S(6)} %eq.15), kind=kLoop, calls=%fused_computation.3 | loop fusion | flops 1572864 | bytes 4194305 | tf_op jit(solution)/shard_map/jit(_where)/select_n | solution.py:30
  145.9 1.3 copy-done.2
  147.4 11.7 %cholesky.44 = f32[128,128]{1,0:T(8,128)S(1)} custom-call(f32[128,128]{1,0:T(8,128)S(1)} %fusion.43), custom_call_target="Cholesky" | custom-call | tf_op jit(solution)/shard_map/jit(cholesky)/cholesky | solution.py:68
  159.1 0.6 compare_reduce_fusion.1
  159.8 0.7 fusion.34
  160.4 9.8 %custom-call.8 = f32[1,128,128]{1,2,0:T(8,128)S(1)} custom-call(f32[1,128,128]{2,1,0:T(8,128)S(1)} %fusion.34), custom_call_target="InvertDiagBlocksLowerTriangular" | custom-call | tf_op jit(solution)/shard_map/triangular_solve/custom-call.0 | solution.py:69
  170.2 0.3 fusion.41
  170.5 0.3 fusion.36
  170.8 0.3 slice_subtract_fusion
  171.1 0.2 fusion.52
  171.3 1.4 gather_fusion
  172.8 11.7 %cholesky.55 = f32[128,128]{1,0:T(8,128)S(1)} custom-call(f32[128,128]{1,0:T(8,128)S(1)} %fusion.40), custom_call_target="Cholesky" | custom-call | tf_op jit(solution)/shard_map/jit(cholesky)/cholesky | solution.py:72
  184.6 0.6 compare_reduce_fusion
  185.2 0.7 fusion.35
  185.9 9.8 %custom-call.9 = f32[1,128,128]{1,2,0:T(8,128)S(1)} custom-call(f32[1,128,128]{2,1,0:T(8,128)S(1)} %fusion.35), custom_call_target="InvertDiagBlocksLowerTriangular" | custom-call | tf_op jit(solution)/shard_map/triangular_solve/custom-call.0 | solution.py:73
  195.7 0.3 bitcast_add_fusion.1
  196.0 0.3 convolution_negate_fusion
  196.3 1.1 broadcast_in_dim.61
  197.4 4.3 %all-to-all-start.5 = ((f32[8,257,128]{2,1,0:T(8,128)}), f32[8,257,128]{2,1,0:T(8,128)}, u32[]{:S(2)}, u32[]{:S(2)}) async-start(f32[8,257,128]{2,1,0:T(8,128)} %broadcast_in_dim.61), calls=%async_computation.5 | async-start | bytes 2162688 | tf_op jit(solution)/shard_map/all_to_all | solution.py:16
  201.8 4.0 %convolution_bitcast_fusion = f32[8,256,256]{1,2,0:T(8,128)} fusion(f32[8,256,256]{1,2,0:T(8,128)} %copy-done.2, f32[128,128]{1,0:T(8,128)S(1)} %fusion.41, f32[128,128]{1,0:T(8,128)S(1)} %copy.44, f32[128,128]{1,0:T(8,128)S(1)} %convolution_negate_fusion), kind=kOutput, calls=%fused_computation.6 | convolution fusion | flops 805568512 | bytes 4390912 | tf_op jit(solution)/shard_map/ab,jbc->jac/dot_general | solution.py:96
  205.8 23.5 %all-to-all-done.5 = f32[8,257,128]{2,1,0:T(8,128)} async-done(((f32[8,257,128]{2,1,0:T(8,128)}), f32[8,257,128]{2,1,0:T(8,128)}, u32[]{:S(2)}, u32[]{:S(2)}) %all-to-all-start.5) | async-done | bytes 1052704 | tf_op jit(solution)/shard_map/all_to_all | solution.py:16
  229.3 0.9 slice.50
  230.2 1.9 fusion.7
  232.1 1.7 convolution_add_fusion
  233.8 1.7 fusion.9
  235.5 1.6 multiply_reduce_fusion
  237.1 0.5 multiply_bitcast_fusion
  237.7 2.9 %copy.49 = f32[256,2048]{1,0:T(8,128)} copy(f32[256,2048]{0,1:T(8,128)} %bitcast.72) | data formatting | bytes 4194304
  (28 shorter events, 0.9 us)
Async XLA Ops:
  0.6 1.7 copy-start
  6.1 31.9 %all-to-all-start = ((bf16[8,256,256]{1,2,0:T(8,128)(2,1)}), bf16[8,256,256]{1,2,0:T(8,128)(2,1)}, u32[]{:S(2)}, u32[]{:S(2)}) async-start(bf16[8,256,256]{1,2,0:T(8,128)(2,1)} %broadcast_in_dim.54), calls=%async_computation | async-start | bytes 2097152 | tf_op jit(solution)/shard_map/all_to_all | solution.py:16
  39.7 1.3 copy-start.3
  42.1 10.1 %collective-permute-start = (f32[4,256,256]{1,2,0:T(8,128)}, f32[4,256,256]{1,2,0:T(8,128)}, u32[]{:S(2)}, u32[]{:S(2)}) collective-permute-start(f32[4,256,256]{1,2,0:T(8,128)} %dynamic-slice_bitcast_fusion), channel_id=1, source_target_pairs={{0,8},{8,0},{1,9},{9,1},{2,10},{10,2},{3,11},{11,3},{4,12},{12,4},... | collective-permute-start | bytes 3145736 | tf_op jit(solution)/shard_map/ppermute | solution.py:24
  133.4 9.8 %collective-permute-start.1 = (f32[4,256,256]{1,2,0:T(8,128)}, f32[4,256,256]{1,2,0:T(8,128)}, u32[]{:S(2)}, u32[]{:S(2)}) collective-permute-start(f32[4,256,256]{1,2,0:T(8,128)} %bitcast.9), channel_id=1, source_target_pairs={{0,8},{8,0},{1,9},{9,1},{2,10},{10,2},{3,11},{11,3},{4,12},{12,4},... | collective-permute-start | bytes 3145736 | tf_op jit(solution)/shard_map/ppermute | solution.py:29
  145.9 1.3 copy-start.2
  197.4 31.9 %all-to-all-start.5 = ((f32[8,257,128]{2,1,0:T(8,128)}), f32[8,257,128]{2,1,0:T(8,128)}, u32[]{:S(2)}, u32[]{:S(2)}) async-start(f32[8,257,128]{2,1,0:T(8,128)} %broadcast_in_dim.61), calls=%async_computation.5 | async-start | bytes 2162688 | tf_op jit(solution)/shard_map/all_to_all | solution.py:16
  229.3 2.9 %copy-start.1 = (f32[8,256,256]{1,2,0:T(8,128)S(1)}, f32[8,256,256]{1,2,0:T(8,128)}, u32[]{:S(2)}) copy-start(f32[8,256,256]{1,2,0:T(8,128)} %convolution_bitcast_fusion) | copy-start | bytes 6291460

commit v9 on v7

--- a/solution.py
+++ b/solution.py
@@ -24,12 +24,6 @@
     return mine + lax.ppermute(theirs, axis, [(0, 1), (1, 0)])
 
 
-def swap_halves_join(half, axis):
-    side = lax.axis_index(axis)
-    other = lax.ppermute(half, axis, [(0, 1), (1, 0)])
-    return jnp.where(side == 0, jnp.concatenate([half, other], 0), jnp.concatenate([other, half], 0))
-
-
 def sum_over_tokens(tiles, pair, ring, outer, lanes=128):
     n_ring = lax.axis_size(ring)
     n_out = lax.axis_size(outer)
@@ -41,8 +35,7 @@
     padded = jnp.pad(flat, ((0, pad), (0, 0))).reshape(n_out, -1, lanes)
     piece = scatter_sum(padded, outer)
     flat = gather_all(piece, outer, n_out).reshape(-1, lanes)[: flat.shape[0]]
-    part = gather_all(flat.reshape(part.shape), ring, n_ring).reshape((n_ring * each,) + part.shape[1:])
-    return swap_halves_join(part, pair)
+    return gather_all(flat.reshape(part.shape), ring, n_ring).reshape((n_ring * each,) + part.shape[1:])
 
 
 def pack_lower(m):
@@ -77,20 +70,42 @@
     return jnp.concatenate([upper, lower], axis=0)
 
 
+def times_inverses_t(left_done, packed):
+    half = packed.shape[-1]
+    low_left, folded, diag = packed[:, :half], packed[:, half:2 * half], packed[:, 2 * half]
+    top = jnp.tril(folded, -1) + diag[:, :, None] * jnp.eye(half, dtype=packed.dtype)
+    low_right_t = jnp.triu(folded)
+    first, second = left_done[..., :half], left_done[..., half:]
+    out_first = jnp.einsum("jac,jdc->jad", first, top, precision=lax.Precision.HIGH)
+    out_second = jnp.einsum("jac,jdc->jad", first, low_left, precision=lax.Precision.HIGH) + jnp.einsum(
+        "jac,jcd->jad", second, low_right_t, precision=lax.Precision.HIGH)
+    return jnp.concatenate([out_first, out_second], axis=-1)
+
+
 def on_device(hidden, sketch):
     states = hidden[0]
     projected = jnp.dot(states, sketch, preferred_element_type=jnp.float32).astype(jnp.bfloat16)
     basis_width = projected.shape[1]
     models = lax.axis_size("mdl")
     me = lax.axis_index("mdl")
+    side = lax.axis_index("c")
     everyone = gather_all(projected, "mdl", models)
     local_tiles = jnp.einsum("ta,jtc->jac", projected, everyone, preferred_element_type=jnp.float32)
-    tiles = sum_over_tokens(local_tiles, "c", "x", "z")
-    gram_total = lax.dynamic_index_in_dim(tiles, me, 0, keepdims=False)
+    own = sum_over_tokens(local_tiles, "c", "x", "z")
+    other = lax.ppermute(own, "c", [(0, 1), (1, 0)])
+    each = own.shape[0]
+    at = me % each
+    mine_here = me // each == side
+    gram_total = jnp.where(mine_here, lax.dynamic_index_in_dim(own, at, 0, keepdims=False),
+                           lax.dynamic_index_in_dim(other, at, 0, keepdims=False))
     inverse = factor_inverse(gram_total)
-    inverses = unpack_lower(gather_all(pack_lower(inverse), "mdl", models))
-    left_done = jnp.einsum("ab,jbc->jac", inverse, tiles, precision=lax.Precision.HIGH)
-    right_done = jnp.einsum("jac,jdc->jad", left_done, inverses, precision=lax.Precision.HIGH)
+    packed = gather_all(pack_lower(inverse), "mdl", models)
+    packed_own = lax.dynamic_slice_in_dim(packed, side * each, each, 0)
+    packed_other = lax.dynamic_slice_in_dim(packed, (1 - side) * each, each, 0)
+    right_own = times_inverses_t(jnp.einsum("ab,jbc->jac", inverse, own, precision=lax.Precision.HIGH), packed_own)
+    right_other = times_inverses_t(jnp.einsum("ab,jbc->jac", inverse, other, precision=lax.Precision.HIGH), packed_other)
+    right_done = jnp.where(side == 0, jnp.concatenate([right_own, right_other], 0),
+                           jnp.concatenate([right_other, right_own], 0))
     cross_gram = right_done.transpose(1, 0, 2).reshape(basis_width, models * basis_width)
     similarity = jnp.sum(right_done * right_done, axis=(1, 2)) / basis_width
     return (cross_gram, similarity[None, :])

time: 248 us -> 245 us (0.988)
  local copies, waits for them, and re-layouts: 18.4 us -> 12 us
  matrix products: 14 us -> 20.1 us
    dot_general x2 -> x8, matrix products: 8.19 us -> 14.3 us  [the longest x2 3.13 us: times_inverses_t(): jnp.einsum('jac,jdc->jad', first, low_left, precision=lax.Precision.HIGH)]
    unnamed x9, local copies, waits for them, and re-layouts: 9.72 us -> 5.94 us
where the time goes in v9:
time: 245 us; the launch traced here: 241 us
  blocking collectives  78.9 us (32%)
  waiting for transfers between devices  51 us (21%)
  other arithmetic  51 us (21%)
  starting transfers between devices  26.8 us (11%)
  matrix products  20.1 us (8%)
  local copies, waits for them, and re-layouts  12 us (5%)
    all_to_all x2, blocking collectives, scatter_sum(): return lax.all_to_all(chunks, axes, 0, 0, tiled=True).sum(axis=0)  46.6 us
    all_to_all x2, waiting for transfers between devices, gather_all(): return lax.all_to_all(copies, axes, 0, 0, tiled=True)  46 us
    all_to_all x2, blocking collectives, gather_all(): return lax.all_to_all(copies, axes, 0, 0, tiled=True)  32.3 us
    another operation x3, other arithmetic, factor_inverse(): top = jnp.linalg.cholesky(gram[:h, :h])  12.4 us
    another operation x3, other arithmetic, factor_inverse(): low = jnp.linalg.cholesky(rest)  12.4 us
    all_to_all x2, starting transfers between devices, gather_all(): return lax.all_to_all(copies, axes, 0, 0, tiled=True)  11.9 us
    another operation x2, other arithmetic, factor_inverse(): low_inv = lax.linalg.triangular_solve(low, eye, left_side=True, lower=True)  10.7 us
    another operation x2, other arithmetic, factor_inverse(): top_inv = lax.linalg.triangular_solve(top, eye, left_side=True, lower=True)  10.5 us
  transfers between devices with their start and end apart: 4, of which 4 were waited for; matrix products, arithmetic and copies ran while one was open for 2% of the time, Pallas kernels for 0%

profile of v9, /device:TPU:1, one launch (start us, length us, event | category | flops | bytes accessed | tf_op | source)
XLA Modules:
  0.0 240.8 jit_solution(8866582889095601774)
XLA Ops:
  0.6 1.7 copy-done
  2.4 2.6 %fusion.2 = bf16[256,256]{1,0:T(8,128)(2,1)S(1)} fusion(bf16[5120,256]{1,0:T(8,128)(2,1)S(1)} %copy-done, bf16[1,256,5120]{2,1,0:T(8,128)(2,1)} %param.5), kind=kOutput, calls=%fused_computation.9 | convolution fusion | flops 671154176 | bytes 5373952 | tf_op jit(solution)/shard_map/dot_general | solution.py:87
  5.1 1.0 broadcast_in_dim.63
  6.1 7.7 %all-to-all-start = ((bf16[8,256,256]{1,2,0:T(8,128)(2,1)}), bf16[8,256,256]{1,2,0:T(8,128)(2,1)}, u32[]{:S(2)}, u32[]{:S(2)}) async-start(bf16[8,256,256]{1,2,0:T(8,128)(2,1)} %broadcast_in_dim.63), calls=%async_computation | async-start | bytes 2097152 | tf_op jit(solution)/shard_map/all_to_all | solution.py:16
  13.8 24.2 %all-to-all-done = bf16[8,256,256]{1,2,0:T(8,128)(2,1)} async-done(((bf16[8,256,256]{1,2,0:T(8,128)(2,1)}), bf16[8,256,256]{1,2,0:T(8,128)(2,1)}, u32[]{:S(2)}, u32[]{:S(2)}) %all-to-all-start) | async-done | bytes 1048608 | tf_op jit(solution)/shard_map/all_to_all | solution.py:16
  38.0 1.7 fusion.37
  39.7 1.3 copy-done.1
  41.0 1.1 dynamic-slice_bitcast_fusion
  42.1 7.5 %collective-permute-start = (f32[4,256,256]{1,2,0:T(8,128)}, f32[4,256,256]{1,2,0:T(8,128)}, u32[]{:S(2)}, u32[]{:S(2)}) collective-permute-start(f32[4,256,256]{1,2,0:T(8,128)} %dynamic-slice_bitcast_fusion), channel_id=1, source_target_pairs={{0,8},{8,0},{1,9},{9,1},{2,10},{10,2},{3,11},{11,3},{4,12},{12,4},... | collective-permute-start | bytes 3145736 | tf_op jit(solution)/shard_map/ppermute | solution.py:24
  49.6 2.6 %collective-permute-done = f32[4,256,256]{1,2,0:T(8,128)} collective-permute-done((f32[4,256,256]{1,2,0:T(8,128)}, f32[4,256,256]{1,2,0:T(8,128)}, u32[]{:S(2)}, u32[]{:S(2)}) %collective-permute-start) | collective-permute-done | bytes 1048608 | tf_op jit(solution)/shard_map/ppermute | solution.py:24
  52.2 1.7 fusion.5
  53.8 18.0 %all_to_all.30 = f32[4,1,256,256]{2,3,1,0:T(8,128)S(1)} all-to-all(f32[4,1,256,256]{2,3,1,0:T(8,128)S(1)} %fusion.5), channel_id=1, replica_groups=mesh['x'=4,'z'=12,'c'=2,'mdl'=8] {'x'}, dimensions={0} | all-to-all | bytes 2097152 | tf_op jit(solution)/shard_map/all_to_all | solution.py:11
  72.1 28.6 %all_to_all.31 = f32[12,43,128]{2,1,0:T(8,128)S(1)} all-to-all(f32[12,43,128]{2,1,0:T(8,128)S(1)} %reshape.70), channel_id=1, replica_groups=mesh['x'=4,'z'=12,'c'=2,'mdl'=8] {'z'}, dimensions={0} | all-to-all | bytes 528384 | tf_op jit(solution)/shard_map/all_to_all | solution.py:11
  100.8 17.6 %all_to_all.32 = f32[12,43,128]{2,1,0:T(8,128)S(1)} all-to-all(f32[12,43,128]{2,1,0:T(8,128)S(1)} %broadcast_in_dim.64), channel_id=1, replica_groups=mesh['x'=4,'z'=12,'c'=2,'mdl'=8] {'z'}, dimensions={0} | all-to-all | bytes 528384 | tf_op jit(solution)/shard_map/all_to_all | solution.py:16
  118.8 14.6 %all_to_all.33 = f32[4,1,256,256]{2,3,1,0:T(8,128)} all-to-all(f32[4,1,256,256]{2,3,1,0:T(8,128)S(1)} %broadcast_in_dim.66), channel_id=1, replica_groups=mesh['x'=4,'z'=12,'c'=2,'mdl'=8] {'x'}, dimensions={0} | all-to-all | bytes 2097152 | tf_op jit(solution)/shard_map/all_to_all | solution.py:16
  133.4 7.4 %collective-permute-start.1 = (f32[4,256,256]{1,2,0:T(8,128)}, f32[4,256,256]{1,2,0:T(8,128)}, u32[]{:S(2)}, u32[]{:S(2)}) collective-permute-start(f32[4,256,256]{1,2,0:T(8,128)} %bitcast.9), channel_id=1, source_target_pairs={{0,8},{8,0},{1,9},{9,1},{2,10},{10,2},{3,11},{11,3},{4,12},{12,4},... | collective-permute-start | bytes 3145736 | tf_op jit(solution)/shard_map/ppermute | solution.py:95
  140.9 2.4 collective-permute-done.1
  143.3 1.1 bitcast_select_fusion
  144.5 11.7 %cholesky.44 = f32[128,128]{1,0:T(8,128)S(1)} custom-call(f32[128,128]{1,0:T(8,128)S(1)} %fusion.60), custom_call_target="Cholesky" | custom-call | tf_op jit(solution)/shard_map/jit(cholesky)/cholesky | solution.py:61
  156.2 0.6 compare_reduce_fusion.1
  156.8 0.7 fusion.51
  157.5 9.8 %custom-call.8 = f32[1,128,128]{1,2,0:T(8,128)S(1)} custom-call(f32[1,128,128]{2,1,0:T(8,128)S(1)} %fusion.51), custom_call_target="InvertDiagBlocksLowerTriangular" | custom-call | tf_op jit(solution)/shard_map/triangular_solve/custom-call.0 | solution.py:62
  167.3 0.3 fusion.58
  167.6 0.3 fusion.53
  167.9 0.2 fusion.81
  168.1 0.3 slice_subtract_fusion
  168.5 11.7 %cholesky.55 = f32[128,128]{1,0:T(8,128)S(1)} custom-call(f32[128,128]{1,0:T(8,128)S(1)} %fusion.57), custom_call_target="Cholesky" | custom-call | tf_op jit(solution)/shard_map/jit(cholesky)/cholesky | solution.py:65
  180.3 0.6 compare_reduce_fusion
  180.9 0.7 fusion.52
  181.6 10.0 %custom-call.9 = f32[1,128,128]{1,2,0:T(8,128)S(1)} custom-call(f32[1,128,128]{2,1,0:T(8,128)S(1)} %fusion.52), custom_call_target="InvertDiagBlocksLowerTriangular" | custom-call | tf_op jit(solution)/shard_map/triangular_solve/custom-call.0 | solution.py:66
  191.6 1.2 gather_fusion
  192.8 0.3 bitcast_add_fusion.1
  193.1 0.3 convolution_negate_fusion
  193.4 1.1 broadcast_in_dim.70
  194.5 4.2 %all-to-all-start.5 = ((f32[8,257,128]{2,1,0:T(8,128)}), f32[8,257,128]{2,1,0:T(8,128)}, u32[]{:S(2)}, u32[]{:S(2)}) async-start(f32[8,257,128]{2,1,0:T(8,128)} %broadcast_in_dim.70), calls=%async_computation.5 | async-start | bytes 2162688 | tf_op jit(solution)/shard_map/all_to_all | solution.py:16
  198.9 2.8 %convolution_bitcast_fusion = f32[4,256,256]{1,2,0:T(8,128)} fusion(f32[4,256,256]{1,2,0:T(8,128)} %collective-permute-done.1, f32[128,128]{1,0:T(8,128)S(1)} %fusion.58, f32[128,128]{1,0:T(8,128)S(1)} %copy.56, f32[128,128]{1,0:T(8,128)S(1)} %convolution_negate_fusion), kind=kOutput, calls=%fused_computation.5 | convolution fusion | flops 402915328 | bytes 2293760 | tf_op jit(solution)/shard_map/ab,jbc->jac/dot_general | solution.py:106
  201.7 2.8 %convolution_bitcast_fusion.1 = f32[4,256,256]{1,2,0:T(8,128)} fusion(f32[128,128]{1,0:T(8,128)S(1)} %fusion.58, f32[128,128]{1,0:T(8,128)S(1)} %copy.56, f32[128,128]{1,0:T(8,128)S(1)} %convolution_negate_fusion, f32[4,1,256,256]{2,3,1,0:T(8,128)} %all_to_all.33), kind=kOutput, calls=%fused_computation.6 | convolution fusion | flops 402915328 | bytes 2293760 | tf_op jit(solution)/shard_map/ab,jbc->jac/dot_general | solution.py:105
  204.6 21.8 %all-to-all-done.5 = f32[8,257,128]{2,1,0:T(8,128)} async-done(((f32[8,257,128]{2,1,0:T(8,128)}), f32[8,257,128]{2,1,0:T(8,128)}, u32[]{:S(2)}, u32[]{:S(2)}) %all-to-all-start.5) | async-done | bytes 1052704 | tf_op jit(solution)/shard_map/all_to_all | solution.py:16
  226.3 1.6 fusion.8
  227.9 0.7 constant_dynamic-slice_fusion
  228.7 1.6 fusion.12
  230.2 1.4 convolution_add_fusion
  231.6 1.4 fusion.10
  233.0 1.4 fusion.14
  234.4 1.4 convolution_add_fusion.1
  235.8 1.6 multiply_reduce_fusion
  237.4 2.9 %copy.65 = f32[256,2048]{1,0:T(8,128)} copy(f32[256,2048]{0,1:T(8,128)} %bitcast.78) | data formatting | bytes 4194304
  240.3 0.5 multiply_bitcast_fusion
  (31 shorter events, 1.2 us)
Async XLA Ops:
  0.6 1.7 copy-start
  6.1 31.9 %all-to-all-start = ((bf16[8,256,256]{1,2,0:T(8,128)(2,1)}), bf16[8,256,256]{1,2,0:T(8,128)(2,1)}, u32[]{:S(2)}, u32[]{:S(2)}) async-start(bf16[8,256,256]{1,2,0:T(8,128)(2,1)} %broadcast_in_dim.63), calls=%async_computation | async-start | bytes 2097152 | tf_op jit(solution)/shard_map/all_to_all | solution.py:16
  39.7 1.3 copy-start.1
  42.1 10.1 %collective-permute-start = (f32[4,256,256]{1,2,0:T(8,128)}, f32[4,256,256]{1,2,0:T(8,128)}, u32[]{:S(2)}, u32[]{:S(2)}) collective-permute-start(f32[4,256,256]{1,2,0:T(8,128)} %dynamic-slice_bitcast_fusion), channel_id=1, source_target_pairs={{0,8},{8,0},{1,9},{9,1},{2,10},{10,2},{3,11},{11,3},{4,12},{12,4},... | collective-permute-start | bytes 3145736 | tf_op jit(solution)/shard_map/ppermute | solution.py:24
  133.4 9.8 %collective-permute-start.1 = (f32[4,256,256]{1,2,0:T(8,128)}, f32[4,256,256]{1,2,0:T(8,128)}, u32[]{:S(2)}, u32[]{:S(2)}) collective-permute-start(f32[4,256,256]{1,2,0:T(8,128)} %bitcast.9), channel_id=1, source_target_pairs={{0,8},{8,0},{1,9},{9,1},{2,10},{10,2},{3,11},{11,3},{4,12},{12,4},... | collective-permute-start | bytes 3145736 | tf_op jit(solution)/shard_map/ppermute | solution.py:95
  194.5 31.9 %all-to-all-start.5 = ((f32[8,257,128]{2,1,0:T(8,128)}), f32[8,257,128]{2,1,0:T(8,128)}, u32[]{:S(2)}, u32[]{:S(2)}) async-start(f32[8,257,128]{2,1,0:T(8,128)} %broadcast_in_dim.70), calls=%async_computation.5 | async-start | bytes 2162688 | tf_op jit(solution)/shard_map/all_to_all | solution.py:16
  226.3 3.9 %copy-start.3 = (f32[4,256,256]{1,2,0:T(8,128)S(1)}, f32[4,256,256]{1,2,0:T(8,128)}, u32[]{:S(2)}) copy-start(f32[4,256,256]{1,2,0:T(8,128)} %convolution_bitcast_fusion) | copy-start | bytes 3145732
  228.7 4.4 %copy-start.2 = (f32[4,256,256]{1,2,0:T(8,128)S(1)}, f32[4,256,256]{1,2,0:T(8,128)}, u32[]{:S(2)}) copy-start(f32[4,256,256]{1,2,0:T(8,128)} %convolution_bitcast_fusion.1) | copy-start | bytes 3145732

commit v10 on v8

--- a/solution.py
+++ b/solution.py
@@ -37,7 +37,7 @@
     each = part.shape[0] // n_ring
     part = scatter_sum(part.reshape((n_ring, each) + part.shape[1:]), ring)
     flat = part.reshape(-1, lanes)
-    pad = (-flat.shape[0]) % n_out
+    pad = (-flat.shape[0]) % (n_out * 8)
     padded = jnp.pad(flat, ((0, pad), (0, 0))).reshape(n_out, -1, lanes)
     piece = scatter_sum(padded, outer)
     flat = gather_all(piece, outer, n_out).reshape(-1, lanes)[: flat.shape[0]]

time: 245 us -> 245 us (level)
  no operation moved by 1% of the time
where the time goes in v10:
time: 245 us; the launch traced here: 240 us
  blocking collectives  78.9 us (32%)
  waiting for transfers between devices  52.9 us (22%)
  other arithmetic  52.3 us (21%)
  starting transfers between devices  26.6 us (11%)
  matrix products  15.1 us (6%)
  local copies, waits for them, and re-layouts  13.6 us (6%)
    all_to_all x2, waiting for transfers between devices, gather_all(): return lax.all_to_all(copies, axes, 0, 0, tiled=True)  47.7 us
    all_to_all x2, blocking collectives, scatter_sum(): return lax.all_to_all(chunks, axes, 0, 0, tiled=True).sum(axis=0)  46.6 us
    all_to_all x2, blocking collectives, gather_all(): return lax.all_to_all(copies, axes, 0, 0, tiled=True)  32.3 us
    another operation x3, other arithmetic, factor_inverse(): top = jnp.linalg.cholesky(gram[:h, :h])  12.4 us
    another operation x3, other arithmetic, factor_inverse(): low = jnp.linalg.cholesky(rest)  12.4 us
    all_to_all x2, starting transfers between devices, gather_all(): return lax.all_to_all(copies, axes, 0, 0, tiled=True)  11.9 us
    another operation x2, other arithmetic, factor_inverse(): top_inv = lax.linalg.triangular_solve(top, eye, left_side=True, lower=True)  10.5 us
    another operation x2, other arithmetic, factor_inverse(): low_inv = lax.linalg.triangular_solve(low, eye, left_side=True, lower=True)  10.5 us
  transfers between devices with their start and end apart: 4, of which 4 were waited for; matrix products, arithmetic and copies ran while one was open for 2% of the time, Pallas kernels for 0%

profile of v10, /device:TPU:1, one launch (start us, length us, event | category | flops | bytes accessed | tf_op | source)
XLA Modules:
  0.0 240.5 jit_solution(1495514085639139072)
XLA Ops:
  0.6 1.7 copy-done
  2.4 2.6 %fusion.2 = bf16[256,256]{1,0:T(8,128)(2,1)S(1)} fusion(bf16[5120,256]{1,0:T(8,128)(2,1)S(1)} %copy-done, bf16[1,256,5120]{2,1,0:T(8,128)(2,1)} %param.5), kind=kOutput, calls=%fused_computation.8 | convolution fusion | flops 671154176 | bytes 5373952 | tf_op jit(solution)/shard_map/dot_general | solution.py:82
  5.0 0.1 copy.37
  5.1 1.0 broadcast_in_dim.54
  6.1 7.7 %all-to-all-start = ((bf16[8,256,256]{1,2,0:T(8,128)(2,1)}), bf16[8,256,256]{1,2,0:T(8,128)(2,1)}, u32[]{:S(2)}, u32[]{:S(2)}) async-start(bf16[8,256,256]{1,2,0:T(8,128)(2,1)} %broadcast_in_dim.54), calls=%async_computation | async-start | bytes 2097152 | tf_op jit(solution)/shard_map/all_to_all | solution.py:16
  13.8 24.2 %all-to-all-done = bf16[8,256,256]{1,2,0:T(8,128)(2,1)} async-done(((bf16[8,256,256]{1,2,0:T(8,128)(2,1)}), bf16[8,256,256]{1,2,0:T(8,128)(2,1)}, u32[]{:S(2)}, u32[]{:S(2)}) %all-to-all-start) | async-done | bytes 1048608 | tf_op jit(solution)/shard_map/all_to_all | solution.py:16
  38.0 1.7 fusion.32
  39.7 1.3 copy-done.3
  41.0 1.1 dynamic-slice_bitcast_fusion
  42.1 7.5 %collective-permute-start = (f32[4,256,256]{1,2,0:T(8,128)}, f32[4,256,256]{1,2,0:T(8,128)}, u32[]{:S(2)}, u32[]{:S(2)}) collective-permute-start(f32[4,256,256]{1,2,0:T(8,128)} %dynamic-slice_bitcast_fusion), channel_id=1, source_target_pairs={{0,8},{8,0},{1,9},{9,1},{2,10},{10,2},{3,11},{11,3},{4,12},{12,4},... | collective-permute-start | bytes 3145736 | tf_op jit(solution)/shard_map/ppermute | solution.py:24
  49.6 2.6 %collective-permute-done = f32[4,256,256]{1,2,0:T(8,128)} collective-permute-done((f32[4,256,256]{1,2,0:T(8,128)}, f32[4,256,256]{1,2,0:T(8,128)}, u32[]{:S(2)}, u32[]{:S(2)}) %collective-permute-start) | collective-permute-done | bytes 1048608 | tf_op jit(solution)/shard_map/ppermute | solution.py:24
  52.2 1.7 fusion.6
  53.8 18.0 %all_to_all.30 = f32[4,1,256,256]{2,3,1,0:T(8,128)S(1)} all-to-all(f32[4,1,256,256]{2,3,1,0:T(8,128)S(1)} %fusion.6), channel_id=1, replica_groups=mesh['x'=4,'z'=12,'c'=2,'mdl'=8] {'x'}, dimensions={0} | all-to-all | bytes 2097152 | tf_op jit(solution)/shard_map/all_to_all | solution.py:11
  71.9 0.1 copy.39
  72.1 28.6 %all_to_all.31 = f32[12,48,128]{2,1,0:T(8,128)S(1)} all-to-all(f32[12,48,128]{2,1,0:T(8,128)S(1)} %bitcast.75), channel_id=1, replica_groups=mesh['x'=4,'z'=12,'c'=2,'mdl'=8] {'z'}, dimensions={0} | all-to-all | bytes 589824 | tf_op jit(solution)/shard_map/all_to_all | solution.py:11
  100.7 17.6 %all_to_all.32 = f32[12,48,128]{2,1,0:T(8,128)S(1)} all-to-all(f32[12,48,128]{2,1,0:T(8,128)S(1)} %broadcast_in_dim.55), channel_id=1, replica_groups=mesh['x'=4,'z'=12,'c'=2,'mdl'=8] {'z'}, dimensions={0} | all-to-all | bytes 589824 | tf_op jit(solution)/shard_map/all_to_all | solution.py:16
  118.5 0.1 copy.40
  118.7 14.7 %all_to_all.33 = f32[4,1,256,256]{2,3,1,0:T(8,128)} all-to-all(f32[4,1,256,256]{2,3,1,0:T(8,128)S(1)} %broadcast_in_dim.57), channel_id=1, replica_groups=mesh['x'=4,'z'=12,'c'=2,'mdl'=8] {'x'}, dimensions={0} | all-to-all | bytes 2097152 | tf_op jit(solution)/shard_map/all_to_all | solution.py:16
  133.4 7.2 %collective-permute-start.1 = (f32[4,256,256]{1,2,0:T(8,128)}, f32[4,256,256]{1,2,0:T(8,128)}, u32[]{:S(2)}, u32[]{:S(2)}) collective-permute-start(f32[4,256,256]{1,2,0:T(8,128)} %bitcast.11), channel_id=1, source_target_pairs={{0,8},{8,0},{1,9},{9,1},{2,10},{10,2},{3,11},{11,3},{4,12},{12,4},... | collective-permute-start | bytes 3145736 | tf_op jit(solution)/shard_map/ppermute | solution.py:29
  140.6 2.6 %collective-permute-done.1 = f32[4,256,256]{1,2,0:T(8,128)} collective-permute-done((f32[4,256,256]{1,2,0:T(8,128)}, f32[4,256,256]{1,2,0:T(8,128)}, u32[]{:S(2)}, u32[]{:S(2)}) %collective-permute-start.1) | collective-permute-done | bytes 1048608 | tf_op jit(solution)/shard_map/ppermute | solution.py:29
  143.2 2.6 %maximum_select_fusion = f32[8,256,256]{1,2,0:T(8,128)S(1)} fusion(f32[4,256,256]{1,2,0:T(8,128)} %collective-permute-done.1, f32[4,256,256]{1,2,0:T(8,128)} %bitcast.11, pred[]{:T(512)S(6)} %eq.15), kind=kLoop, calls=%fused_computation.3 | loop fusion | flops 1572864 | bytes 4194305 | tf_op jit(solution)/shard_map/jit(_where)/select_n | solution.py:30
  145.8 1.3 copy-done.2
  147.3 11.7 %cholesky.44 = f32[128,128]{1,0:T(8,128)S(1)} custom-call(f32[128,128]{1,0:T(8,128)S(1)} %fusion.43), custom_call_target="Cholesky" | custom-call | tf_op jit(solution)/shard_map/jit(cholesky)/cholesky | solution.py:68
  159.1 0.6 compare_reduce_fusion.1
  159.7 0.7 fusion.34
  160.4 9.8 %custom-call.8 = f32[1,128,128]{1,2,0:T(8,128)S(1)} custom-call(f32[1,128,128]{2,1,0:T(8,128)S(1)} %fusion.34), custom_call_target="InvertDiagBlocksLowerTriangular" | custom-call | tf_op jit(solution)/shard_map/triangular_solve/custom-call.0 | solution.py:69
  170.2 0.3 fusion.41
  170.5 0.3 fusion.36
  170.8 0.3 slice_subtract_fusion
  171.0 0.2 fusion.52
  171.2 1.4 gather_fusion
  172.8 11.7 %cholesky.55 = f32[128,128]{1,0:T(8,128)S(1)} custom-call(f32[128,128]{1,0:T(8,128)S(1)} %fusion.40), custom_call_target="Cholesky" | custom-call | tf_op jit(solution)/shard_map/jit(cholesky)/cholesky | solution.py:72
  184.5 0.6 compare_reduce_fusion
  185.2 0.7 fusion.35
  185.8 9.8 %custom-call.9 = f32[1,128,128]{1,2,0:T(8,128)S(1)} custom-call(f32[1,128,128]{2,1,0:T(8,128)S(1)} %fusion.35), custom_call_target="InvertDiagBlocksLowerTriangular" | custom-call | tf_op jit(solution)/shard_map/triangular_solve/custom-call.0 | solution.py:73
  195.7 0.3 bitcast_add_fusion.1
  195.9 0.3 convolution_negate_fusion
  196.2 1.1 broadcast_in_dim.61
  197.3 4.3 %all-to-all-start.5 = ((f32[8,257,128]{2,1,0:T(8,128)}), f32[8,257,128]{2,1,0:T(8,128)}, u32[]{:S(2)}, u32[]{:S(2)}) async-start(f32[8,257,128]{2,1,0:T(8,128)} %broadcast_in_dim.61), calls=%async_computation.5 | async-start | bytes 2162688 | tf_op jit(solution)/shard_map/all_to_all | solution.py:16
  201.8 4.0 %convolution_bitcast_fusion = f32[8,256,256]{1,2,0:T(8,128)} fusion(f32[8,256,256]{1,2,0:T(8,128)} %copy-done.2, f32[128,128]{1,0:T(8,128)S(1)} %fusion.41, f32[128,128]{1,0:T(8,128)S(1)} %copy.44, f32[128,128]{1,0:T(8,128)S(1)} %convolution_negate_fusion), kind=kOutput, calls=%fused_computation.6 | convolution fusion | flops 805568512 | bytes 4390912 | tf_op jit(solution)/shard_map/ab,jbc->jac/dot_general | solution.py:96
  205.7 23.5 %all-to-all-done.5 = f32[8,257,128]{2,1,0:T(8,128)} async-done(((f32[8,257,128]{2,1,0:T(8,128)}), f32[8,257,128]{2,1,0:T(8,128)}, u32[]{:S(2)}, u32[]{:S(2)}) %all-to-all-start.5) | async-done | bytes 1052704 | tf_op jit(solution)/shard_map/all_to_all | solution.py:16
  229.2 0.9 slice.50
  230.1 1.9 fusion.7
  232.1 1.7 convolution_add_fusion
  233.8 1.7 fusion.9
  235.5 1.6 multiply_reduce_fusion
  237.1 0.5 multiply_bitcast_fusion
  237.6 2.9 %copy.49 = f32[256,2048]{1,0:T(8,128)} copy(f32[256,2048]{0,1:T(8,128)} %bitcast.74) | data formatting | bytes 4194304
  (26 shorter events, 0.8 us)
Async XLA Ops:
  0.6 1.7 copy-start
  6.1 31.9 %all-to-all-start = ((bf16[8,256,256]{1,2,0:T(8,128)(2,1)}), bf16[8,256,256]{1,2,0:T(8,128)(2,1)}, u32[]{:S(2)}, u32[]{:S(2)}) async-start(bf16[8,256,256]{1,2,0:T(8,128)(2,1)} %broadcast_in_dim.54), calls=%async_computation | async-start | bytes 2097152 | tf_op jit(solution)/shard_map/all_to_all | solution.py:16
  39.7 1.3 copy-start.3
  42.1 10.1 %collective-permute-start = (f32[4,256,256]{1,2,0:T(8,128)}, f32[4,256,256]{1,2,0:T(8,128)}, u32[]{:S(2)}, u32[]{:S(2)}) collective-permute-start(f32[4,256,256]{1,2,0:T(8,128)} %dynamic-slice_bitcast_fusion), channel_id=1, source_target_pairs={{0,8},{8,0},{1,9},{9,1},{2,10},{10,2},{3,11},{11,3},{4,12},{12,4},... | collective-permute-start | bytes 3145736 | tf_op jit(solution)/shard_map/ppermute | solution.py:24
  133.4 9.8 %collective-permute-start.1 = (f32[4,256,256]{1,2,0:T(8,128)}, f32[4,256,256]{1,2,0:T(8,128)}, u32[]{:S(2)}, u32[]{:S(2)}) collective-permute-start(f32[4,256,256]{1,2,0:T(8,128)} %bitcast.11), channel_id=1, source_target_pairs={{0,8},{8,0},{1,9},{9,1},{2,10},{10,2},{3,11},{11,3},{4,12},{12,4},... | collective-permute-start | bytes 3145736 | tf_op jit(solution)/shard_map/ppermute | solution.py:29
  145.8 1.3 copy-start.2
  197.3 31.9 %all-to-all-start.5 = ((f32[8,257,128]{2,1,0:T(8,128)}), f32[8,257,128]{2,1,0:T(8,128)}, u32[]{:S(2)}, u32[]{:S(2)}) async-start(f32[8,257,128]{2,1,0:T(8,128)} %broadcast_in_dim.61), calls=%async_computation.5 | async-start | bytes 2162688 | tf_op jit(solution)/shard_map/all_to_all | solution.py:16
  229.2 2.9 %copy-start.1 = (f32[8,256,256]{1,2,0:T(8,128)S(1)}, f32[8,256,256]{1,2,0:T(8,128)}, u32[]{:S(2)}) copy-start(f32[8,256,256]{1,2,0:T(8,128)} %convolution_bitcast_fusion) | copy-start | bytes 6291460

commit v11 on v8

--- a/solution.py
+++ b/solution.py
@@ -16,24 +16,10 @@
     return lax.all_to_all(copies, axes, 0, 0, tiled=True)
 
 
-def swap_halves_sum(tiles, axis):
-    side = lax.axis_index(axis)
-    halves = tiles.reshape((2, tiles.shape[0] // 2) + tiles.shape[1:])
-    mine = lax.dynamic_index_in_dim(halves, side, 0, keepdims=False)
-    theirs = lax.dynamic_index_in_dim(halves, 1 - side, 0, keepdims=False)
-    return mine + lax.ppermute(theirs, axis, [(0, 1), (1, 0)])
-
-
-def swap_halves_join(half, axis):
-    side = lax.axis_index(axis)
-    other = lax.ppermute(half, axis, [(0, 1), (1, 0)])
-    return jnp.where(side == 0, jnp.concatenate([half, other], 0), jnp.concatenate([other, half], 0))
-
-
 def sum_over_tokens(tiles, pair, ring, outer, lanes=128):
     n_ring = lax.axis_size(ring)
     n_out = lax.axis_size(outer)
-    part = swap_halves_sum(tiles, pair)
+    part = scatter_sum(tiles.reshape((2, tiles.shape[0] // 2) + tiles.shape[1:]), pair)
     each = part.shape[0] // n_ring
     part = scatter_sum(part.reshape((n_ring, each) + part.shape[1:]), ring)
     flat = part.reshape(-1, lanes)
@@ -42,7 +28,7 @@
     piece = scatter_sum(padded, outer)
     flat = gather_all(piece, outer, n_out).reshape(-1, lanes)[: flat.shape[0]]
     part = gather_all(flat.reshape(part.shape), ring, n_ring).reshape((n_ring * each,) + part.shape[1:])
-    return swap_halves_join(part, pair)
+    return gather_all(part, pair, 2).reshape((2 * part.shape[0],) + part.shape[1:])
 
 
 def pack_lower(m):

time: 245 us -> 251 us (1.024)
  blocking collectives: 78.9 us -> 121 us
  waiting for transfers between devices: 52.9 us -> 34.7 us
  starting transfers between devices: 26.6 us -> 8.5 us
    all_to_all x2 -> x3, blocking collectives: 32.3 us -> 60.4 us  [gather_all(): return lax.all_to_all(copies, axes, 0, 0, tiled=True)]
    ppermute x2 -> x0, starting transfers between devices: 14.7 us -> none  [the longest x1 7.49 us: swap_halves_sum(): return mine + lax.ppermute(theirs, axis, [(0, 1), (1, 0)])]
    all_to_all x2 -> x3, blocking collectives: 46.6 us -> 60.5 us  [scatter_sum(): return lax.all_to_all(chunks, axes, 0, 0, tiled=True).sum(axis=0)]
    all_to_all x2, waiting for transfers between devices: 47.7 us -> 34.7 us  [gather_all(): return lax.all_to_all(copies, axes, 0, 0, tiled=True)]
    ppermute x2 -> x0, waiting for transfers between devices: 5.18 us -> none  [the longest x1 2.61 us: swap_halves_sum(): return mine + lax.ppermute(theirs, axis, [(0, 1), (1, 0)])]
    reduce_sum x2 -> x3, other arithmetic: 0.09 us -> 4.17 us  [scatter_sum(): return lax.all_to_all(chunks, axes, 0, 0, tiled=True).sum(axis=0)]
    all_to_all x2, starting transfers between devices: 11.9 us -> 8.5 us  [gather_all(): return lax.all_to_all(copies, axes, 0, 0, tiled=True)]
    select_n x1 -> x0, other arithmetic: 2.62 us -> none  [swap_halves_join(): jnp.where(side == 0, jnp.concatenate([half, other], 0), jnp.concatenate([...]
  transfers between devices with their start and end apart: 4 -> 2, of which waited for: 4 -> 2; matrix products, arithmetic and copies ran while one was open for 2% -> 2% of each run, Pallas kernels for 0% -> 0%
where the time goes in v11:
time: 251 us; the launch traced here: 246 us
  blocking collectives  121 us (48%)
  other arithmetic  52.1 us (21%)
  waiting for transfers between devices  34.7 us (14%)
  local copies, waits for them, and re-layouts  15.1 us (6%)
  matrix products  13.9 us (6%)
  starting transfers between devices  8.5 us (3%)
    all_to_all x3, blocking collectives, scatter_sum(): return lax.all_to_all(chunks, axes, 0, 0, tiled=True).sum(axis=0)  60.5 us
    all_to_all x3, blocking collectives, gather_all(): return lax.all_to_all(copies, axes, 0, 0, tiled=True)  60.4 us
    all_to_all x2, waiting for transfers between devices, gather_all(): return lax.all_to_all(copies, axes, 0, 0, tiled=True)  34.7 us
    another operation x3, other arithmetic, factor_inverse(): top = jnp.linalg.cholesky(gram[:h, :h])  12.4 us
    another operation x3, other arithmetic, factor_inverse(): low = jnp.linalg.cholesky(rest)  12.4 us
    another operation x2, other arithmetic, factor_inverse(): low_inv = lax.linalg.triangular_solve(low, eye, left_side=True, lower=True)  10.5 us
    another operation x2, other arithmetic, factor_inverse(): top_inv = lax.linalg.triangular_solve(top, eye, left_side=True, lower=True)  10.5 us
    all_to_all x2, starting transfers between devices, gather_all(): return lax.all_to_all(copies, axes, 0, 0, tiled=True)  8.5 us
  transfers between devices with their start and end apart: 2, of which 2 were waited for; matrix products, arithmetic and copies ran while one was open for 2% of the time, Pallas kernels for 0%

profile of v11, /device:TPU:1, one launch (start us, length us, event | category | flops | bytes accessed | tf_op | source)
XLA Modules:
  0.0 246.1 jit_solution(7801253905957347505)
XLA Ops:
  0.6 1.7 copy-done
  2.4 2.6 %fusion.2 = bf16[256,256]{1,0:T(8,128)(2,1)S(1)} fusion(bf16[5120,256]{1,0:T(8,128)(2,1)S(1)} %copy-done, bf16[1,256,5120]{2,1,0:T(8,128)(2,1)} %param.5), kind=kOutput, calls=%fused_computation.7 | convolution fusion | flops 671154176 | bytes 5373952 | tf_op jit(solution)/shard_map/dot_general | solution.py:68
  5.0 0.1 copy.37
  5.1 30.2 %all_to_all.40 = bf16[8,256,256]{1,2,0:T(8,128)(2,1)S(1)} all-to-all(bf16[8,256,256]{1,2,0:T(8,128)(2,1)S(1)} %broadcast_in_dim.61), channel_id=1, replica_groups=mesh['x'=4,'z'=12,'c'=2,'mdl'=8] {'mdl'}, dimensions={0} | all-to-all | bytes 2097152 | tf_op jit(solution)/shard_map/all_to_all | solution.py:16
  35.3 0.4 fusion.31
  35.8 12.9 %all_to_all.41 = f32[2,4,256,256]{2,3,1,0:T(8,128)} all-to-all(f32[2,4,256,256]{2,3,1,0:T(8,128)S(1)} %bitcast.65), channel_id=1, replica_groups=mesh['x'=4,'z'=12,'c'=2,'mdl'=8] {'c'}, dimensions={0} | all-to-all | bytes 4194304 | tf_op jit(solution)/shard_map/all_to_all | solution.py:11
  48.6 2.8 %reduce_sum.36 = f32[4,256,256]{1,2,0:T(8,128)} reduce(f32[2,4,256,256]{2,3,1,0:T(8,128)} %all_to_all.41, f32[]{:T(128)} %constant.59.clone.1), dimensions={0}, to_apply=%region_0.0 | reduce | flops 262144 | bytes 3145732 | tf_op jit(solution)/shard_map/reduce_sum | solution.py:11
  51.5 2.5 %copy.38 = f32[4,1,256,256]{3,2,1,0:T(8,128)} copy(f32[4,1,256,256]{2,3,0,1:T(8,128)} %bitcast.66) | data formatting | bytes 2097152 | tf_op jit(solution)/shard_map/reshape | solution.py:24
  54.0 19.1 %all_to_all.42 = f32[4,1,256,256]{3,2,1,0:T(8,128)} all-to-all(f32[4,1,256,256]{3,2,1,0:T(8,128)} %copy.38), channel_id=1, replica_groups=mesh['x'=4,'z'=12,'c'=2,'mdl'=8] {'x'}, dimensions={0} | all-to-all | bytes 2097152 | tf_op jit(solution)/shard_map/all_to_all | solution.py:11
  73.1 1.3 reduce_sum.37
  74.5 28.5 %all_to_all.43 = f32[12,43,128]{2,1,0:T(8,128)S(1)} all-to-all(f32[12,43,128]{2,1,0:T(8,128)S(1)} %reshape.68), channel_id=1, replica_groups=mesh['x'=4,'z'=12,'c'=2,'mdl'=8] {'z'}, dimensions={0} | all-to-all | bytes 528384 | tf_op jit(solution)/shard_map/all_to_all | solution.py:11
  103.0 20.3 %all_to_all.44 = f32[12,43,128]{2,1,0:T(8,128)S(1)} all-to-all(f32[12,43,128]{2,1,0:T(8,128)S(1)} %broadcast_in_dim.62), channel_id=1, replica_groups=mesh['x'=4,'z'=12,'c'=2,'mdl'=8] {'z'}, dimensions={0} | all-to-all | bytes 528384 | tf_op jit(solution)/shard_map/all_to_all | solution.py:16
  123.5 0.1 copy.39
  123.6 1.1 broadcast_in_dim.64
  124.7 4.2 %all-to-all-start.5 = ((f32[4,1,256,256]{2,3,1,0:T(8,128)}), f32[4,1,256,256]{2,3,1,0:T(8,128)}, u32[]{:S(2)}, u32[]{:S(2)}) async-start(f32[4,1,256,256]{2,3,1,0:T(8,128)} %broadcast_in_dim.64), calls=%async_computation.5 | async-start | bytes 2097152 | tf_op jit(solution)/shard_map/all_to_all | solution.py:16
  129.0 11.2 %all-to-all-done.5 = f32[4,1,256,256]{2,3,1,0:T(8,128)} async-done(((f32[4,1,256,256]{2,3,1,0:T(8,128)}), f32[4,1,256,256]{2,3,1,0:T(8,128)}, u32[]{:S(2)}, u32[]{:S(2)}) %all-to-all-start.5) | async-done | bytes 1048608 | tf_op jit(solution)/shard_map/all_to_all | solution.py:16
  140.2 1.4 broadcast_in_dim.66
  141.6 9.9 %all_to_all.45 = f32[2,4,256,256]{2,3,1,0:T(8,128)S(1)} all-to-all(f32[2,4,256,256]{2,3,1,0:T(8,128)S(1)} %broadcast_in_dim.66), channel_id=1, replica_groups=mesh['x'=4,'z'=12,'c'=2,'mdl'=8] {'c'}, dimensions={0} | all-to-all | bytes 4194304 | tf_op jit(solution)/shard_map/all_to_all | solution.py:16
  151.5 1.3 copy-done.2
  152.8 0.1 copy.40
  153.0 11.7 %cholesky.44 = f32[128,128]{1,0:T(8,128)S(1)} custom-call(f32[128,128]{1,0:T(8,128)S(1)} %fusion.42), custom_call_target="Cholesky" | custom-call | tf_op jit(solution)/shard_map/jit(cholesky)/cholesky | solution.py:54
  164.7 0.6 compare_reduce_fusion.1
  165.3 0.7 fusion.33
  166.0 9.8 %custom-call.8 = f32[1,128,128]{1,2,0:T(8,128)S(1)} custom-call(f32[1,128,128]{2,1,0:T(8,128)S(1)} %fusion.33), custom_call_target="InvertDiagBlocksLowerTriangular" | custom-call | tf_op jit(solution)/shard_map/triangular_solve/custom-call.0 | solution.py:55
  175.8 0.3 fusion.40
  176.1 0.3 fusion.35
  176.4 0.3 convolution_subtract_fusion
  176.7 0.2 fusion.51
  176.9 1.4 gather_fusion
  178.3 0.1 copy.42
  178.4 11.7 %cholesky.55 = f32[128,128]{1,0:T(8,128)S(1)} custom-call(f32[128,128]{1,0:T(8,128)S(1)} %fusion.39), custom_call_target="Cholesky" | custom-call | tf_op jit(solution)/shard_map/jit(cholesky)/cholesky | solution.py:58
  190.2 0.6 compare_reduce_fusion
  190.8 0.7 fusion.34
  191.5 9.8 %custom-call.9 = f32[1,128,128]{1,2,0:T(8,128)S(1)} custom-call(f32[1,128,128]{2,1,0:T(8,128)S(1)} %fusion.34), custom_call_target="InvertDiagBlocksLowerTriangular" | custom-call | tf_op jit(solution)/shard_map/triangular_solve/custom-call.0 | solution.py:59
  201.3 0.3 bitcast_add_fusion
  201.6 0.3 convolution_negate_fusion
  201.9 1.1 broadcast_in_dim.70
  203.0 4.3 %all-to-all-start.7 = ((f32[8,257,128]{2,1,0:T(8,128)}), f32[8,257,128]{2,1,0:T(8,128)}, u32[]{:S(2)}, u32[]{:S(2)}) async-start(f32[8,257,128]{2,1,0:T(8,128)} %broadcast_in_dim.70), calls=%async_computation.7 | async-start | bytes 2162688 | tf_op jit(solution)/shard_map/all_to_all | solution.py:16
  207.3 0.1 copy.43
  207.4 4.0 %convolution_bitcast_fusion = f32[8,256,256]{1,2,0:T(8,128)} fusion(f32[8,256,256]{1,2,0:T(8,128)} %bitcast.63, f32[128,128]{1,0:T(8,128)S(1)} %fusion.40, f32[128,128]{1,0:T(8,128)S(1)} %copy.43, f32[128,128]{1,0:T(8,128)S(1)} %convolution_negate_fusion), kind=kOutput, calls=%fused_computation.5 | convolution fusion | flops 805568512 | bytes 4390912 | tf_op jit(solution)/shard_map/ab,jbc->jac/dot_general | solution.py:82
  211.4 23.5 %all-to-all-done.7 = f32[8,257,128]{2,1,0:T(8,128)} async-done(((f32[8,257,128]{2,1,0:T(8,128)}), f32[8,257,128]{2,1,0:T(8,128)}, u32[]{:S(2)}, u32[]{:S(2)}) %all-to-all-start.7) | async-done | bytes 1052704 | tf_op jit(solution)/shard_map/all_to_all | solution.py:16
  234.9 0.9 slice.50
  235.8 1.9 fusion.6
  237.7 1.7 convolution_add_fusion
  239.4 1.7 fusion.8
  241.1 1.6 multiply_reduce_fusion
  242.7 0.5 multiply_bitcast_fusion
  243.2 2.9 %copy.48 = f32[256,2048]{1,0:T(8,128)} copy(f32[256,2048]{0,1:T(8,128)} %bitcast.64) | data formatting | bytes 4194304
  (23 shorter events, 0.5 us)
Async XLA Ops:
  0.6 1.7 copy-start
  124.7 15.5 %all-to-all-start.5 = ((f32[4,1,256,256]{2,3,1,0:T(8,128)}), f32[4,1,256,256]{2,3,1,0:T(8,128)}, u32[]{:S(2)}, u32[]{:S(2)}) async-start(f32[4,1,256,256]{2,3,1,0:T(8,128)} %broadcast_in_dim.64), calls=%async_computation.5 | async-start | bytes 2097152 | tf_op jit(solution)/shard_map/all_to_all | solution.py:16
  151.5 1.3 copy-start.2
  203.0 31.9 %all-to-all-start.7 = ((f32[8,257,128]{2,1,0:T(8,128)}), f32[8,257,128]{2,1,0:T(8,128)}, u32[]{:S(2)}, u32[]{:S(2)}) async-start(f32[8,257,128]{2,1,0:T(8,128)} %broadcast_in_dim.70), calls=%async_computation.7 | async-start | bytes 2162688 | tf_op jit(solution)/shard_map/all_to_all | solution.py:16
  234.9 2.9 %copy-start.1 = (f32[8,256,256]{1,2,0:T(8,128)S(1)}, f32[8,256,256]{1,2,0:T(8,128)}, u32[]{:S(2)}) copy-start(f32[8,256,256]{1,2,0:T(8,128)} %convolution_bitcast_fusion) | copy-start | bytes 6291460

commit v12 on v8

--- a/solution.py
+++ b/solution.py
@@ -27,7 +27,9 @@
 def swap_halves_join(half, axis):
     side = lax.axis_index(axis)
     other = lax.ppermute(half, axis, [(0, 1), (1, 0)])
-    return jnp.where(side == 0, jnp.concatenate([half, other], 0), jnp.concatenate([other, half], 0))
+    both = jnp.stack([half, other])
+    order = jnp.stack([side, 1 - side])
+    return jnp.take(both, order, axis=0).reshape((2 * half.shape[0],) + half.shape[1:])
 
 
 def sum_over_tokens(tiles, pair, ring, outer, lanes=128):

time: 245 us -> 254 us (1.037)
  local copies, waits for them, and re-layouts: 13.7 us -> 20.2 us
    gather x0 -> x2, local copies, waits for them, and re-layouts: none -> 6.5 us  [swap_halves_join(): jnp.take(both, order, axis=0).reshape((2 * half.shape[0],) + half.shape[1:])]
    another operation x0 -> x1, other arithmetic: none -> 2.99 us  [swap_halves_join(): both = jnp.stack([half, other])]
where the time goes in v12:
time: 254 us; the launch traced here: 249 us
  blocking collectives  78.9 us (31%)
  other arithmetic  54.7 us (22%)
  waiting for transfers between devices  52.6 us (21%)
  starting transfers between devices  26.6 us (10%)
  local copies, waits for them, and re-layouts  20.2 us (8%)
  matrix products  15.1 us (6%)
    all_to_all x2, waiting for transfers between devices, gather_all(): return lax.all_to_all(copies, axes, 0, 0, tiled=True)  47.7 us
    all_to_all x2, blocking collectives, scatter_sum(): return lax.all_to_all(chunks, axes, 0, 0, tiled=True).sum(axis=0)  46.6 us
    all_to_all x2, blocking collectives, gather_all(): return lax.all_to_all(copies, axes, 0, 0, tiled=True)  32.3 us
    another operation x3, other arithmetic, factor_inverse(): top = jnp.linalg.cholesky(gram[:h, :h])  12.4 us
    another operation x3, other arithmetic, factor_inverse(): low = jnp.linalg.cholesky(rest)  12.4 us
    all_to_all x2, starting transfers between devices, gather_all(): return lax.all_to_all(copies, axes, 0, 0, tiled=True)  11.9 us
    another operation x2, other arithmetic, factor_inverse(): top_inv = lax.linalg.triangular_solve(top, eye, left_side=True, lower=True)  10.5 us
    another operation x2, other arithmetic, factor_inverse(): low_inv = lax.linalg.triangular_solve(low, eye, left_side=True, lower=True)  10.5 us
  transfers between devices with their start and end apart: 4, of which 4 were waited for; matrix products, arithmetic and copies ran while one was open for 2% of the time, Pallas kernels for 0%

profile of v12, /device:TPU:1, one launch (start us, length us, event | category | flops | bytes accessed | tf_op | source)
XLA Modules:
  0.0 249.1 jit_solution(4030699378976366420)
XLA Ops:
  0.6 1.7 copy-done
  2.4 2.6 %fusion.2 = bf16[256,256]{1,0:T(8,128)(2,1)S(1)} fusion(bf16[5120,256]{1,0:T(8,128)(2,1)S(1)} %copy-done, bf16[1,256,5120]{2,1,0:T(8,128)(2,1)} %param.5), kind=kOutput, calls=%fused_computation.9 | convolution fusion | flops 671154176 | bytes 5373952 | tf_op jit(solution)/shard_map/dot_general | solution.py:84
  5.1 1.0 broadcast_in_dim.71
  6.1 7.7 %all-to-all-start = ((bf16[8,256,256]{1,2,0:T(8,128)(2,1)}), bf16[8,256,256]{1,2,0:T(8,128)(2,1)}, u32[]{:S(2)}, u32[]{:S(2)}) async-start(bf16[8,256,256]{1,2,0:T(8,128)(2,1)} %broadcast_in_dim.71), calls=%async_computation | async-start | bytes 2097152 | tf_op jit(solution)/shard_map/all_to_all | solution.py:16
  13.8 24.2 %all-to-all-done = bf16[8,256,256]{1,2,0:T(8,128)(2,1)} async-done(((bf16[8,256,256]{1,2,0:T(8,128)(2,1)}), bf16[8,256,256]{1,2,0:T(8,128)(2,1)}, u32[]{:S(2)}, u32[]{:S(2)}) %all-to-all-start) | async-done | bytes 1048608 | tf_op jit(solution)/shard_map/all_to_all | solution.py:16
  38.0 1.7 fusion.32
  39.7 1.3 copy-done.3
  41.0 1.1 dynamic-slice_bitcast_fusion
  42.1 7.5 %collective-permute-start = (f32[4,256,256]{1,2,0:T(8,128)}, f32[4,256,256]{1,2,0:T(8,128)}, u32[]{:S(2)}, u32[]{:S(2)}) collective-permute-start(f32[4,256,256]{1,2,0:T(8,128)} %dynamic-slice_bitcast_fusion), channel_id=1, source_target_pairs={{0,8},{8,0},{1,9},{9,1},{2,10},{10,2},{3,11},{11,3},{4,12},{12,4},... | collective-permute-start | bytes 3145736 | tf_op jit(solution)/shard_map/ppermute | solution.py:24
  49.6 2.6 %collective-permute-done = f32[4,256,256]{1,2,0:T(8,128)} collective-permute-done((f32[4,256,256]{1,2,0:T(8,128)}, f32[4,256,256]{1,2,0:T(8,128)}, u32[]{:S(2)}, u32[]{:S(2)}) %collective-permute-start) | collective-permute-done | bytes 1048608 | tf_op jit(solution)/shard_map/ppermute | solution.py:24
  52.2 1.7 fusion.6
  53.8 18.0 %all_to_all.30 = f32[4,1,256,256]{2,3,1,0:T(8,128)S(1)} all-to-all(f32[4,1,256,256]{2,3,1,0:T(8,128)S(1)} %fusion.6), channel_id=1, replica_groups=mesh['x'=4,'z'=12,'c'=2,'mdl'=8] {'x'}, dimensions={0} | all-to-all | bytes 2097152 | tf_op jit(solution)/shard_map/all_to_all | solution.py:11
  72.1 28.6 %all_to_all.31 = f32[12,43,128]{2,1,0:T(8,128)S(1)} all-to-all(f32[12,43,128]{2,1,0:T(8,128)S(1)} %reshape.167), channel_id=1, replica_groups=mesh['x'=4,'z'=12,'c'=2,'mdl'=8] {'z'}, dimensions={0} | all-to-all | bytes 528384 | tf_op jit(solution)/shard_map/all_to_all | solution.py:11
  100.8 17.6 %all_to_all.32 = f32[12,43,128]{2,1,0:T(8,128)S(1)} all-to-all(f32[12,43,128]{2,1,0:T(8,128)S(1)} %broadcast_in_dim.72), channel_id=1, replica_groups=mesh['x'=4,'z'=12,'c'=2,'mdl'=8] {'z'}, dimensions={0} | all-to-all | bytes 528384 | tf_op jit(solution)/shard_map/all_to_all | solution.py:16
  118.6 14.7 %all_to_all.33 = f32[4,1,256,256]{3,2,1,0:T(8,128)} all-to-all(f32[4,1,256,256]{3,2,1,0:T(8,128)S(1)} %broadcast_in_dim.74), channel_id=1, replica_groups=mesh['x'=4,'z'=12,'c'=2,'mdl'=8] {'x'}, dimensions={0} | all-to-all | bytes 2097152 | tf_op jit(solution)/shard_map/all_to_all | solution.py:16
  133.3 7.2 %collective-permute-start.1 = (f32[4,256,256]{2,1,0:T(8,128)}, f32[4,256,256]{2,1,0:T(8,128)}, u32[]{:S(2)}, u32[]{:S(2)}) collective-permute-start(f32[4,256,256]{2,1,0:T(8,128)} %bitcast.12), channel_id=1, source_target_pairs={{0,8},{8,0},{1,9},{9,1},{2,10},{10,2},{3,11},{11,3},{4,12},{12,4},... | collective-permute-start | bytes 3145736 | tf_op jit(solution)/shard_map/ppermute | solution.py:29
  140.9 2.3 collective-permute-done.1
  143.1 3.0 %pad_maximum_fusion = f32[2,4,256,256]{3,2,1,0:T(8,128)} fusion(f32[1,4,256,256]{3,2,1,0:T(8,128)} %bitcast.13, f32[1,4,256,256]{3,2,1,0:T(8,128)} %bitcast.11), kind=kLoop, calls=%fused_computation.4 | loop fusion | flops 524288 | bytes 4194304 | tf_op jit(solution)/shard_map/stack | solution.py:30
  146.1 3.6 %gather_fusion = f32[2,4,256,256]{3,2,1,0:T(8,128)} fusion(f32[2,4,256,256]{3,2,1,0:T(8,128)} %pad_maximum_fusion, s32[1024]{0:T(1024)S(1)} %pad_clamp_fusion), kind=kCustom, calls=%fused_computation | custom fusion | bytes 4194312 | tf_op jit(solution)/shard_map/jit(_take)/gather | solution.py:32
  149.7 2.9 %copy.40 = f32[8,256,256]{1,2,0:T(8,128)} copy(f32[8,256,256]{2,1,0:T(8,128)} %bitcast.82) | data formatting | bytes 4194304 | tf_op jit(solution)/shard_map/jit(_take)/gather | solution.py:32
  152.6 1.8 broadcast_select_fusion
  154.5 1.3 copy-done.2
  155.9 11.7 %cholesky.44 = f32[128,128]{1,0:T(8,128)S(1)} custom-call(f32[128,128]{1,0:T(8,128)S(1)} %fusion.43), custom_call_target="Cholesky" | custom-call | tf_op jit(solution)/shard_map/jit(cholesky)/cholesky | solution.py:70
  167.7 0.6 compare_reduce_fusion.1
  168.3 0.7 fusion.34
  169.0 9.8 %custom-call.8 = f32[1,128,128]{1,2,0:T(8,128)S(1)} custom-call(f32[1,128,128]{2,1,0:T(8,128)S(1)} %fusion.34), custom_call_target="InvertDiagBlocksLowerTriangular" | custom-call | tf_op jit(solution)/shard_map/triangular_solve/custom-call.0 | solution.py:71
  178.8 0.3 fusion.41
  179.1 0.3 fusion.36
  179.4 0.3 convolution_subtract_fusion
  179.7 0.2 fusion.53
  179.9 1.4 gather_fusion.1
  181.4 11.7 %cholesky.55 = f32[128,128]{1,0:T(8,128)S(1)} custom-call(f32[128,128]{1,0:T(8,128)S(1)} %fusion.40), custom_call_target="Cholesky" | custom-call | tf_op jit(solution)/shard_map/jit(cholesky)/cholesky | solution.py:74
  193.2 0.6 compare_reduce_fusion
  193.8 0.7 fusion.35
  194.5 9.8 %custom-call.9 = f32[1,128,128]{1,2,0:T(8,128)S(1)} custom-call(f32[1,128,128]{2,1,0:T(8,128)S(1)} %fusion.35), custom_call_target="InvertDiagBlocksLowerTriangular" | custom-call | tf_op jit(solution)/shard_map/triangular_solve/custom-call.0 | solution.py:75
  204.3 0.3 bitcast_add_fusion.1
  204.6 0.3 convolution_negate_fusion
  204.9 1.1 broadcast_in_dim.79
  205.9 4.3 %all-to-all-start.5 = ((f32[8,257,128]{2,1,0:T(8,128)}), f32[8,257,128]{2,1,0:T(8,128)}, u32[]{:S(2)}, u32[]{:S(2)}) async-start(f32[8,257,128]{2,1,0:T(8,128)} %broadcast_in_dim.79), calls=%async_computation.5 | async-start | bytes 2162688 | tf_op jit(solution)/shard_map/all_to_all | solution.py:16
  210.4 4.0 %convolution_bitcast_fusion = f32[8,256,256]{1,2,0:T(8,128)} fusion(f32[8,256,256]{1,2,0:T(8,128)} %copy-done.2, f32[128,128]{1,0:T(8,128)S(1)} %fusion.41, f32[128,128]{1,0:T(8,128)S(1)} %copy.44, f32[128,128]{1,0:T(8,128)S(1)} %convolution_negate_fusion), kind=kOutput, calls=%fused_computation.7 | convolution fusion | flops 805568512 | bytes 4390912 | tf_op jit(solution)/shard_map/ab,jbc->jac/dot_general | solution.py:98
  214.4 23.5 %all-to-all-done.5 = f32[8,257,128]{2,1,0:T(8,128)} async-done(((f32[8,257,128]{2,1,0:T(8,128)}), f32[8,257,128]{2,1,0:T(8,128)}, u32[]{:S(2)}, u32[]{:S(2)}) %all-to-all-start.5) | async-done | bytes 1052704 | tf_op jit(solution)/shard_map/all_to_all | solution.py:16
  237.8 0.9 slice.52
  238.8 1.9 fusion.7
  240.7 1.7 convolution_add_fusion
  242.4 1.7 fusion.9
  244.1 1.6 multiply_reduce_fusion
  245.7 0.5 multiply_bitcast_fusion
  246.2 2.9 %copy.49 = f32[256,2048]{1,0:T(8,128)} copy(f32[256,2048]{0,1:T(8,128)} %bitcast.81) | data formatting | bytes 4194304
  (35 shorter events, 1.4 us)
Async XLA Ops:
  0.6 1.7 copy-start
  6.1 31.9 %all-to-all-start = ((bf16[8,256,256]{1,2,0:T(8,128)(2,1)}), bf16[8,256,256]{1,2,0:T(8,128)(2,1)}, u32[]{:S(2)}, u32[]{:S(2)}) async-start(bf16[8,256,256]{1,2,0:T(8,128)(2,1)} %broadcast_in_dim.71), calls=%async_computation | async-start | bytes 2097152 | tf_op jit(solution)/shard_map/all_to_all | solution.py:16
  39.7 1.3 copy-start.3
  42.1 10.1 %collective-permute-start = (f32[4,256,256]{1,2,0:T(8,128)}, f32[4,256,256]{1,2,0:T(8,128)}, u32[]{:S(2)}, u32[]{:S(2)}) collective-permute-start(f32[4,256,256]{1,2,0:T(8,128)} %dynamic-slice_bitcast_fusion), channel_id=1, source_target_pairs={{0,8},{8,0},{1,9},{9,1},{2,10},{10,2},{3,11},{11,3},{4,12},{12,4},... | collective-permute-start | bytes 3145736 | tf_op jit(solution)/shard_map/ppermute | solution.py:24
  133.3 9.8 %collective-permute-start.1 = (f32[4,256,256]{2,1,0:T(8,128)}, f32[4,256,256]{2,1,0:T(8,128)}, u32[]{:S(2)}, u32[]{:S(2)}) collective-permute-start(f32[4,256,256]{2,1,0:T(8,128)} %bitcast.12), channel_id=1, source_target_pairs={{0,8},{8,0},{1,9},{9,1},{2,10},{10,2},{3,11},{11,3},{4,12},{12,4},... | collective-permute-start | bytes 3145736 | tf_op jit(solution)/shard_map/ppermute | solution.py:29
  154.5 1.3 copy-start.2
  205.9 31.9 %all-to-all-start.5 = ((f32[8,257,128]{2,1,0:T(8,128)}), f32[8,257,128]{2,1,0:T(8,128)}, u32[]{:S(2)}, u32[]{:S(2)}) async-start(f32[8,257,128]{2,1,0:T(8,128)} %broadcast_in_dim.79), calls=%async_computation.5 | async-start | bytes 2162688 | tf_op jit(solution)/shard_map/all_to_all | solution.py:16
  237.8 2.9 %copy-start.1 = (f32[8,256,256]{1,2,0:T(8,128)S(1)}, f32[8,256,256]{1,2,0:T(8,128)}, u32[]{:S(2)}) copy-start(f32[8,256,256]{1,2,0:T(8,128)} %convolution_bitcast_fusion) | copy-start | bytes 6291460

commit v13 on v8

--- a/solution.py
+++ b/solution.py
@@ -4,7 +4,7 @@
 from jax.sharding import Mesh
 from jax.sharding import PartitionSpec as P
 
-HIGH = lax.Precision.HIGHEST
+HIGH = lax.Precision.HIGH
 
 
 def scatter_sum(chunks, axes):

time: 245 us -> 245 us (level)
  no operation moved by 1% of the time
where the time goes in v13:
time: 245 us; the launch traced here: 240 us
  blocking collectives  78.9 us (32%)
  waiting for transfers between devices  52.9 us (22%)
  other arithmetic  52.3 us (21%)
  starting transfers between devices  26.6 us (11%)
  matrix products  15 us (6%)
  local copies, waits for them, and re-layouts  13.7 us (6%)
    all_to_all x2, waiting for transfers between devices, gather_all(): return lax.all_to_all(copies, axes, 0, 0, tiled=True)  47.7 us
    all_to_all x2, blocking collectives, scatter_sum(): return lax.all_to_all(chunks, axes, 0, 0, tiled=True).sum(axis=0)  46.6 us
    all_to_all x2, blocking collectives, gather_all(): return lax.all_to_all(copies, axes, 0, 0, tiled=True)  32.3 us
    another operation x3, other arithmetic, factor_inverse(): top = jnp.linalg.cholesky(gram[:h, :h])  12.4 us
    another operation x3, other arithmetic, factor_inverse(): low = jnp.linalg.cholesky(rest)  12.4 us
    all_to_all x2, starting transfers between devices, gather_all(): return lax.all_to_all(copies, axes, 0, 0, tiled=True)  11.9 us
    another operation x2, other arithmetic, factor_inverse(): low_inv = lax.linalg.triangular_solve(low, eye, left_side=True, lower=True)  10.5 us
    another operation x2, other arithmetic, factor_inverse(): top_inv = lax.linalg.triangular_solve(top, eye, left_side=True, lower=True)  10.5 us
  transfers between devices with their start and end apart: 4, of which 4 were waited for; matrix products, arithmetic and copies ran while one was open for 2% of the time, Pallas kernels for 0%

profile of v13, /device:TPU:1, one launch (start us, length us, event | category | flops | bytes accessed | tf_op | source)
XLA Modules:
  0.0 240.4 jit_solution(13213348853285993415)
XLA Ops:
  0.6 1.7 copy-done
  2.4 2.6 %fusion.2 = bf16[256,256]{1,0:T(8,128)(2,1)S(1)} fusion(bf16[5120,256]{1,0:T(8,128)(2,1)S(1)} %copy-done, bf16[1,256,5120]{2,1,0:T(8,128)(2,1)} %param.5), kind=kOutput, calls=%fused_computation.8 | convolution fusion | flops 671154176 | bytes 5373952 | tf_op jit(solution)/shard_map/dot_general | solution.py:82
  5.0 0.1 copy.37
  5.1 1.0 broadcast_in_dim.54
  6.1 7.7 %all-to-all-start = ((bf16[8,256,256]{1,2,0:T(8,128)(2,1)}), bf16[8,256,256]{1,2,0:T(8,128)(2,1)}, u32[]{:S(2)}, u32[]{:S(2)}) async-start(bf16[8,256,256]{1,2,0:T(8,128)(2,1)} %broadcast_in_dim.54), calls=%async_computation | async-start | bytes 2097152 | tf_op jit(solution)/shard_map/all_to_all | solution.py:16
  13.8 24.2 %all-to-all-done = bf16[8,256,256]{1,2,0:T(8,128)(2,1)} async-done(((bf16[8,256,256]{1,2,0:T(8,128)(2,1)}), bf16[8,256,256]{1,2,0:T(8,128)(2,1)}, u32[]{:S(2)}, u32[]{:S(2)}) %all-to-all-start) | async-done | bytes 1048608 | tf_op jit(solution)/shard_map/all_to_all | solution.py:16
  38.0 1.7 fusion.32
  39.7 1.3 copy-done.3
  41.0 1.1 dynamic-slice_bitcast_fusion
  42.1 7.5 %collective-permute-start = (f32[4,256,256]{1,2,0:T(8,128)}, f32[4,256,256]{1,2,0:T(8,128)}, u32[]{:S(2)}, u32[]{:S(2)}) collective-permute-start(f32[4,256,256]{1,2,0:T(8,128)} %dynamic-slice_bitcast_fusion), channel_id=1, source_target_pairs={{0,8},{8,0},{1,9},{9,1},{2,10},{10,2},{3,11},{11,3},{4,12},{12,4},... | collective-permute-start | bytes 3145736 | tf_op jit(solution)/shard_map/ppermute | solution.py:24
  49.6 2.6 %collective-permute-done = f32[4,256,256]{1,2,0:T(8,128)} collective-permute-done((f32[4,256,256]{1,2,0:T(8,128)}, f32[4,256,256]{1,2,0:T(8,128)}, u32[]{:S(2)}, u32[]{:S(2)}) %collective-permute-start) | collective-permute-done | bytes 1048608 | tf_op jit(solution)/shard_map/ppermute | solution.py:24
  52.2 1.7 fusion.6
  53.8 18.0 %all_to_all.30 = f32[4,1,256,256]{2,3,1,0:T(8,128)S(1)} all-to-all(f32[4,1,256,256]{2,3,1,0:T(8,128)S(1)} %fusion.6), channel_id=1, replica_groups=mesh['x'=4,'z'=12,'c'=2,'mdl'=8] {'x'}, dimensions={0} | all-to-all | bytes 2097152 | tf_op jit(solution)/shard_map/all_to_all | solution.py:11
  71.9 0.1 copy.39
  72.1 28.6 %all_to_all.31 = f32[12,43,128]{2,1,0:T(8,128)S(1)} all-to-all(f32[12,43,128]{2,1,0:T(8,128)S(1)} %reshape.67), channel_id=1, replica_groups=mesh['x'=4,'z'=12,'c'=2,'mdl'=8] {'z'}, dimensions={0} | all-to-all | bytes 528384 | tf_op jit(solution)/shard_map/all_to_all | solution.py:11
  100.8 17.6 %all_to_all.32 = f32[12,43,128]{2,1,0:T(8,128)S(1)} all-to-all(f32[12,43,128]{2,1,0:T(8,128)S(1)} %broadcast_in_dim.55), channel_id=1, replica_groups=mesh['x'=4,'z'=12,'c'=2,'mdl'=8] {'z'}, dimensions={0} | all-to-all | bytes 528384 | tf_op jit(solution)/shard_map/all_to_all | solution.py:16
  118.6 0.1 copy.40
  118.8 14.7 %all_to_all.33 = f32[4,1,256,256]{2,3,1,0:T(8,128)} all-to-all(f32[4,1,256,256]{2,3,1,0:T(8,128)S(1)} %broadcast_in_dim.57), channel_id=1, replica_groups=mesh['x'=4,'z'=12,'c'=2,'mdl'=8] {'x'}, dimensions={0} | all-to-all | bytes 2097152 | tf_op jit(solution)/shard_map/all_to_all | solution.py:16
  133.4 7.2 %collective-permute-start.1 = (f32[4,256,256]{1,2,0:T(8,128)}, f32[4,256,256]{1,2,0:T(8,128)}, u32[]{:S(2)}, u32[]{:S(2)}) collective-permute-start(f32[4,256,256]{1,2,0:T(8,128)} %bitcast.9), channel_id=1, source_target_pairs={{0,8},{8,0},{1,9},{9,1},{2,10},{10,2},{3,11},{11,3},{4,12},{12,4},... | collective-permute-start | bytes 3145736 | tf_op jit(solution)/shard_map/ppermute | solution.py:29
  140.7 2.6 %collective-permute-done.1 = f32[4,256,256]{1,2,0:T(8,128)} collective-permute-done((f32[4,256,256]{1,2,0:T(8,128)}, f32[4,256,256]{1,2,0:T(8,128)}, u32[]{:S(2)}, u32[]{:S(2)}) %collective-permute-start.1) | collective-permute-done | bytes 1048608 | tf_op jit(solution)/shard_map/ppermute | solution.py:29
  143.3 2.6 %maximum_select_fusion = f32[8,256,256]{1,2,0:T(8,128)S(1)} fusion(f32[4,256,256]{1,2,0:T(8,128)} %collective-permute-done.1, f32[4,256,256]{1,2,0:T(8,128)} %bitcast.9, pred[]{:T(512)S(6)} %eq.15), kind=kLoop, calls=%fused_computation.3 | loop fusion | flops 1572864 | bytes 4194305 | tf_op jit(solution)/shard_map/jit(_where)/select_n | solution.py:30
  145.9 1.3 copy-done.2
  147.4 11.7 %cholesky.44 = f32[128,128]{1,0:T(8,128)S(1)} custom-call(f32[128,128]{1,0:T(8,128)S(1)} %fusion.43), custom_call_target="Cholesky" | custom-call | tf_op jit(solution)/shard_map/jit(cholesky)/cholesky | solution.py:68
  159.1 0.6 compare_reduce_fusion.1
  159.8 0.7 fusion.34
  160.4 9.8 %custom-call.8 = f32[1,128,128]{1,2,0:T(8,128)S(1)} custom-call(f32[1,128,128]{2,1,0:T(8,128)S(1)} %fusion.34), custom_call_target="InvertDiagBlocksLowerTriangular" | custom-call | tf_op jit(solution)/shard_map/triangular_solve/custom-call.0 | solution.py:69
  170.2 0.3 fusion.41
  170.5 0.2 fusion.36
  170.8 0.2 slice_subtract_fusion
  171.0 0.2 fusion.52
  171.2 1.4 gather_fusion
  172.7 11.7 %cholesky.55 = f32[128,128]{1,0:T(8,128)S(1)} custom-call(f32[128,128]{1,0:T(8,128)S(1)} %fusion.40), custom_call_target="Cholesky" | custom-call | tf_op jit(solution)/shard_map/jit(cholesky)/cholesky | solution.py:72
  184.5 0.6 compare_reduce_fusion
  185.1 0.7 fusion.35
  185.8 9.8 %custom-call.9 = f32[1,128,128]{1,2,0:T(8,128)S(1)} custom-call(f32[1,128,128]{2,1,0:T(8,128)S(1)} %fusion.35), custom_call_target="InvertDiagBlocksLowerTriangular" | custom-call | tf_op jit(solution)/shard_map/triangular_solve/custom-call.0 | solution.py:73
  195.6 0.3 bitcast_add_fusion.1
  195.9 0.3 convolution_negate_fusion
  196.1 1.1 broadcast_in_dim.61
  197.2 4.3 %all-to-all-start.5 = ((f32[8,257,128]{2,1,0:T(8,128)}), f32[8,257,128]{2,1,0:T(8,128)}, u32[]{:S(2)}, u32[]{:S(2)}) async-start(f32[8,257,128]{2,1,0:T(8,128)} %broadcast_in_dim.61), calls=%async_computation.5 | async-start | bytes 2162688 | tf_op jit(solution)/shard_map/all_to_all | solution.py:16
  201.7 4.0 %convolution_bitcast_fusion = f32[8,256,256]{1,2,0:T(8,128)} fusion(f32[8,256,256]{1,2,0:T(8,128)} %copy-done.2, f32[128,128]{1,0:T(8,128)S(1)} %fusion.41, f32[128,128]{1,0:T(8,128)S(1)} %copy.44, f32[128,128]{1,0:T(8,128)S(1)} %convolution_negate_fusion), kind=kOutput, calls=%fused_computation.6 | convolution fusion | flops 805568512 | bytes 4390912 | tf_op jit(solution)/shard_map/ab,jbc->jac/dot_general | solution.py:96
  205.7 23.5 %all-to-all-done.5 = f32[8,257,128]{2,1,0:T(8,128)} async-done(((f32[8,257,128]{2,1,0:T(8,128)}), f32[8,257,128]{2,1,0:T(8,128)}, u32[]{:S(2)}, u32[]{:S(2)}) %all-to-all-start.5) | async-done | bytes 1052704 | tf_op jit(solution)/shard_map/all_to_all | solution.py:16
  229.1 0.9 slice.50
  230.0 1.9 fusion.7
  232.0 1.7 convolution_add_fusion
  233.7 1.7 fusion.9
  235.4 1.6 multiply_reduce_fusion
  237.0 0.5 multiply_bitcast_fusion
  237.5 2.9 %copy.49 = f32[256,2048]{1,0:T(8,128)} copy(f32[256,2048]{0,1:T(8,128)} %bitcast.72) | data formatting | bytes 4194304
  (28 shorter events, 0.9 us)
Async XLA Ops:
  0.6 1.7 copy-start
  6.1 31.9 %all-to-all-start = ((bf16[8,256,256]{1,2,0:T(8,128)(2,1)}), bf16[8,256,256]{1,2,0:T(8,128)(2,1)}, u32[]{:S(2)}, u32[]{:S(2)}) async-start(bf16[8,256,256]{1,2,0:T(8,128)(2,1)} %broadcast_in_dim.54), calls=%async_computation | async-start | bytes 2097152 | tf_op jit(solution)/shard_map/all_to_all | solution.py:16
  39.7 1.3 copy-start.3
  42.1 10.1 %collective-permute-start = (f32[4,256,256]{1,2,0:T(8,128)}, f32[4,256,256]{1,2,0:T(8,128)}, u32[]{:S(2)}, u32[]{:S(2)}) collective-permute-start(f32[4,256,256]{1,2,0:T(8,128)} %dynamic-slice_bitcast_fusion), channel_id=1, source_target_pairs={{0,8},{8,0},{1,9},{9,1},{2,10},{10,2},{3,11},{11,3},{4,12},{12,4},... | collective-permute-start | bytes 3145736 | tf_op jit(solution)/shard_map/ppermute | solution.py:24
  133.4 9.8 %collective-permute-start.1 = (f32[4,256,256]{1,2,0:T(8,128)}, f32[4,256,256]{1,2,0:T(8,128)}, u32[]{:S(2)}, u32[]{:S(2)}) collective-permute-start(f32[4,256,256]{1,2,0:T(8,128)} %bitcast.9), channel_id=1, source_target_pairs={{0,8},{8,0},{1,9},{9,1},{2,10},{10,2},{3,11},{11,3},{4,12},{12,4},... | collective-permute-start | bytes 3145736 | tf_op jit(solution)/shard_map/ppermute | solution.py:29
  145.9 1.3 copy-start.2
  197.2 31.9 %all-to-all-start.5 = ((f32[8,257,128]{2,1,0:T(8,128)}), f32[8,257,128]{2,1,0:T(8,128)}, u32[]{:S(2)}, u32[]{:S(2)}) async-start(f32[8,257,128]{2,1,0:T(8,128)} %broadcast_in_dim.61), calls=%async_computation.5 | async-start | bytes 2162688 | tf_op jit(solution)/shard_map/all_to_all | solution.py:16
  229.1 2.9 %copy-start.1 = (f32[8,256,256]{1,2,0:T(8,128)S(1)}, f32[8,256,256]{1,2,0:T(8,128)}, u32[]{:S(2)}) copy-start(f32[8,256,256]{1,2,0:T(8,128)} %convolution_bitcast_fusion) | copy-start | bytes 6291460
